TPU v7x, 256 devices: a whole 4x4x8 slice. The times are simulated.
256 devices in a mesh: ctx: 64 (over y, z, core), ch: 4 (over x).
Axes of the slice: x: 4, y: 4, z: 8, core: 2. Of those that a mesh axis runs over, the one named last changes fastest.
Arguments:
- tokens: bfloat16 [16384, 4096], P('ctx', 'ch'), may hold values from -6 to 6
- in_weight: bfloat16 [3, 4096, 4096], P(None, 'ctx', 'ch'), may hold values from -0.09375 to 0.09375
- short_taps: float32 [3, 3, 4096], P(None, None, 'ch'), may hold values from -4 to 4
- long_filter: float32 [4, 1024, 16384], P('ch', 'ctx'), may hold values from -0.046875 to 0.046875
- skip_gain: float32 [4, 1024], P('ch', 'ctx'), may hold values from 0.25 to 2
Outputs:
- gated_output: bfloat16 [4096, 16384], P('ch', 'ctx')
All inputs are finite; a program needn't handle non-finite values.
Results may differ from a plain program's by a relative error of at most 0.015.
Values may be sent and summed in bfloat16 or wider, within the bound.
No kernel may reach another device: no remote copies, remote signals or barrier semaphores. Data moves between devices by JAX's collectives and lax.ppermute only.
A program may use at most 128 MiB of HBM per device.

v0:
```python
import math

import jax
import jax.numpy as jnp
from jax import lax
from jax.sharding import PartitionSpec as P

BLOCK = 1024
FACTOR = 32


def shifted(block, axis, size, distance):
    route = [(i - distance, i) for i in range(size) if 0 <= i - distance < size]
    return lax.ppermute(block, axis, route)


def unit_wave(rows, cols, period, scale_rows):
    outer = rows // FACTOR
    hi = jnp.arange(outer, dtype=jnp.int32)[:, None] * (FACTOR * scale_rows)
    lo = jnp.arange(FACTOR, dtype=jnp.int32)[:, None] * scale_rows
    col = jnp.arange(cols, dtype=jnp.int32)[None, :]
    step = 2.0 * math.pi / period
    hi_phase = step * ((hi * col) % period).astype(jnp.float32)
    lo_phase = step * ((lo * col) % period).astype(jnp.float32)
    hc, hs = jnp.cos(hi_phase)[:, None, :], jnp.sin(hi_phase)[:, None, :]
    lc, ls = jnp.cos(lo_phase)[None, :, :], jnp.sin(lo_phase)[None, :, :]
    cos_t = (hc * lc - hs * ls).reshape(rows, cols)
    sin_t = (hs * lc + hc * ls).reshape(rows, cols)
    return cos_t, sin_t


def spectral_tables(tile_extent):
    period = 2 * tile_extent
    cos_f, sin_f = unit_wave(tile_extent, tile_extent, period, 1)
    alternating = jnp.where(jnp.arange(tile_extent) % 2 == 0, 1.0, -1.0).astype(jnp.float32)
    first_col = (jnp.arange(tile_extent) == 0)[None, :]
    forward = jnp.concatenate(
        [cos_f, jnp.where(first_col, alternating[:, None], -sin_f)], axis=1
    ).astype(jnp.bfloat16)
    cos_b, sin_b = unit_wave(tile_extent, period, period, 1)
    first_row = (jnp.arange(tile_extent) == 0)[:, None]
    alt_t = jnp.where(jnp.arange(period) % 2 == 0, 1.0, -1.0).astype(jnp.float32)[None, :]
    weights = jnp.where(first_row, 1.0, 2.0) / period
    inverse = jnp.concatenate(
        [weights * cos_b, jnp.where(first_row, alt_t / period, -(2.0 / period) * sin_b)], axis=0
    ).astype(jnp.bfloat16)
    return forward, inverse


def global_causal_smear(gate_wave, kernel_table_lines, leftover_lines, tile_extent):
    lane_total, context_extent = gate_wave.shape
    groups = context_extent // tile_extent
    forward, inverse = spectral_tables(tile_extent)
    slot0 = (jnp.arange(tile_extent) == 0)[None, None, :]
    source = gate_wave.reshape(lane_total * groups, tile_extent)
    kernel = kernel_table_lines.astype(jnp.bfloat16).reshape(lane_total * groups, tile_extent)
    spec_x = jnp.dot(source, forward, preferred_element_type=jnp.float32)
    spec_k = jnp.dot(kernel, forward, preferred_element_type=jnp.float32)
    spec_x = spec_x.reshape(lane_total, groups, 2 * tile_extent)
    spec_k = spec_k.reshape(lane_total, groups, 2 * tile_extent)
    x_re, x_im = spec_x[:, :, :tile_extent], spec_x[:, :, tile_extent:]
    k_re, k_im = spec_k[:, :, :tile_extent], spec_k[:, :, tile_extent:]
    pad = jnp.zeros((lane_total, groups - 1, tile_extent), jnp.float32)
    xp_re = jnp.concatenate([pad, x_re], axis=1)
    xp_im = jnp.concatenate([pad, x_im], axis=1)
    rr = ii = ri = ir = None
    for offset in range(groups):
        s_re = xp_re[:, groups - 1 - offset : 2 * groups - 1 - offset]
        s_im = xp_im[:, groups - 1 - offset : 2 * groups - 1 - offset]
        f_re = k_re[:, offset : offset + 1]
        f_im = k_im[:, offset : offset + 1]
        terms = (f_re * s_re, f_im * s_im, f_re * s_im, f_im * s_re)
        if rr is None:
            rr, ii, ri, ir = terms
        else:
            rr, ii, ri, ir = rr + terms[0], ii + terms[1], ri + terms[2], ir + terms[3]
    y_re = rr - jnp.where(slot0, 0.0, ii)
    y_im = jnp.where(slot0, ii, ri + ir)
    packed = jnp.concatenate([y_re, y_im], axis=2).astype(jnp.bfloat16)
    rows = jnp.dot(
        packed.reshape(lane_total * groups, 2 * tile_extent),
        inverse,
        preferred_element_type=jnp.float32,
    ).reshape(lane_total, groups, 2 * tile_extent)
    front_half = rows[:, :, :tile_extent]
    back_half = rows[:, :, tile_extent:]
    carried = jnp.concatenate(
        [jnp.zeros((lane_total, 1, tile_extent), jnp.float32), back_half[:, :-1]], axis=1
    )
    affine_mapping = (front_half + carried).reshape(lane_total, context_extent)
    wide = gate_wave.astype(jnp.float32)
    return (affine_mapping + leftover_lines[:, None] * wide).astype(jnp.bfloat16)


def short_conv(projected_float, local_taps, previous):
    context_extent = projected_float.shape[2]
    extended = jnp.concatenate([previous, projected_float], axis=2)
    result = jnp.zeros_like(projected_float)
    for offset in range(3):
        result = (
            result
            + local_taps[:, offset, :][:, :, None]
            * extended[:, :, 2 - offset : 2 - offset + context_extent]
        )
    return result


def make_shards(n_ctx, n_ch, tile_extent):
    def project(weight_local, whole_tokens):
        whole = lax.all_gather(weight_local, "ctx", axis=1, tiled=True)
        summed = jnp.einsum("pdc,ld->pcl", whole, whole_tokens, preferred_element_type=jnp.float32)
        return summed.astype(jnp.bfloat16)

    def featured(projected, taps):
        local_tokens = projected.shape[2]
        previous = shifted(projected[:, :, local_tokens - 2 :], "ctx", n_ctx, 1)
        return short_conv(projected.astype(jnp.float32), taps, previous.astype(jnp.float32))

    def shards(tokens, in_weight, short_taps, long_filter, skip_gain):
        local_tokens, local_features = tokens.shape
        copies = jnp.broadcast_to(tokens[None], (n_ch, local_tokens, local_features))
        pieces = lax.all_to_all(copies, "ch", split_axis=0, concat_axis=0, tiled=True)
        whole_tokens = pieces.transpose(1, 0, 2).reshape(local_tokens, n_ch * local_features)
        projected12 = project(in_weight[1:3], whole_tokens)
        embed12 = featured(projected12, short_taps[1:3])
        gate_wave = (embed12[0] * embed12[1]).astype(jnp.bfloat16)
        weight0, gate_wave = lax.optimization_barrier((in_weight[0:1], gate_wave))
        per_channel_view = lax.all_to_all(gate_wave, "ctx", split_axis=0, concat_axis=1, tiled=True)
        blended_lines = global_causal_smear(
            per_channel_view, long_filter[0], skip_gain[0], tile_extent
        )
        projected0 = project(weight0, whole_tokens)
        embed0 = featured(projected0, short_taps[0:1])
        by_token = lax.all_to_all(blended_lines, "ctx", split_axis=1, concat_axis=0, tiled=True)
        gated_output = (embed0[0] * by_token.astype(jnp.float32)).astype(jnp.bfloat16)
        return gated_output

    return shards


def solution(mesh):
    placed = (
        P("ctx", "ch"),
        P(None, "ctx", "ch"),
        P(None, None, "ch"),
        P("ch", "ctx", None),
        P("ch", "ctx"),
    )
    return jax.shard_map(
        make_shards(mesh.shape["ctx"], mesh.shape["ch"], BLOCK),
        mesh=mesh,
        in_specs=placed,
        out_specs=P("ch", "ctx"),
        check_vma=False,
    )
```

profile of v0, /device:TPU:1, one launch (start us, length us, event | category | flops | bytes accessed | tf_op | source)
XLA Modules:
  0.0 262.2 jit_solution(7263330939914112992)
XLA Ops:
  6.5 1.7 slice.293
  8.2 2.7 %broadcast_in_dim.101 = bf16[4,256,1024]{2,1,0:T(8,128)(2,1)} broadcast(bf16[256,1024]{1,0:T(8,128)(2,1)} %param.5), dimensions={1,2} | broadcast | bytes 2621440 | tf_op jit(solution)/shard_map/broadcast_in_dim | solution.py:121
  10.9 4.8 %all-to-all-start = ((bf16[4,256,1024]{2,1,0:T(8,128)(2,1)}), bf16[4,256,1024]{2,1,0:T(8,128)(2,1)S(1)}, u32[]{:S(2)}, u32[]{:S(2)}) async-start(bf16[4,256,1024]{2,1,0:T(8,128)(2,1)} %broadcast_in_dim.101), calls=%async_computation | async-start | bytes 4194304 | tf_op jit(solution)/shard_map/all_to_all | solution.py:122
  15.8 24.5 %all-to-all-done = bf16[4,256,1024]{2,1,0:T(8,128)(2,1)S(1)} async-done(((bf16[4,256,1024]{2,1,0:T(8,128)(2,1)}), bf16[4,256,1024]{2,1,0:T(8,128)(2,1)S(1)}, u32[]{:S(2)}, u32[]{:S(2)}) %all-to-all-start) | async-done | bytes 2097184 | tf_op jit(solution)/shard_map/all_to_all | solution.py:122
  40.2 3.0 %copy.14 = bf16[256,4,1024]{2,1,0:T(4,128)(2,1)} copy(bf16[256,4,1024]{2,0,1:T(8,128)(2,1)S(1)} %bitcast.163) | data formatting | bytes 4194304 | tf_op jit(solution)/shard_map/transpose | solution.py:123
  43.2 4.5 %reshape.317 = bf16[256,4096,1]{1,0,2:T(8,128)(2,1)} reshape(bf16[256,4,1024]{2,1,0:T(4,128)(2,1)} %copy.14) | data formatting | bytes 4194304 | tf_op jit(solution)/shard_map/reshape | solution.py:123
  47.7 65.9 %all-gather.3.cloned.1.call-done = bf16[2,4096,1024]{2,1,0:T(8,128)(2,1)} async-done(((bf16[2,64,1024]{2,1,0:T(8,128)(2,1)}), bf16[2,4096,1024]{2,1,0:T(8,128)(2,1)}) %all-gather.3.cloned.1.call-update) | async-done | bytes 16777232 | tf_op jit(solution)/shard_map/all_gather | solution.py:110
  113.6 12.3 %fusion.83 = (f32[2,1024,256]{1,2,0:T(8,128)}, bf16[2,1024,256]{1,2,0:T(8,128)(2,1)S(1)}) fusion(bf16[256,4096,1]{1,0,2:T(8,128)(2,1)} %reshape.317, bf16[2,4096,1024]{2,1,0:T(8,128)(2,1)} %all-gather.3.cloned.1.call-done), kind=kOutput, calls=%fused_computation.190 | convolution fusion | flops 4296015872 | bytes 22020096 | tf_op jit(solution)/shard_map/pdc,ld->pcl/dot_general | solution.py:111
  125.9 2.1 collective-permute-start
  128.0 1.6 slice.291
  129.6 3.8 %fusion.14 = f32[2,1024,256]{1,2,0:T(8,128)S(1)} fusion(f32[2,1024,2]{1,2,0:T(2,128)S(1)} %convert_element_type.112, f32[2,1024,256]{1,2,0:T(8,128)} %get-tuple-element.53, f32[2,1024]{1,0:T(2,128)S(1)} %get-tuple-element.57, f32[2,1024]{1,0:T(2,128)S(1)} %get-tuple-element.58, f32[2,1024]{1,0:T(2,128)S(1)} %bitcast.237), kind=kLoop, calls=%fused_computation.55 | loop fusion | flops 3670016 | bytes 4235264 | tf_op jit(solution)/shard_map/add | solution.py:101
  133.5 1.3 convert_element_type.122
  134.8 1.0 convert_element_type.123
  137.0 0.8 add_negate_fusion
  137.8 0.8 subtract_convert_fusion
  139.0 1.3 fusion.10
  140.6 0.9 fusion.78
  141.6 0.6 copy.100
  142.3 0.6 copy.101
  142.9 0.6 copy.102
  143.5 0.6 copy.103
  144.2 0.6 copy.104
  144.8 0.6 copy.105
  145.4 0.6 copy.106
  146.1 0.6 copy.107
  146.7 0.6 copy.108
  147.4 0.6 copy.109
  148.0 0.6 copy.110
  148.7 0.6 copy.111
  149.3 0.6 copy.125
  150.0 1.0 fusion.52
  151.0 1.1 fusion.55
  152.1 1.6 add_multiply_fusion
  153.7 2.8 %fusion.3 = bf16[1024,2048]{1,0:T(8,128)(2,1)} fusion(bf16[32,32,2048]{2,1,0:T(8,128)(2,1)S(1)} %add_multiply_fusion, bf16[2048]{0:T(1024)(128)(2,1)S(1)} %select_multiply_fusion, pred[1024]{0:T(1024)(128)(4,1)S(1)} %iota_compare_fusion), kind=kLoop, calls=%fused_computation.5 | loop fusion | flops 2097152 | bytes 8393728 | tf_op jit(solution)/shard_map/convert.3
  156.5 4.5 %multiply_subtract_fusion = f32[32,32,2048]{2,1,0:T(8,128)} fusion(f32[32,2048]{1,0:T(8,128)S(1)} %get-tuple-element.55, f32[32,2048]{1,0:T(8,128)S(1)} %get-tuple-element.52, f32[32,2048]{1,0:T(8,128)S(1)} %get-tuple-element.56, f32[32,2048]{1,0:T(8,128)S(1)} %get-tuple-element.51), kind=kLoop, calls=%fused_computation.11 | loop fusion | flops 6291456 | bytes 9437184 | tf_op jit(solution)/shard_map/sub | solution.py:27
  161.0 1.2 copy.15
  162.2 8.5 %all-to-all-start.1 = ((bf16[64,16,256]{2,1,0:T(8,128)(2,1)}), bf16[64,16,256]{2,1,0:T(8,128)(2,1)S(1)}, u32[]{:S(2)}, u32[]{:S(2)}) async-start(bf16[64,16,256]{2,1,0:T(8,128)(2,1)} %bitcast.14), calls=%async_computation.1 | async-start | bytes 1048576 | tf_op jit(solution)/shard_map/all_to_all | solution.py:128
  170.7 5.3 %fusion.79 = (f32[16,1,1024]{2,1,0:T(1,128)S(1)}, f32[16,1,1024]{2,1,0:T(1,128)S(1)}, f32[16,1,1024]{2,1,0:T(1,128)S(1)}, f32[16,1,1024]{2,1,0:T(1,128)S(1)}, f3...) fusion(f32[16,16,2048]{2,1,0:T(8,128)} %bitcast.171), kind=kLoop, calls=%fused_computation.186 | loop fusion | bytes 1703936 | tf_op jit(solution)/shard_map/slice | solution.py:70
  176.6 0.6 copy.113
  177.9 0.6 copy.115
  178.5 0.6 copy.116
  179.2 0.6 copy.117
  179.8 0.6 copy.118
  180.5 0.6 copy.119
  181.1 0.6 copy.120
  181.7 0.6 copy.121
  183.0 0.6 copy.123
  183.7 0.6 copy.124
  184.3 5.9 %fusion.4 = bf16[1024,2048]{1,0:T(8,128)(2,1)} fusion(f32[32,32,2048]{2,1,0:T(8,128)} %multiply_subtract_fusion, f32[1024]{0:T(1024)S(1)} %select_multiply_fusion.1), kind=kLoop, calls=%fused_computation.7 | loop fusion | flops 4194304 | bytes 12587008 | tf_op jit(solution)/shard_map/convert.2
  190.3 1.1 dot_general.23
  191.4 3.8 %fusion.7 = f32[16,16,2048]{2,1,0:T(8,128)S(1)} fusion(bf16[16,16,1024]{2,1,0:T(8,128)(2,1)} %dot_general.23, bf16[1024,1024]{1,0:T(8,128)(2,1)} %copy-done.3, bf16[1024,1024]{1,0:T(8,128)(2,1)} %bitcast.169), kind=kOutput, calls=%fused_computation.43 | convolution fusion | flops 1082130432 | bytes 6815744 | tf_op jit(solution)/shard_map/dot_general | solution.py:57
  196.8 4.5 %subtract_convert_fusion.1 = bf16[16,16,1024]{2,1,0:T(8,128)(2,1)S(1)} fusion(f32[16,16,1024]{2,1,0:T(8,128)S(1)} %get-tuple-element.42, f32[16,1024]{1,0:T(8,128)S(1)} %bitcast.205, f32[16,1024]{1,0:T(8,128)S(1)} %bitcast.207, f32[16,1024]{1,0:T(8,128)S(1)} %bitcast.211, f32[16,1024]{1,0:T(8,128)S(1)} %bitcast.213, f32[16,1024]{1,0:T(8,128)S(1)} %bitcast.215, ...), kind=kLoop, calls=%fused_computation.83 | loop fusion | flops 17039360 | bytes 4719616 | tf_op jit(solution)/shard_map/convert.4
  201.3 5.2 %select_convert_fusion = bf16[16,16,1024]{2,1,0:T(8,128)(2,1)S(1)} fusion(f32[16,16,1024]{2,1,0:T(8,128)S(1)} %get-tuple-element.42, f32[16,16,1024]{2,1,0:T(8,128)S(1)} %get-tuple-element.41, f32[16,1024]{1,0:T(8,128)S(1)} %bitcast.174, f32[16,1024]{1,0:T(8,128)S(1)} %bitcast.176, f32[16,1024]{1,0:T(8,128)S(1)} %bitcast.178, f32[16,1024]{1,0:T(8,128)S(1)} %bitcast.180, ...), kind=kLoop, calls=%fused_computation.82 | loop fusion | flops 25165824 | bytes 4719616 | tf_op jit(solution)/shard_map/convert.5
  206.5 2.4 fusion
  209.0 1.2 slice_add_fusion
  210.2 2.6 reshape.315
  212.7 2.6 %fusion.32 = bf16[16,64,256]{2,0,1:T(8,128)(2,1)} fusion(f32[16,64,256]{2,1,0:T(8,128)} %reshape.315, f32[16]{0:T(128)S(1)} %bitcast.241, bf16[64,16,256]{2,1,0:T(8,128)(2,1)S(1)} %all-to-all-done.1), kind=kLoop, calls=%fused_computation.81 | loop fusion | flops 1048576 | bytes 2097216 | tf_op jit(solution)/shard_map/convert_element_type | solution.py:92
  215.4 10.3 %all-to-all-start.2 = ((bf16[16,64,256]{2,0,1:T(8,128)(2,1)}), bf16[16,64,256]{2,0,1:T(8,128)(2,1)S(1)}, u32[]{:S(2)}, u32[]{:S(2)}) async-start(bf16[16,64,256]{2,0,1:T(8,128)(2,1)} %fusion.32), calls=%async_computation.2 | async-start | bytes 1048576 | tf_op jit(solution)/shard_map/all_to_all | solution.py:134
  225.7 0.8 fusion.81
  226.6 1.6 copy.55
  228.1 14.9 %all-to-all-done.2 = bf16[16,64,256]{2,0,1:T(8,128)(2,1)S(1)} async-done(((bf16[16,64,256]{2,0,1:T(8,128)(2,1)}), bf16[16,64,256]{2,0,1:T(8,128)(2,1)S(1)}, u32[]{:S(2)}, u32[]{:S(2)}) %all-to-all-start.2) | async-done | bytes 524320 | tf_op jit(solution)/shard_map/all_to_all | solution.py:134
  243.5 6.3 %fusion.16 = bf16[1024,256]{0,1:T(8,128)(2,1)S(1)} fusion(bf16[256,4096]{1,0:T(8,128)(2,1)} %bitcast.172, bf16[1,4096,1024]{2,1,0:T(8,128)(2,1)} %all-gather.5.cloned.1.call-done), kind=kOutput, calls=%fused_computation.61 | convolution fusion | flops 2147745792 | bytes 11010048 | tf_op jit(solution)/shard_map/pdc,ld->pcl/dot_general | solution.py:111
  249.9 3.3 %collective-permute-start.1 = (bf16[1,1024,2]{1,2,0:T(2,128)(2,1)S(1)}, bf16[1,1024,2]{1,2,0:T(2,128)(2,1)S(1)}, u32[]{:S(2)}, u32[]{:S(2)}) collective-permute-start(bf16[1,1024,2]{1,2,0:T(2,128)(2,1)S(1)} %slice.377), channel_id=1, source_target_pairs={{0,4},{4,8},{8,12},{12,16},{16,20},{20,24},{24,28},{28,32},{32,36}... | collective-permute-start | bytes 12296 | tf_op jit(solution)/shard_map/ppermute | solution.py:14
  254.4 1.0 copy.19
  (108 shorter events, 7.1 us)
Async XLA Ops:
  6.5 9.2 %copy-start.32 = (f32[3,3,1024]{2,1,0:T(4,128)S(1)}, f32[3,3,1024]{2,1,0:T(4,128)}, u32[]{:S(2)}) copy-start(f32[3,3,1024]{2,1,0:T(4,128)} %param.7) | copy-start | bytes 110596
  6.5 107.1 %all-gather.3.cloned.1.call-start = ((), (), s32[]{:S(2)}) async-start(), calls=%async_computation.3 | async-start | bytes 17039360 | tf_op jit(solution)/shard_map/all_gather | solution.py:110
  10.9 29.3 %all-to-all-start = ((bf16[4,256,1024]{2,1,0:T(8,128)(2,1)}), bf16[4,256,1024]{2,1,0:T(8,128)(2,1)S(1)}, u32[]{:S(2)}, u32[]{:S(2)}) async-start(bf16[4,256,1024]{2,1,0:T(8,128)(2,1)} %broadcast_in_dim.101), calls=%async_computation | async-start | bytes 4194304 | tf_op jit(solution)/shard_map/all_to_all | solution.py:122
  15.7 227.8 %all-gather.5.cloned.1.call-start = ((), (), s32[]{:S(2)}) async-start(), calls=%async_computation.4 | async-start | bytes 8519680 | tf_op jit(solution)/shard_map/all_gather | solution.py:110
  125.9 3.7 %collective-permute-start = (bf16[2,1024,2]{1,2,0:T(2,128)(2,1)S(1)}, bf16[2,1024,2]{1,2,0:T(2,128)(2,1)S(1)}, u32[]{:S(2)}, u32[]{:S(2)}) collective-permute-start(bf16[2,1024,2]{1,2,0:T(2,128)(2,1)S(1)} %slice.372), channel_id=1, source_target_pairs={{0,4},{4,8},{8,12},{12,16},{16,20},{20,24},{24,28},{28,32},{32,36}... | collective-permute-start | bytes 24584 | tf_op jit(solution)/shard_map/ppermute | solution.py:14
  137.0 2.0 copy-start.31
  138.6 1.7 copy-start.2
  139.0 1.6 copy-start.3
  140.6 11.5 %copy-start.4 = (f32[2048,256]{0,1:T(8,128)}, f32[2048,256]{0,1:T(8,128)S(1)}, u32[]{:S(2)}) copy-start(f32[2048,256]{0,1:T(8,128)S(1)} %fusion.10) | copy-start | bytes 6291460
  162.2 28.0 %all-to-all-start.1 = ((bf16[64,16,256]{2,1,0:T(8,128)(2,1)}), bf16[64,16,256]{2,1,0:T(8,128)(2,1)S(1)}, u32[]{:S(2)}, u32[]{:S(2)}) async-start(bf16[64,16,256]{2,1,0:T(8,128)(2,1)} %bitcast.14), calls=%async_computation.1 | async-start | bytes 1048576 | tf_op jit(solution)/shard_map/all_to_all | solution.py:128
  195.3 0.8 copy-start.5
  195.3 0.9 copy-start.6
  195.3 0.9 copy-start.7
  195.3 0.9 copy-start.8
  195.3 0.9 copy-start.9
  195.3 1.0 copy-start.10
  195.3 1.0 copy-start.11
  195.4 1.0 copy-start.12
  195.4 1.0 copy-start.13
  195.4 1.0 copy-start.14
  195.4 1.1 copy-start.15
  195.4 1.1 copy-start.16
  195.4 1.1 copy-start.17
  195.4 1.1 copy-start.18
  195.4 1.1 copy-start.19
  195.4 1.1 copy-start.20
  195.4 1.1 copy-start.21
  195.5 1.1 copy-start.22
  195.5 1.2 copy-start.23
  195.5 1.2 copy-start.24
  195.5 1.2 copy-start.25
  195.5 1.2 copy-start.26
  195.5 1.2 copy-start.27
  195.5 1.2 copy-start.28
  195.5 1.2 copy-start.29
  195.5 1.2 copy-start.30
  196.8 9.7 %copy-start = (bf16[1024,2048]{1,0:T(8,128)(2,1)S(1)}, bf16[1024,2048]{1,0:T(8,128)(2,1)}, u32[]{:S(2)}) copy-start(bf16[1024,2048]{1,0:T(8,128)(2,1)} %fusion.3) | copy-start | bytes 12582916
  196.8 9.8 %copy-start.1 = (bf16[1024,2048]{1,0:T(8,128)(2,1)S(1)}, bf16[1024,2048]{1,0:T(8,128)(2,1)}, u32[]{:S(2)}) copy-start(bf16[1024,2048]{1,0:T(8,128)(2,1)} %fusion.4) | copy-start | bytes 12582916
  208.9 3.8 %copy-start.33 = (f32[1,16]{1,0:T(1,128)S(1)}, f32[1,16]{1,0:T(1,128)}, u32[]{:S(2)}) copy-start(f32[1,16]{1,0:T(1,128)} %param.9) | copy-start | bytes 196
  215.4 27.6 %all-to-all-start.2 = ((bf16[16,64,256]{2,0,1:T(8,128)(2,1)}), bf16[16,64,256]{2,0,1:T(8,128)(2,1)S(1)}, u32[]{:S(2)}, u32[]{:S(2)}) async-start(bf16[16,64,256]{2,0,1:T(8,128)(2,1)} %fusion.32), calls=%async_computation.2 | async-start | bytes 1048576 | tf_op jit(solution)/shard_map/all_to_all | solution.py:134
  249.9 4.1 %collective-permute-start.1 = (bf16[1,1024,2]{1,2,0:T(2,128)(2,1)S(1)}, bf16[1,1024,2]{1,2,0:T(2,128)(2,1)S(1)}, u32[]{:S(2)}, u32[]{:S(2)}) collective-permute-start(bf16[1,1024,2]{1,2,0:T(2,128)(2,1)S(1)} %slice.377), channel_id=1, source_target_pairs={{0,4},{4,8},{8,12},{12,16},{16,20},{20,24},{24,28},{28,32},{32,36}... | collective-permute-start | bytes 12296 | tf_op jit(solution)/shard_map/ppermute | solution.py:14
Sparse Core Ops, SparseCore 0:
  10.1 103.4 all-gather.2
  133.7 82.5 all-gather.4
where the time goes:
time: 264 us; the launch traced here: 262 us
  waiting for transfers between devices  106 us (40%)
  local copies, waits for them, and re-layouts  47.8 us (18%)
  other arithmetic  39.4 us (15%)
  starting transfers between devices  29 us (11%)
  matrix products  26.1 us (10%)
  between operations  14 us (5%)
    all_gather x2, waiting for transfers between devices, project(): whole = lax.all_gather(weight_local, 'ctx', axis=1, tiled=True)  65.9 us
    all_to_all x1, waiting for transfers between devices, shards(): lax.all_to_all(copies, 'ch', split_axis=0, concat_axis=0, tiled=True)  24.5 us
    another operation x6, other arithmetic  19.6 us
    dot_general x2, matrix products, project(): jnp.einsum('pdc,ld->pcl', whole, whole_tokens, preferred_element_type=jnp...  18.6 us
    unnamed x102, local copies, waits for them, and re-layouts  18 us
    all_to_all x1, waiting for transfers between devices, shards(): lax.all_to_all(blended_lines, 'ctx', split_axis=1, concat_axis=0, tiled=T...  14.9 us
    all_to_all x1, starting transfers between devices, shards(): lax.all_to_all(blended_lines, 'ctx', split_axis=1, concat_axis=0, tiled=T...  10.3 us
    all_to_all x1, starting transfers between devices, shards(): lax.all_to_all(gate_wave, 'ctx', split_axis=0, concat_axis=1, tiled=True)  8.45 us
  transfers between devices with their start and end apart: 7, of which 4 were waited for; matrix products, arithmetic and copies ran while one was open for 33% of the time, Pallas kernels for 0%

commit v1 on v0

--- a/solution.py
+++ b/solution.py
@@ -47,17 +47,26 @@
     return forward, inverse
 
 
-def global_causal_smear(gate_wave, kernel_table_lines, leftover_lines, tile_extent):
+def filter_spectra(kernel_table_lines, forward, tile_extent):
+    lane_total, context_extent = kernel_table_lines.shape
+    groups = context_extent // tile_extent
+    kernel = (
+        kernel_table_lines.astype(jnp.bfloat16)
+        .reshape(lane_total, groups, tile_extent)
+        .transpose(1, 0, 2)
+        .reshape(groups * lane_total, tile_extent)
+    )
+    spec_k = jnp.dot(kernel, forward, preferred_element_type=jnp.float32)
+    return spec_k.reshape(groups, lane_total, 2 * tile_extent)
+
+
+def global_causal_smear(gate_wave, spec_k, leftover_lines, forward, inverse, tile_extent):
     lane_total, context_extent = gate_wave.shape
     groups = context_extent // tile_extent
-    forward, inverse = spectral_tables(tile_extent)
     slot0 = (jnp.arange(tile_extent) == 0)[None, None, :]
     source = gate_wave.reshape(lane_total * groups, tile_extent)
-    kernel = kernel_table_lines.astype(jnp.bfloat16).reshape(lane_total * groups, tile_extent)
     spec_x = jnp.dot(source, forward, preferred_element_type=jnp.float32)
-    spec_k = jnp.dot(kernel, forward, preferred_element_type=jnp.float32)
     spec_x = spec_x.reshape(lane_total, groups, 2 * tile_extent)
-    spec_k = spec_k.reshape(lane_total, groups, 2 * tile_extent)
     x_re, x_im = spec_x[:, :, :tile_extent], spec_x[:, :, tile_extent:]
     k_re, k_im = spec_k[:, :, :tile_extent], spec_k[:, :, tile_extent:]
     pad = jnp.zeros((lane_total, groups - 1, tile_extent), jnp.float32)
@@ -67,8 +76,8 @@
     for offset in range(groups):
         s_re = xp_re[:, groups - 1 - offset : 2 * groups - 1 - offset]
         s_im = xp_im[:, groups - 1 - offset : 2 * groups - 1 - offset]
-        f_re = k_re[:, offset : offset + 1]
-        f_im = k_im[:, offset : offset + 1]
+        f_re = k_re[offset][:, None, :]
+        f_im = k_im[offset][:, None, :]
         terms = (f_re * s_re, f_im * s_im, f_re * s_im, f_im * s_re)
         if rr is None:
             rr, ii, ri, ir = terms
@@ -106,11 +115,6 @@
 
 
 def make_shards(n_ctx, n_ch, tile_extent):
-    def project(weight_local, whole_tokens):
-        whole = lax.all_gather(weight_local, "ctx", axis=1, tiled=True)
-        summed = jnp.einsum("pdc,ld->pcl", whole, whole_tokens, preferred_element_type=jnp.float32)
-        return summed.astype(jnp.bfloat16)
-
     def featured(projected, taps):
         local_tokens = projected.shape[2]
         previous = shifted(projected[:, :, local_tokens - 2 :], "ctx", n_ctx, 1)
@@ -121,18 +125,26 @@
         copies = jnp.broadcast_to(tokens[None], (n_ch, local_tokens, local_features))
         pieces = lax.all_to_all(copies, "ch", split_axis=0, concat_axis=0, tiled=True)
         whole_tokens = pieces.transpose(1, 0, 2).reshape(local_tokens, n_ch * local_features)
-        projected12 = project(in_weight[1:3], whole_tokens)
-        embed12 = featured(projected12, short_taps[1:3])
-        gate_wave = (embed12[0] * embed12[1]).astype(jnp.bfloat16)
-        weight0, gate_wave = lax.optimization_barrier((in_weight[0:1], gate_wave))
+        whole_weight = lax.all_gather(in_weight, "ctx", axis=1, tiled=True)
+        forward, inverse = spectral_tables(tile_extent)
+        spec_k = filter_spectra(long_filter[0], forward, tile_extent)
+        whole_weight, forward, inverse, spec_k = lax.optimization_barrier(
+            (whole_weight, forward, inverse, spec_k)
+        )
+        summed = jnp.einsum(
+            "pdc,ld->pcl", whole_weight, whole_tokens, preferred_element_type=jnp.float32
+        )
+        embedding_result = featured(summed.astype(jnp.bfloat16), short_taps)
+        gate_wave = (embedding_result[1] * embedding_result[2]).astype(jnp.bfloat16)
         per_channel_view = lax.all_to_all(gate_wave, "ctx", split_axis=0, concat_axis=1, tiled=True)
         blended_lines = global_causal_smear(
-            per_channel_view, long_filter[0], skip_gain[0], tile_extent
+            per_channel_view, spec_k, skip_gain[0], forward, inverse, tile_extent
         )
-        projected0 = project(weight0, whole_tokens)
-        embed0 = featured(projected0, short_taps[0:1])
-        by_token = lax.all_to_all(blended_lines, "ctx", split_axis=1, concat_axis=0, tiled=True)
-        gated_output = (embed0[0] * by_token.astype(jnp.float32)).astype(jnp.bfloat16)
+        lanes, span = blended_lines.shape
+        outgoing = blended_lines.reshape(lanes, n_ctx, span // n_ctx).transpose(1, 0, 2)
+        returned = lax.all_to_all(outgoing, "ctx", split_axis=0, concat_axis=0, tiled=True)
+        by_token = returned.reshape(n_ctx * lanes, span // n_ctx)
+        gated_output = (embedding_result[0] * by_token.astype(jnp.float32)).astype(jnp.bfloat16)
         return gated_output
 
     return shards

time: 264 us -> 246 us (0.932)
  blocking collectives: 0 us -> 23.4 us
  local copies, waits for them, and re-layouts: 47.8 us -> 27.8 us
  starting transfers between devices: 29 us -> 16 us
  matrix products: 26.1 us -> 20.4 us
  waiting for transfers between devices: 106 us -> 101 us
  other arithmetic: 39.4 us -> 42.4 us
    all_to_all x1, waiting for transfers between devices: 24.5 us -> 0.01 us  [shards(): lax.all_to_all(copies, 'ch', split_axis=0, concat_axis=0, tiled=True)]
    all_to_all x0 -> x1, blocking collectives: none -> 23.4 us  [shards(): lax.all_to_all(outgoing, 'ctx', split_axis=0, concat_axis=0, tiled=True)]
    all_gather x2 -> x1, waiting for transfers between devices: 65.9 us -> 86 us  [shards(): whole_weight = lax.all_gather(in_weight, 'ctx', axis=1, tiled=True)]
    unnamed x102 -> x65, local copies, waits for them, and re-layouts: 18 us -> 0.44 us
    all_to_all x1 -> x0, waiting for transfers between devices: 14.9 us -> none  [shards(): lax.all_to_all(blended_lines, 'ctx', split_axis=1, concat_axis=0, tiled=T...]
    all_to_all x1, waiting for transfers between devices: 0.01 us -> 12.9 us  [shards(): lax.all_to_all(gate_wave, 'ctx', split_axis=0, concat_axis=1, tiled=True)]
    concatenate x0 -> x2, other arithmetic: none -> 10.9 us  [the longest x1 8.41 us: spectral_tables(): jnp.concatenate([weights * cos_b, jnp.where(first_row, alt_t / period, -(...]
    all_to_all x1 -> x0, starting transfers between devices: 10.3 us -> none  [shards(): lax.all_to_all(blended_lines, 'ctx', split_axis=1, concat_axis=0, tiled=T...]
  transfers between devices with their start and end apart: 7 -> 4, of which waited for: 4 -> 3; matrix products, arithmetic and copies ran while one was open for 33% -> 17% of each run, Pallas kernels for 0% -> 0%
where the time goes in v1:
time: 246 us; the launch traced here: 245 us
  waiting for transfers between devices  101 us (41%)
  other arithmetic  42.4 us (17%)
  local copies, waits for them, and re-layouts  27.8 us (11%)
  blocking collectives  23.4 us (10%)
  matrix products  20.4 us (8%)
  starting transfers between devices  16 us (7%)
  between operations  14.1 us (6%)
    all_gather x1, waiting for transfers between devices, shards(): whole_weight = lax.all_gather(in_weight, 'ctx', axis=1, tiled=True)  86 us
    all_to_all x1, blocking collectives, shards(): lax.all_to_all(outgoing, 'ctx', split_axis=0, concat_axis=0, tiled=True)  23.4 us
    another operation x6, other arithmetic  16.2 us
    all_to_all x1, waiting for transfers between devices, shards(): lax.all_to_all(gate_wave, 'ctx', split_axis=0, concat_axis=1, tiled=True)  12.9 us
    dot_general x1, matrix products, shards(): jnp.einsum('pdc,ld->pcl', whole_weight, whole_tokens, preferred_element_t...  11.6 us
    all_to_all x1, starting transfers between devices, shards(): lax.all_to_all(gate_wave, 'ctx', split_axis=0, concat_axis=1, tiled=True)  9.28 us
    concatenate x1, other arithmetic, spectral_tables(): jnp.concatenate([weights * cos_b, jnp.where(first_row, alt_t / period, -(...  8.41 us
  transfers between devices with their start and end apart: 4, of which 3 were waited for; matrix products, arithmetic and copies ran while one was open for 17% of the time, Pallas kernels for 0%

profile of v1, /device:TPU:1, one launch (start us, length us, event | category | flops | bytes accessed | tf_op | source)
XLA Modules:
  0.0 244.7 jit_solution(10390779374928449564)
XLA Ops:
  6.5 0.0 all-gather.2.cloned.1.call-start
  6.5 0.7 all-gather.2.cloned.1.call-update
  7.3 2.7 %broadcast_in_dim.110 = bf16[4,256,1024]{2,1,0:T(8,128)(2,1)} broadcast(bf16[256,1024]{1,0:T(8,128)(2,1)} %param.5), dimensions={1,2} | broadcast | bytes 2621440 | tf_op jit(solution)/shard_map/broadcast_in_dim | solution.py:125
  9.9 4.8 %all-to-all-start = ((bf16[4,256,1024]{2,1,0:T(8,128)(2,1)}), bf16[4,256,1024]{2,1,0:T(8,128)(2,1)S(1)}, u32[]{:S(2)}, u32[]{:S(2)}) async-start(bf16[4,256,1024]{2,1,0:T(8,128)(2,1)} %broadcast_in_dim.110), calls=%async_computation | async-start | bytes 4194304 | tf_op jit(solution)/shard_map/all_to_all | solution.py:126
  14.8 0.0 copy-done
  14.8 0.1 convert_element_type.97
  14.8 0.3 copy.30
  15.1 0.3 copy.20
  15.5 0.5 fusion.48
  16.0 0.6 fusion.51
  16.6 1.0 fusion.38
  17.6 0.8 add_negate_fusion
  18.4 0.8 subtract_convert_fusion
  19.3 0.3 fusion.6
  19.6 2.5 %pad_maximum_fusion.1 = bf16[1024,2048]{1,0:T(8,128)(2,1)} fusion(bf16[1024,1024]{1,0:T(8,128)(2,1)S(1)} %fusion.6, bf16[1024,1024]{1,0:T(8,128)(2,1)S(1)} %bitcast.122), kind=kLoop, calls=%fused_computation.39 | loop fusion | flops 8388608 | bytes 8388608 | tf_op jit(solution)/shard_map/concatenate | solution.py:37
  22.1 2.6 %fusion.62 = f32[2048,256]{0,1:T(8,128)} fusion(bf16[256,1024]{1,0:T(8,128)(2,1)S(1)} %bitcast.129, bf16[1024,1024]{1,0:T(8,128)(2,1)S(1)} %fusion.6, bf16[1024,1024]{1,0:T(8,128)(2,1)S(1)} %bitcast.123), kind=kOutput, calls=%fused_computation.168 | convolution fusion | flops 1082130432 | bytes 6815744 | tf_op jit(solution)/shard_map/dot_general | solution.py:59
  24.7 1.1 fusion.41
  25.8 1.6 add_multiply_fusion
  27.4 2.8 %fusion.2 = bf16[1024,2048]{1,0:T(8,128)(2,1)} fusion(bf16[32,32,2048]{2,1,0:T(8,128)(2,1)S(1)} %add_multiply_fusion, bf16[2048]{0:T(1024)(128)(2,1)S(1)} %select_multiply_fusion, pred[1024]{0:T(1024)(128)(4,1)S(1)} %iota_compare_fusion), kind=kLoop, calls=%fused_computation.4 | loop fusion | flops 2097152 | bytes 8393728 | tf_op jit(solution)/shard_map/convert.4
  30.2 1.2 multiply_subtract_fusion
  31.5 0.0 copy-done.27
  31.5 2.5 %fusion.3 = bf16[1024,2048]{1,0:T(8,128)(2,1)} fusion(f32[32,32,2048]{2,1,0:T(8,128)S(1)} %multiply_subtract_fusion, f32[1024]{0:T(1024)S(1)} %select_multiply_fusion.1), kind=kLoop, calls=%fused_computation.6 | loop fusion | flops 4194304 | bytes 12587008 | tf_op jit(solution)/shard_map/convert.3
  34.0 8.4 %pad_maximum_fusion = bf16[2048,2048]{1,0:T(8,128)(2,1)} fusion(bf16[1024,2048]{1,0:T(8,128)(2,1)} %fusion.2, bf16[1024,2048]{1,0:T(8,128)(2,1)} %fusion.3), kind=kLoop, calls=%fused_computation | loop fusion | flops 16777216 | bytes 16777216 | tf_op jit(solution)/shard_map/concatenate | solution.py:44
  42.4 0.0 all-to-all-done
  42.4 3.1 %copy.21 = bf16[256,4,1024]{2,1,0:T(4,128)(2,1)} copy(bf16[256,4,1024]{2,0,1:T(8,128)(2,1)S(1)} %bitcast.121) | data formatting | bytes 4194304 | tf_op jit(solution)/shard_map/transpose | solution.py:127
  45.6 3.3 %reshape.337 = bf16[256,4096,1]{1,0,2:T(8,128)(2,1)S(1)} reshape(bf16[256,4,1024]{2,1,0:T(4,128)(2,1)} %copy.21) | data formatting | bytes 4194304 | tf_op jit(solution)/shard_map/reshape | solution.py:127
  48.8 86.0 %all-gather.2.cloned.1.call-done = bf16[3,4096,1024]{2,1,0:T(8,128)(2,1)} async-done(((bf16[3,64,1024]{2,1,0:T(8,128)(2,1)}), bf16[3,4096,1024]{2,1,0:T(8,128)(2,1)}) %all-gather.2.cloned.1.call-update) | async-done | bytes 25165840 | tf_op jit(solution)/shard_map/all_gather | solution.py:128
  134.9 11.6 %fusion.65 = (f32[3,1024,256]{1,2,0:T(8,128)S(1)}, bf16[3,1024,256]{1,2,0:T(8,128)(2,1)S(1)}) fusion(bf16[256,4096,1]{1,0,2:T(8,128)(2,1)S(1)} %reshape.337, bf16[3,4096,1024]{2,1,0:T(8,128)(2,1)} %all-gather.2.cloned.1.call-done), kind=kOutput, calls=%fused_computation.171 | convolution fusion | flops 6444023808 | bytes 31981568 | tf_op jit(solution)/shard_map/pdc,ld->pcl/dot_general | solution.py:134
  146.5 1.9 collective-permute-start
  148.5 1.1 collective-permute-done
  149.6 0.9 fusion.10
  150.5 0.9 fusion.12
  151.5 2.0 copy.22
  153.5 9.3 %all-to-all-start.1 = ((bf16[64,16,256]{2,1,0:T(8,128)(2,1)}), bf16[64,16,256]{2,1,0:T(8,128)(2,1)}, u32[]{:S(2)}, u32[]{:S(2)}) async-start(bf16[64,16,256]{2,1,0:T(8,128)(2,1)} %bitcast.127), calls=%async_computation.1 | async-start | bytes 1048576 | tf_op jit(solution)/shard_map/all_to_all | solution.py:139
  162.8 2.1 slice_bitcast_fusion.31
  164.9 2.2 slice_bitcast_fusion.32
  167.1 12.9 %all-to-all-done.1 = bf16[64,16,256]{2,1,0:T(8,128)(2,1)} async-done(((bf16[64,16,256]{2,1,0:T(8,128)(2,1)}), bf16[64,16,256]{2,1,0:T(8,128)(2,1)}, u32[]{:S(2)}, u32[]{:S(2)}) %all-to-all-start.1) | async-done | bytes 524320 | tf_op jit(solution)/shard_map/all_to_all | solution.py:139
  180.0 2.0 copy.23
  182.0 2.2 dot_general.19
  184.2 0.0 copy-start.5
  184.2 0.0 copy-start.6
  184.2 0.0 copy-start.7
  184.2 0.0 copy-start.8
  184.2 0.0 copy-start.9
  184.2 0.0 copy-start.10
  184.2 0.0 copy-start.11
  184.4 0.0 slice-start
  184.4 3.8 %fusion.4 = f32[16,16,2048]{2,1,0:T(8,128)S(1)} fusion(bf16[16,16,1024]{2,1,0:T(8,128)(2,1)} %dot_general.19, bf16[1024,2048]{1,0:T(8,128)(2,1)} %pad_maximum_fusion.1), kind=kOutput, calls=%fused_computation.40 | convolution fusion | flops 1073741824 | bytes 6815744 | tf_op jit(solution)/shard_map/dot_general | solution.py:68
  188.2 0.0 slice-start.1
  188.2 0.2 fusion.63
  188.7 4.5 %subtract_convert_fusion.1 = bf16[16,16,1024]{2,1,0:T(8,128)(2,1)S(1)} fusion(f32[16,16,1024]{2,1,0:T(8,128)S(1)} %get-tuple-element.46, f32[16,1024]{1,0:T(8,128)S(1)} %copy-done.12, f32[16,1024]{1,0:T(8,128)S(1)} %copy-done.13, f32[16,1024]{1,0:T(8,128)S(1)} %copy-done.15, f32[16,1024]{1,0:T(8,128)S(1)} %copy-done.16, f32[16,1024]{1,0:T(8,128)S(1)} %copy-done.17, ...), kind=kLoop, calls=%fused_computation.67 | loop fusion | flops 17039360 | bytes 4719616 | tf_op jit(solution)/shard_map/convert.1
  193.3 5.2 %select_convert_fusion = bf16[16,16,1024]{2,1,0:T(8,128)(2,1)S(1)} fusion(f32[16,16,1024]{2,1,0:T(8,128)S(1)} %get-tuple-element.46, f32[16,16,1024]{2,1,0:T(8,128)S(1)} %get-tuple-element.45, f32[16,1024]{1,0:T(8,128)S(1)} %get-tuple-element.14, f32[16,1024]{1,0:T(8,128)S(1)} %get-tuple-element.15, f32[16,1024]{1,0:T(8,128)S(1)} %get-tuple-element.16, ...), kind=kLoop, calls=%fused_computation.66 | loop fusion | flops 25165824 | bytes 4719616 | tf_op jit(solution)/shard_map/convert.2
  198.5 2.4 fusion
  200.9 0.0 copy-start.28
  200.9 0.1 slice.345
  201.0 1.2 slice_add_fusion
  202.2 2.5 %reshape.335 = f32[16,64,256]{2,1,0:T(8,128)} reshape(f32[16,16,1024]{2,1,0:T(8,128)} %slice_add_fusion) | data formatting | bytes 2097152 | tf_op jit(solution)/shard_map/reshape | solution.py:99
  204.7 0.0 copy-done.28
  204.7 2.0 fusion.19
  206.7 23.4 %all_to_all.23 = bf16[64,16,256]{2,1,0:T(8,128)(2,1)S(1)} all-to-all(bf16[64,16,256]{2,1,0:T(8,128)(2,1)S(1)} %fusion.19), channel_id=1, replica_groups=mesh['ctx'=64,'ch'=4] {'ctx'}, dimensions={0} | all-to-all | bytes 1048576 | tf_op jit(solution)/shard_map/all_to_all | solution.py:145
  230.0 1.1 bitcast_convert_fusion
  231.1 2.6 %copy.25 = f32[1024,256]{0,1:T(8,128)} copy(f32[1024,256]{1,0:T(8,128)} %bitcast_convert_fusion) | data formatting | bytes 2097152 | tf_op jit(solution)/shard_map/convert_element_type | solution.py:147
  233.7 2.2 fusion.14
  235.9 2.0 copy.26
  (60 shorter events, 0.2 us)
Async XLA Ops:
  6.5 8.2 %copy-start = (f32[1,16,16384]{2,1,0:T(8,128)S(1)}, f32[1,16,16384]{2,1,0:T(8,128)}, u32[]{:S(2)}) copy-start(f32[1,16,16384]{2,1,0:T(8,128)} %param.8) | copy-start | bytes 3145732
  6.5 128.4 %all-gather.2.cloned.1.call-start = ((), (), s32[]{:S(2)}) async-start(), calls=%async_computation.3 | async-start | bytes 25559040 | tf_op jit(solution)/shard_map/all_gather | solution.py:128
  9.9 32.5 %all-to-all-start = ((bf16[4,256,1024]{2,1,0:T(8,128)(2,1)}), bf16[4,256,1024]{2,1,0:T(8,128)(2,1)S(1)}, u32[]{:S(2)}, u32[]{:S(2)}) async-start(bf16[4,256,1024]{2,1,0:T(8,128)(2,1)} %broadcast_in_dim.110), calls=%async_computation | async-start | bytes 4194304 | tf_op jit(solution)/shard_map/all_to_all | solution.py:126
  30.2 1.3 copy-start.27
  146.5 3.1 %collective-permute-start = (bf16[3,1024,2]{1,2,0:T(2,128)(2,1)S(1)}, bf16[3,1024,2]{1,2,0:T(2,128)(2,1)S(1)}, u32[]{:S(2)}, u32[]{:S(2)}) collective-permute-start(bf16[3,1024,2]{1,2,0:T(2,128)(2,1)S(1)} %slice.336), channel_id=1, source_target_pairs={{0,4},{4,8},{8,12},{12,16},{16,20},{20,24},{24,28},{28,32},{32,36}... | collective-permute-start | bytes 36872 | tf_op jit(solution)/shard_map/ppermute | solution.py:14
  153.5 26.5 %all-to-all-start.1 = ((bf16[64,16,256]{2,1,0:T(8,128)(2,1)}), bf16[64,16,256]{2,1,0:T(8,128)(2,1)}, u32[]{:S(2)}, u32[]{:S(2)}) async-start(bf16[64,16,256]{2,1,0:T(8,128)(2,1)} %bitcast.127), calls=%async_computation.1 | async-start | bytes 1048576 | tf_op jit(solution)/shard_map/all_to_all | solution.py:139
  184.2 4.3 %copy-start.1 = (f32[16,1024]{1,0:T(8,128)S(1)}, f32[16,1024]{1,0:T(8,128)}, u32[]{:S(2)}) copy-start(f32[16,1024]{1,0:T(8,128)} %get-tuple-element.19) | copy-start | bytes 196612
  184.2 4.3 %copy-start.2 = (f32[16,1024]{1,0:T(8,128)S(1)}, f32[16,1024]{1,0:T(8,128)}, u32[]{:S(2)}) copy-start(f32[16,1024]{1,0:T(8,128)} %get-tuple-element.20) | copy-start | bytes 196612
  184.2 4.3 %copy-start.3 = (f32[16,1024]{1,0:T(8,128)S(1)}, f32[16,1024]{1,0:T(8,128)}, u32[]{:S(2)}) copy-start(f32[16,1024]{1,0:T(8,128)} %get-tuple-element.21) | copy-start | bytes 196612
  184.2 4.3 %copy-start.4 = (f32[16,1024]{1,0:T(8,128)S(1)}, f32[16,1024]{1,0:T(8,128)}, u32[]{:S(2)}) copy-start(f32[16,1024]{1,0:T(8,128)} %get-tuple-element.22) | copy-start | bytes 196612
  184.2 4.3 %copy-start.5 = (f32[16,1024]{1,0:T(8,128)S(1)}, f32[16,1024]{1,0:T(8,128)}, u32[]{:S(2)}) copy-start(f32[16,1024]{1,0:T(8,128)} %get-tuple-element.23) | copy-start | bytes 196612
  184.2 4.3 %copy-start.6 = (f32[16,1024]{1,0:T(8,128)S(1)}, f32[16,1024]{1,0:T(8,128)}, u32[]{:S(2)}) copy-start(f32[16,1024]{1,0:T(8,128)} %get-tuple-element.24) | copy-start | bytes 196612
  184.2 4.3 %copy-start.7 = (f32[16,1024]{1,0:T(8,128)S(1)}, f32[16,1024]{1,0:T(8,128)}, u32[]{:S(2)}) copy-start(f32[16,1024]{1,0:T(8,128)} %get-tuple-element.25) | copy-start | bytes 196612
  184.2 4.3 %copy-start.8 = (f32[16,1024]{1,0:T(8,128)S(1)}, f32[16,1024]{1,0:T(8,128)}, u32[]{:S(2)}) copy-start(f32[16,1024]{1,0:T(8,128)} %get-tuple-element.26) | copy-start | bytes 196612
  184.2 4.3 %copy-start.9 = (f32[16,1024]{1,0:T(8,128)S(1)}, f32[16,1024]{1,0:T(8,128)}, u32[]{:S(2)}) copy-start(f32[16,1024]{1,0:T(8,128)} %get-tuple-element.27) | copy-start | bytes 196612
  184.2 4.3 %copy-start.10 = (f32[16,1024]{1,0:T(8,128)S(1)}, f32[16,1024]{1,0:T(8,128)}, u32[]{:S(2)}) copy-start(f32[16,1024]{1,0:T(8,128)} %get-tuple-element.28) | copy-start | bytes 196612
  184.2 4.3 %copy-start.11 = (f32[16,1024]{1,0:T(8,128)S(1)}, f32[16,1024]{1,0:T(8,128)}, u32[]{:S(2)}) copy-start(f32[16,1024]{1,0:T(8,128)} %get-tuple-element.29) | copy-start | bytes 196612
  184.2 4.3 %copy-start.12 = (f32[16,1024]{1,0:T(8,128)S(1)}, f32[16,1024]{1,0:T(8,128)}, u32[]{:S(2)}) copy-start(f32[16,1024]{1,0:T(8,128)} %get-tuple-element.30) | copy-start | bytes 196612
  184.2 4.3 %copy-start.13 = (f32[16,1024]{1,0:T(8,128)S(1)}, f32[16,1024]{1,0:T(8,128)}, u32[]{:S(2)}) copy-start(f32[16,1024]{1,0:T(8,128)} %get-tuple-element.31) | copy-start | bytes 196612
  184.3 4.3 %copy-start.14 = (f32[16,1024]{1,0:T(8,128)S(1)}, f32[16,1024]{1,0:T(8,128)}, u32[]{:S(2)}) copy-start(f32[16,1024]{1,0:T(8,128)} %get-tuple-element.32) | copy-start | bytes 196612
  184.3 4.3 %copy-start.15 = (f32[16,1024]{1,0:T(8,128)S(1)}, f32[16,1024]{1,0:T(8,128)}, u32[]{:S(2)}) copy-start(f32[16,1024]{1,0:T(8,128)} %get-tuple-element.33) | copy-start | bytes 196612
  184.3 4.3 %copy-start.16 = (f32[16,1024]{1,0:T(8,128)S(1)}, f32[16,1024]{1,0:T(8,128)}, u32[]{:S(2)}) copy-start(f32[16,1024]{1,0:T(8,128)} %get-tuple-element.34) | copy-start | bytes 196612
  184.3 4.3 %copy-start.17 = (f32[16,1024]{1,0:T(8,128)S(1)}, f32[16,1024]{1,0:T(8,128)}, u32[]{:S(2)}) copy-start(f32[16,1024]{1,0:T(8,128)} %get-tuple-element.35) | copy-start | bytes 196612
  184.3 4.3 %copy-start.18 = (f32[16,1024]{1,0:T(8,128)S(1)}, f32[16,1024]{1,0:T(8,128)}, u32[]{:S(2)}) copy-start(f32[16,1024]{1,0:T(8,128)} %get-tuple-element.36) | copy-start | bytes 196612
  184.3 4.3 %copy-start.19 = (f32[16,1024]{1,0:T(8,128)S(1)}, f32[16,1024]{1,0:T(8,128)}, u32[]{:S(2)}) copy-start(f32[16,1024]{1,0:T(8,128)} %get-tuple-element.37) | copy-start | bytes 196612
  184.3 4.3 %copy-start.20 = (f32[16,1024]{1,0:T(8,128)S(1)}, f32[16,1024]{1,0:T(8,128)}, u32[]{:S(2)}) copy-start(f32[16,1024]{1,0:T(8,128)} %get-tuple-element.38) | copy-start | bytes 196612
  184.3 4.3 %copy-start.21 = (f32[16,1024]{1,0:T(8,128)S(1)}, f32[16,1024]{1,0:T(8,128)}, u32[]{:S(2)}) copy-start(f32[16,1024]{1,0:T(8,128)} %get-tuple-element.39) | copy-start | bytes 196612
  184.3 4.3 %copy-start.22 = (f32[16,1024]{1,0:T(8,128)S(1)}, f32[16,1024]{1,0:T(8,128)}, u32[]{:S(2)}) copy-start(f32[16,1024]{1,0:T(8,128)} %get-tuple-element.40) | copy-start | bytes 196612
  184.3 4.3 %copy-start.23 = (f32[16,1024]{1,0:T(8,128)S(1)}, f32[16,1024]{1,0:T(8,128)}, u32[]{:S(2)}) copy-start(f32[16,1024]{1,0:T(8,128)} %get-tuple-element.41) | copy-start | bytes 196612
  184.4 4.3 %copy-start.24 = (f32[16,1024]{1,0:T(8,128)S(1)}, f32[16,1024]{1,0:T(8,128)}, u32[]{:S(2)}) copy-start(f32[16,1024]{1,0:T(8,128)} %get-tuple-element.42) | copy-start | bytes 196612
  184.4 4.3 %copy-start.25 = (f32[16,1024]{1,0:T(8,128)S(1)}, f32[16,1024]{1,0:T(8,128)}, u32[]{:S(2)}) copy-start(f32[16,1024]{1,0:T(8,128)} %get-tuple-element.43) | copy-start | bytes 196612
  184.4 4.3 %copy-start.26 = (f32[16,1024]{1,0:T(8,128)S(1)}, f32[16,1024]{1,0:T(8,128)}, u32[]{:S(2)}) copy-start(f32[16,1024]{1,0:T(8,128)} %get-tuple-element.44) | copy-start | bytes 196612
  184.4 14.1 %slice-start = ((s8[8388608]{0:T(1024)(128)(4,1)}), s8[4194304]{0:T(1024)(128)(4,1)S(1)}, s32[]{:S(2)}) async-start(s8[8388608]{0:T(1024)(128)(4,1)} %bitcast.119), calls=%async_computation.4 | async-start | bytes 8388608
  188.2 10.3 %slice-start.1 = ((s8[8388608]{0:T(1024)(128)(4,1)}), s8[4194304]{0:T(1024)(128)(4,1)S(1)}, s32[]{:S(2)}) async-start(s8[8388608]{0:T(1024)(128)(4,1)} %bitcast.119), calls=%async_computation.5 | async-start | bytes 8388608
  200.9 3.8 %copy-start.28 = (f32[1,16]{1,0:T(1,128)S(1)}, f32[1,16]{1,0:T(1,128)}, u32[]{:S(2)}) copy-start(f32[1,16]{1,0:T(1,128)} %param.9) | copy-start | bytes 196
Sparse Core Ops, SparseCore 0:
  10.1 124.7 all-gather.1

commit v2 on v1

--- a/solution.py
+++ b/solution.py
@@ -3,6 +3,8 @@
 import jax
 import jax.numpy as jnp
 from jax import lax
+import numpy as np
+from jax.sharding import Mesh, NamedSharding
 from jax.sharding import PartitionSpec as P
 
 BLOCK = 1024
@@ -115,17 +117,41 @@
 
 
 def make_shards(n_ctx, n_ch, tile_extent):
+    ctx = ("yh", "cq")
+    swap = [(0, 1), (1, 0)]
+
     def featured(projected, taps):
         local_tokens = projected.shape[2]
-        previous = shifted(projected[:, :, local_tokens - 2 :], "ctx", n_ctx, 1)
+        previous = shifted(projected[:, :, local_tokens - 2 :], ctx, n_ctx, 1)
         return short_conv(projected.astype(jnp.float32), taps, previous.astype(jnp.float32))
 
+    def by_half(half, own, other):
+        first = jnp.where(half == 0, own, other)
+        second = jnp.where(half == 0, other, own)
+        return jnp.stack([first, second])
+
     def shards(tokens, in_weight, short_taps, long_filter, skip_gain):
+        half = lax.axis_index("yh")
         local_tokens, local_features = tokens.shape
-        copies = jnp.broadcast_to(tokens[None], (n_ch, local_tokens, local_features))
+        branches, local_rows, lanes = in_weight.shape
+        width = lanes // 2
+        own_cols = lax.dynamic_slice_in_dim(in_weight, half * width, width, axis=2)
+        other_cols = lax.dynamic_slice_in_dim(in_weight, (1 - half) * width, width, axis=2)
+        partner_rows = lax.ppermute(other_cols, "yh", swap)
+        rows_pair = by_half(half, own_cols, partner_rows)
+        gathered = lax.all_gather(rows_pair, "cq", axis=0, tiled=False)
+        whole_weight = gathered.transpose(2, 0, 1, 3, 4).reshape(branches, -1, width)
+        partner_tokens = lax.ppermute(tokens, "yh", swap)
+        token_pair = by_half(half, tokens, partner_tokens)
+        copies = jnp.broadcast_to(token_pair[None], (n_ch,) + token_pair.shape)
         pieces = lax.all_to_all(copies, "ch", split_axis=0, concat_axis=0, tiled=True)
-        whole_tokens = pieces.transpose(1, 0, 2).reshape(local_tokens, n_ch * local_features)
-        whole_weight = lax.all_gather(in_weight, "ctx", axis=1, tiled=True)
+        n_q = n_ctx // 2
+        whole_tokens = (
+            pieces.transpose(1, 2, 0, 3)
+            .reshape(2 * local_tokens, 2, n_q, local_rows)
+            .transpose(0, 2, 1, 3)
+            .reshape(2 * local_tokens, -1)
+        )
         forward, inverse = spectral_tables(tile_extent)
         spec_k = filter_spectra(long_filter[0], forward, tile_extent)
         whole_weight, forward, inverse, spec_k = lax.optimization_barrier(
@@ -133,17 +159,21 @@
         )
         summed = jnp.einsum(
             "pdc,ld->pcl", whole_weight, whole_tokens, preferred_element_type=jnp.float32
-        )
-        embedding_result = featured(summed.astype(jnp.bfloat16), short_taps)
+        ).astype(jnp.bfloat16)
+        own_part = lax.dynamic_slice_in_dim(summed, half * local_tokens, local_tokens, axis=2)
+        other_part = lax.dynamic_slice_in_dim(summed, (1 - half) * local_tokens, local_tokens, axis=2)
+        received = lax.ppermute(other_part, "yh", swap)
+        projected = jnp.concatenate(list(by_half(half, own_part, received)), axis=1)
+        embedding_result = featured(projected, short_taps)
         gate_wave = (embedding_result[1] * embedding_result[2]).astype(jnp.bfloat16)
-        per_channel_view = lax.all_to_all(gate_wave, "ctx", split_axis=0, concat_axis=1, tiled=True)
+        per_channel_view = lax.all_to_all(gate_wave, ctx, split_axis=0, concat_axis=1, tiled=True)
         blended_lines = global_causal_smear(
             per_channel_view, spec_k, skip_gain[0], forward, inverse, tile_extent
         )
-        lanes, span = blended_lines.shape
-        outgoing = blended_lines.reshape(lanes, n_ctx, span // n_ctx).transpose(1, 0, 2)
-        returned = lax.all_to_all(outgoing, "ctx", split_axis=0, concat_axis=0, tiled=True)
-        by_token = returned.reshape(n_ctx * lanes, span // n_ctx)
+        lines, span = blended_lines.shape
+        outgoing = blended_lines.reshape(lines, n_ctx, span // n_ctx).transpose(1, 0, 2)
+        returned = lax.all_to_all(outgoing, ctx, split_axis=0, concat_axis=0, tiled=True)
+        by_token = returned.reshape(n_ctx * lines, span // n_ctx)
         gated_output = (embedding_result[0] * by_token.astype(jnp.float32)).astype(jnp.bfloat16)
         return gated_output
 
@@ -151,17 +181,27 @@
 
 
 def solution(mesh):
+    n_ctx = mesh.shape["ctx"]
+    grid = np.asarray(mesh.devices).reshape(2, n_ctx // 2, mesh.shape["ch"])
+    split_mesh = Mesh(grid, ("yh", "cq", "ch"))
+    ctx = ("yh", "cq")
     placed = (
-        P("ctx", "ch"),
-        P(None, "ctx", "ch"),
+        P(ctx, "ch"),
+        P(None, ctx, "ch"),
         P(None, None, "ch"),
-        P("ch", "ctx", None),
-        P("ch", "ctx"),
-    )
-    return jax.shard_map(
-        make_shards(mesh.shape["ctx"], mesh.shape["ch"], BLOCK),
-        mesh=mesh,
+        P("ch", ctx, None),
+        P("ch", ctx),
+    )
+    mapped = jax.shard_map(
+        make_shards(n_ctx, mesh.shape["ch"], BLOCK),
+        mesh=split_mesh,
         in_specs=placed,
-        out_specs=P("ch", "ctx"),
+        out_specs=P("ch", ctx),
         check_vma=False,
     )
+    out_sharding = NamedSharding(mesh, P("ch", "ctx"))
+
+    def run(*args):
+        return lax.with_sharding_constraint(mapped(*args), out_sharding)
+
+    return run

time: 246 us -> 248 us (level)
  waiting for transfers between devices: 101 us -> 61.9 us
  other arithmetic: 42.4 us -> 58.5 us
  starting transfers between devices: 16 us -> 30.5 us
  local copies, waits for them, and re-layouts: 27.8 us -> 41.5 us
  matrix products: 20.4 us -> 17.3 us
    all_gather x1, waiting for transfers between devices: 86 us -> 0.01 us  [shards(): gathered = lax.all_gather(rows_pair, 'cq', axis=0, tiled=False)]
    all_to_all x1, waiting for transfers between devices: 0.01 us -> 27.4 us  [shards(): lax.all_to_all(copies, 'ch', split_axis=0, concat_axis=0, tiled=True)]
    ppermute x0 -> x3, waiting for transfers between devices: none -> 21.5 us  [the longest x1 17.9 us: shards(): received = lax.ppermute(other_part, 'yh', swap)]
    ppermute x0 -> x3, starting transfers between devices: none -> 7.7 us  [the longest x1 3.82 us: shards(): partner_rows = lax.ppermute(other_cols, 'yh', swap)]
    add x1, other arithmetic: 0.94 us -> 8.41 us  [short_conv(): result + local_taps[:, offset, :][:, :, None] * extended[:, :, 2 - offset...]
    all_gather x0 -> x1, local copies, waits for them, and re-layouts: none -> 6.79 us  [shards(): gathered = lax.all_gather(rows_pair, 'cq', axis=0, tiled=False)]
    ppermute x1, starting transfers between devices: 1.92 us -> 7.28 us  [shifted(): return lax.ppermute(block, axis, route)]
    convert_element_type x3 -> x1, local copies, waits for them, and re-layouts: 6.63 us -> 1.52 us  [featured(): previous.astype(jnp.float32)]
  transfers between devices with their start and end apart: 4 -> 7, of which waited for: 3 -> 4; matrix products, arithmetic and copies ran while one was open for 17% -> 25% of each run, Pallas kernels for 0% -> 0%
where the time goes in v2:
time: 248 us; the launch traced here: 247 us
  waiting for transfers between devices  61.9 us (25%)
  other arithmetic  58.5 us (24%)
  local copies, waits for them, and re-layouts  41.5 us (17%)
  starting transfers between devices  30.5 us (12%)
  blocking collectives  23.4 us (9%)
  matrix products  17.3 us (7%)
  between operations  14.2 us (6%)
    all_to_all x1, waiting for transfers between devices, shards(): lax.all_to_all(copies, 'ch', split_axis=0, concat_axis=0, tiled=True)  27.4 us
    all_to_all x1, blocking collectives, shards(): lax.all_to_all(outgoing, ctx, split_axis=0, concat_axis=0, tiled=True)  23.4 us
    ppermute x1, waiting for transfers between devices, shards(): received = lax.ppermute(other_part, 'yh', swap)  17.9 us
    another operation x6, other arithmetic, run(): return lax.with_sharding_constraint(mapped(*args), out_sharding)  16.3 us
    all_to_all x1, waiting for transfers between devices, shards(): lax.all_to_all(gate_wave, ctx, split_axis=0, concat_axis=1, tiled=True)  12.9 us
    all_to_all x1, starting transfers between devices, shards(): lax.all_to_all(gate_wave, ctx, split_axis=0, concat_axis=1, tiled=True)  10.3 us
    concatenate x1, other arithmetic, spectral_tables(): jnp.concatenate([weights * cos_b, jnp.where(first_row, alt_t / period, -(...  8.51 us
    add x1, other arithmetic, short_conv(): result + local_taps[:, offset, :][:, :, None] * extended[:, :, 2 - offset...  8.41 us
  transfers between devices with their start and end apart: 7, of which 4 were waited for; matrix products, arithmetic and copies ran while one was open for 25% of the time, Pallas kernels for 0%

profile of v2, /device:TPU:1, one launch (start us, length us, event | category | flops | bytes accessed | tf_op | source)
XLA Modules:
  0.0 247.1 jit_solution(15955891847969928776)
XLA Ops:
  6.5 0.9 constant_dynamic-slice_fusion.1
  7.5 3.8 %collective-permute-start = (bf16[3,64,512]{2,1,0:T(8,128)(2,1)S(1)}, bf16[3,64,512]{2,1,0:T(8,128)(2,1)S(1)}, u32[]{:S(2)}, u32[]{:S(2)}) collective-permute-start(bf16[3,64,512]{2,1,0:T(8,128)(2,1)S(1)} %constant_dynamic-slice_fusion.1), channel_id=1, source_target_pairs={{0,128},{128,0},{1,129},{129,1},{2,130},{130,2},{3,131},{131,3},{4... | collective-permute-start | bytes 589832 | tf_op jit(solution)/shard_map/ppermute | solution.py:140
  11.3 3.6 %collective-permute-done = bf16[3,64,512]{2,1,0:T(8,128)(2,1)S(1)} collective-permute-done((bf16[3,64,512]{2,1,0:T(8,128)(2,1)S(1)}, bf16[3,64,512]{2,1,0:T(8,128)(2,1)S(1)}, u32[]{:S(2)}, u32[]{:S(2)}) %collective-permute-start) | collective-permute-done | bytes 196640 | tf_op jit(solution)/shard_map/ppermute | solution.py:140
  14.9 1.0 select_bitcast_fusion.3
  15.9 0.8 pad_maximum_fusion.5
  16.7 0.0 all-gather.3.cloned.1.call-update
  16.7 3.8 %collective-permute-start.1 = (bf16[256,1024]{1,0:T(8,128)(2,1)}, bf16[256,1024]{1,0:T(8,128)(2,1)}, u32[]{:S(2)}, u32[]{:S(2)}) collective-permute-start(bf16[256,1024]{1,0:T(8,128)(2,1)} %param.5), channel_id=1, source_target_pairs={{0,128},{128,0},{1,129},{129,1},{2,130},{130,2},{3,131},{131,3},{4... | collective-permute-start | bytes 1572872 | tf_op jit(solution)/shard_map/ppermute | solution.py:144
  20.5 1.3 convert_element_type.97
  21.8 0.3 copy.40
  22.1 1.1 copy.25
  23.2 0.5 fusion.50
  23.7 0.6 fusion.53
  24.3 1.0 fusion.40
  25.4 0.8 add_negate_fusion
  26.2 0.8 subtract_convert_fusion
  27.0 0.3 fusion.6
  27.4 2.6 %pad_maximum_fusion.1 = bf16[1024,2048]{1,0:T(8,128)(2,1)} fusion(bf16[1024,1024]{1,0:T(8,128)(2,1)S(1)} %fusion.6, bf16[1024,1024]{1,0:T(8,128)(2,1)S(1)} %bitcast.142), kind=kLoop, calls=%fused_computation.41 | loop fusion | flops 8388608 | bytes 8388608 | tf_op jit(solution)/shard_map/concatenate | solution.py:39
  30.0 1.1 fusion.43
  31.1 3.5 %add_multiply_fusion = bf16[32,32,2048]{2,1,0:T(8,128)(2,1)} fusion(f32[32,2048]{1,0:T(8,128)S(1)} %get-tuple-element.62, f32[32,2048]{1,0:T(8,128)S(1)} %get-tuple-element.57, f32[32,2048]{1,0:T(8,128)S(1)} %get-tuple-element.63, f32[32,2048]{1,0:T(8,128)S(1)} %get-tuple-element.56), kind=kLoop, calls=%fused_computation.7 | loop fusion | flops 10485760 | bytes 5242880 | tf_op jit(solution)/shard_map/mul | solution.py:47
  34.7 1.1 select_bitcast_fusion.1
  35.8 1.1 pad_maximum_fusion.4
  36.9 2.5 %copy.26 = bf16[2,256,1024]{1,0,2:T(2,128)(2,1)S(1)} copy(bf16[2,256,1024]{2,1,0:T(8,128)(2,1)} %pad_maximum_fusion.4) | data formatting | bytes 2097152 | tf_op jit(solution)/shard_map/stack | solution.py:131
  39.4 4.1 %broadcast_in_dim.110 = bf16[4,2,256,1024]{2,1,3,0:T(2,128)(2,1)} broadcast(bf16[2,256,1024]{1,0,2:T(2,128)(2,1)S(1)} %copy.26), dimensions={1,2,3} | broadcast | bytes 5242880 | tf_op jit(solution)/shard_map/broadcast_in_dim | solution.py:146
  43.5 5.2 %all-to-all-start = ((bf16[4,2,256,1024]{2,1,3,0:T(2,128)(2,1)}), bf16[4,2,256,1024]{2,1,3,0:T(2,128)(2,1)}, u32[]{:S(2)}, u32[]{:S(2)}) async-start(bf16[4,2,256,1024]{2,1,3,0:T(2,128)(2,1)} %broadcast_in_dim.110), calls=%async_computation | async-start | bytes 8388608 | tf_op jit(solution)/shard_map/all_to_all | solution.py:147
  48.7 4.4 %fusion.64 = f32[2048,256]{0,1:T(8,128)} fusion(bf16[256,1024]{1,0:T(8,128)(2,1)S(1)} %bitcast.150, bf16[1024,1024]{1,0:T(8,128)(2,1)} %copy-done.1, bf16[1024,1024]{1,0:T(8,128)(2,1)S(1)} %bitcast.143), kind=kOutput, calls=%fused_computation.182 | convolution fusion | flops 1082130432 | bytes 6815744 | tf_op jit(solution)/shard_map/dot_general | solution.py:61
  53.1 2.9 %fusion.2 = bf16[1024,2048]{1,0:T(8,128)(2,1)} fusion(bf16[32,32,2048]{2,1,0:T(8,128)(2,1)S(1)} %copy-done, bf16[2048]{0:T(1024)(128)(2,1)S(1)} %select_multiply_fusion, pred[1024]{0:T(1024)(128)(4,1)S(1)} %iota_compare_fusion), kind=kLoop, calls=%fused_computation.4 | loop fusion | flops 2097152 | bytes 8393728 | tf_op jit(solution)/shard_map/convert.4 | solution.py:205
  56.0 1.2 multiply_subtract_fusion
  57.2 2.5 %fusion.3 = bf16[1024,2048]{1,0:T(8,128)(2,1)} fusion(f32[32,32,2048]{2,1,0:T(8,128)S(1)} %multiply_subtract_fusion, f32[1024]{0:T(1024)S(1)} %select_multiply_fusion.1), kind=kLoop, calls=%fused_computation.6 | loop fusion | flops 4194304 | bytes 12587008 | tf_op jit(solution)/shard_map/convert.3 | solution.py:205
  59.7 8.5 %pad_maximum_fusion = bf16[2048,2048]{1,0:T(8,128)(2,1)} fusion(bf16[1024,2048]{1,0:T(8,128)(2,1)} %fusion.2, bf16[1024,2048]{1,0:T(8,128)(2,1)} %fusion.3), kind=kLoop, calls=%fused_computation | loop fusion | flops 16777216 | bytes 16777216 | tf_op jit(solution)/shard_map/concatenate | solution.py:46
  68.2 27.4 %all-to-all-done = bf16[4,2,256,1024]{2,1,3,0:T(2,128)(2,1)} async-done(((bf16[4,2,256,1024]{2,1,3,0:T(2,128)(2,1)}), bf16[4,2,256,1024]{2,1,3,0:T(2,128)(2,1)}, u32[]{:S(2)}, u32[]{:S(2)}) %all-to-all-start) | async-done | bytes 4194336 | tf_op jit(solution)/shard_map/all_to_all | solution.py:147
  95.6 7.6 %reshape.341 = bf16[512,2,32,64]{0,3,2,1:T(8,128)(2,1)} reshape(bf16[2,256,4,1024]{1,0,3,2:T(2,128)(2,1)} %bitcast.15) | data formatting | bytes 8388608 | tf_op jit(solution)/shard_map/reshape | solution.py:151
  103.2 4.7 %copy.27 = bf16[512,32,2,64]{0,3,2,1:T(8,128)(2,1)} copy(bf16[512,32,2,64]{0,3,1,2:T(8,128)(2,1)} %bitcast.138) | data formatting | bytes 8388608 | tf_op jit(solution)/shard_map/transpose | solution.py:152
  108.0 6.8 %copy.24 = bf16[64,3,64,512]{3,2,0,1:T(8,128)(2,1)S(1)} copy(bf16[64,3,64,512]{3,2,1,0:T(8,128)(2,1)} %all-gather.3.cloned.1.call-done) | data formatting | bytes 25165824 | tf_op jit(solution)/shard_map/all_gather | solution.py:142
  114.8 0.0 copy-start.37
  114.8 6.7 %convolution_convert_fusion = bf16[3,512,512]{2,1,0:T(8,128)(2,1)S(1)} fusion(bf16[3,4096,512]{2,1,0:T(8,128)(2,1)S(1)} %bitcast.139, bf16[512,4096,1]{0,1,2:T(8,128)(2,1)S(1)} %bitcast.144), kind=kOutput, calls=%fused_computation.57 | convolution fusion | flops 6443237376 | bytes 18350080 | tf_op jit(solution)/shard_map/pdc,ld->pcl/dot_general | solution.py:160
  121.5 0.1 constant_dynamic-slice_fusion
  121.6 0.1 collective-permute-start.2
  121.8 17.9 %collective-permute-done.2 = bf16[3,512,256]{2,1,0:T(8,128)(2,1)} collective-permute-done((bf16[3,512,256]{2,1,0:T(8,128)(2,1)S(1)}, bf16[3,512,256]{2,1,0:T(8,128)(2,1)}, u32[]{:S(2)}, u32[]{:S(2)}) %collective-permute-start.2) | collective-permute-done | bytes 786464 | tf_op jit(solution)/shard_map/ppermute | solution.py:165
  139.7 1.4 broadcast_select_fusion
  141.1 0.3 fusion.20
  141.4 0.3 copy.30
  141.7 7.3 %collective-permute-start.3 = (bf16[3,1024,2]{1,2,0:T(2,128)(2,1)S(1)}, bf16[3,1024,2]{1,2,0:T(2,128)(2,1)S(1)}, u32[]{:S(2)}, u32[]{:S(2)}) collective-permute-start(bf16[3,1024,2]{1,2,0:T(2,128)(2,1)S(1)} %copy.30), channel_id=1, source_target_pairs={{0,4},{4,8},{8,12},{12,16},{16,20},{20,24},{24,28},{28,32},{32,36}... | collective-permute-start | bytes 36872 | tf_op jit(solution)/shard_map/ppermute | solution.py:16
  149.0 1.9 fusion.12
  150.9 1.5 copy.31
  152.4 8.4 %fusion.10 = f32[3,1024,256]{2,1,0:T(8,128)S(1)} fusion(f32[3,1024,2]{2,1,0:T(8,128)} %copy.31, f32[3,1024,256]{2,1,0:T(8,128)} %fusion.12, f32[3,1024]{1,0:T(4,128)S(1)} %get-tuple-element.64, f32[3,1024]{1,0:T(4,128)S(1)} %get-tuple-element.65, f32[3,1024]{1,0:T(4,128)S(1)} %bitcast.151), kind=kLoop, calls=%fused_computation.51 | loop fusion | flops 5505024 | bytes 6352896 | tf_op jit(solution)/shard_map/add | solution.py:112
  160.8 0.9 fusion.13
  161.7 10.3 %all-to-all-start.1 = ((bf16[64,16,256]{2,1,0:T(8,128)(2,1)}), bf16[64,16,256]{2,1,0:T(8,128)(2,1)}, u32[]{:S(2)}, u32[]{:S(2)}) async-start(bf16[64,16,256]{2,1,0:T(8,128)(2,1)} %bitcast.145), calls=%async_computation.1 | async-start | bytes 1048576 | tf_op jit(solution)/shard_map/all_to_all | solution.py:169
  172.1 2.1 slice_bitcast_fusion.31
  174.2 2.2 slice_bitcast_fusion.32
  176.4 12.9 %all-to-all-done.1 = bf16[64,16,256]{2,1,0:T(8,128)(2,1)} async-done(((bf16[64,16,256]{2,1,0:T(8,128)(2,1)}), bf16[64,16,256]{2,1,0:T(8,128)(2,1)}, u32[]{:S(2)}, u32[]{:S(2)}) %all-to-all-start.1) | async-done | bytes 524320 | tf_op jit(solution)/shard_map/all_to_all | solution.py:169
  189.3 2.0 copy.32
  191.3 2.2 dot_general.19
  193.7 3.8 %fusion.4 = f32[16,16,2048]{2,1,0:T(8,128)S(1)} fusion(bf16[16,16,1024]{2,1,0:T(8,128)(2,1)} %dot_general.19, bf16[1024,2048]{1,0:T(8,128)(2,1)} %pad_maximum_fusion.1), kind=kOutput, calls=%fused_computation.42 | convolution fusion | flops 1073741824 | bytes 6815744 | tf_op jit(solution)/shard_map/dot_general | solution.py:70
  197.5 0.2 fusion.65
  198.0 4.5 %subtract_convert_fusion.1 = bf16[16,16,1024]{2,1,0:T(8,128)(2,1)S(1)} fusion(f32[16,16,1024]{2,1,0:T(8,128)S(1)} %get-tuple-element.48, f32[16,1024]{1,0:T(8,128)S(1)} %copy-done.20, f32[16,1024]{1,0:T(8,128)S(1)} %copy-done.21, f32[16,1024]{1,0:T(8,128)S(1)} %copy-done.23, f32[16,1024]{1,0:T(8,128)S(1)} %copy-done.24, f32[16,1024]{1,0:T(8,128)S(1)} %copy-done.25, ...), kind=kLoop, calls=%fused_computation.72 | loop fusion | flops 17039360 | bytes 4719616 | tf_op jit(solution)/shard_map/convert.1 | solution.py:205
  202.5 5.2 %select_convert_fusion = bf16[16,16,1024]{2,1,0:T(8,128)(2,1)S(1)} fusion(f32[16,16,1024]{2,1,0:T(8,128)S(1)} %get-tuple-element.48, f32[16,16,1024]{2,1,0:T(8,128)S(1)} %get-tuple-element.47, f32[16,1024]{1,0:T(8,128)S(1)} %get-tuple-element.16, f32[16,1024]{1,0:T(8,128)S(1)} %get-tuple-element.17, f32[16,1024]{1,0:T(8,128)S(1)} %get-tuple-element.18, ...), kind=kLoop, calls=%fused_computation.71 | loop fusion | flops 25165824 | bytes 4719616 | tf_op jit(solution)/shard_map/convert.2 | solution.py:205
  207.8 2.4 fusion
  210.2 0.0 copy-start.38
  210.2 0.1 slice.346
  210.3 1.2 slice_add_fusion
  211.5 2.5 %reshape.343 = f32[16,64,256]{2,1,0:T(8,128)} reshape(f32[16,16,1024]{2,1,0:T(8,128)} %slice_add_fusion) | data formatting | bytes 2097152 | tf_op jit(solution)/shard_map/reshape | solution.py:101
  214.0 2.0 fusion.21
  216.0 23.4 %all_to_all.23 = bf16[64,16,256]{2,1,0:T(8,128)(2,1)S(1)} all-to-all(bf16[64,16,256]{2,1,0:T(8,128)(2,1)S(1)} %fusion.21), channel_id=1, replica_groups=mesh['yh'=2,'cq'=32,'ch'=4] {'yh','cq'}, dimensions={0} | all-to-all | bytes 1048576 | tf_op jit(solution)/shard_map/all_to_all | solution.py:175
  239.3 0.9 fusion.15
  (93 shorter events, 0.2 us)
Async XLA Ops:
  6.5 101.4 %all-gather.3.cloned.1.call-start = ((), (), s32[]{:S(2)}) async-start(), calls=%async_computation.3 | async-start | bytes 12976128 | tf_op jit(solution)/shard_map/all_gather | solution.py:142
  7.5 7.4 %collective-permute-start = (bf16[3,64,512]{2,1,0:T(8,128)(2,1)S(1)}, bf16[3,64,512]{2,1,0:T(8,128)(2,1)S(1)}, u32[]{:S(2)}, u32[]{:S(2)}) collective-permute-start(bf16[3,64,512]{2,1,0:T(8,128)(2,1)S(1)} %constant_dynamic-slice_fusion.1), channel_id=1, source_target_pairs={{0,128},{128,0},{1,129},{129,1},{2,130},{130,2},{3,131},{131,3},{4... | collective-permute-start | bytes 589832 | tf_op jit(solution)/shard_map/ppermute | solution.py:140
  16.7 18.0 %collective-permute-start.1 = (bf16[256,1024]{1,0:T(8,128)(2,1)}, bf16[256,1024]{1,0:T(8,128)(2,1)}, u32[]{:S(2)}, u32[]{:S(2)}) collective-permute-start(bf16[256,1024]{1,0:T(8,128)(2,1)} %param.5), channel_id=1, source_target_pairs={{0,128},{128,0},{1,129},{129,1},{2,130},{130,2},{3,131},{131,3},{4... | collective-permute-start | bytes 1572872 | tf_op jit(solution)/shard_map/ppermute | solution.py:144
  25.4 5.7 %copy-start.5 = (f32[32,2048]{1,0:T(8,128)}, f32[32,2048]{1,0:T(8,128)S(1)}, u32[]{:S(2)}) copy-start(f32[32,2048]{1,0:T(8,128)S(1)} %get-tuple-element.62) | copy-start | bytes 786436
  25.4 5.7 %copy-start.7 = (f32[32,2048]{1,0:T(8,128)}, f32[32,2048]{1,0:T(8,128)S(1)}, u32[]{:S(2)}) copy-start(f32[32,2048]{1,0:T(8,128)S(1)} %get-tuple-element.63) | copy-start | bytes 786436
  27.4 2.6 %copy-start.1 = (bf16[1024,1024]{1,0:T(8,128)(2,1)}, bf16[1024,1024]{1,0:T(8,128)(2,1)S(1)}, u32[]{:S(2)}) copy-start(bf16[1024,1024]{1,0:T(8,128)(2,1)S(1)} %fusion.6) | copy-start | bytes 6291460
  30.0 4.7 %copy-start.35 = (bf16[256,1024]{1,0:T(8,128)(2,1)S(1)}, bf16[256,1024]{1,0:T(8,128)(2,1)}, u32[]{:S(2)}) copy-start(bf16[256,1024]{1,0:T(8,128)(2,1)} %param.5) | copy-start | bytes 1572868
  31.1 4.7 %copy-start.3 = (f32[32,2048]{1,0:T(8,128)}, f32[32,2048]{1,0:T(8,128)S(1)}, u32[]{:S(2)}) copy-start(f32[32,2048]{1,0:T(8,128)S(1)} %get-tuple-element.57) | copy-start | bytes 786436
  43.5 5.2 %copy-start.36 = (bf16[16,16,1024]{2,1,0:T(8,128)(2,1)S(1)}, bf16[16,16,1024]{2,1,0:T(8,128)(2,1)}, u32[]{:S(2)}) copy-start(bf16[16,16,1024]{2,1,0:T(8,128)(2,1)} %copy.25) | copy-start | bytes 1572868
  43.5 52.1 %all-to-all-start = ((bf16[4,2,256,1024]{2,1,3,0:T(2,128)(2,1)}), bf16[4,2,256,1024]{2,1,3,0:T(2,128)(2,1)}, u32[]{:S(2)}, u32[]{:S(2)}) async-start(bf16[4,2,256,1024]{2,1,3,0:T(2,128)(2,1)} %broadcast_in_dim.110), calls=%async_computation | async-start | bytes 8388608 | tf_op jit(solution)/shard_map/all_to_all | solution.py:147
  48.7 4.4 %copy-start = (bf16[32,32,2048]{2,1,0:T(8,128)(2,1)S(1)}, bf16[32,32,2048]{2,1,0:T(8,128)(2,1)}, u32[]{:S(2)}) copy-start(bf16[32,32,2048]{2,1,0:T(8,128)(2,1)} %add_multiply_fusion) | copy-start | bytes 12582916
  53.1 2.9 %copy-start.4 = (f32[32,2048]{1,0:T(8,128)S(1)}, f32[32,2048]{1,0:T(8,128)}, u32[]{:S(2)}) copy-start(f32[32,2048]{1,0:T(8,128)} %copy-done.3) | copy-start | bytes 786436
  53.1 2.9 %copy-start.6 = (f32[32,2048]{1,0:T(8,128)S(1)}, f32[32,2048]{1,0:T(8,128)}, u32[]{:S(2)}) copy-start(f32[32,2048]{1,0:T(8,128)} %copy-done.5) | copy-start | bytes 786436
  53.1 2.9 %copy-start.8 = (f32[32,2048]{1,0:T(8,128)S(1)}, f32[32,2048]{1,0:T(8,128)}, u32[]{:S(2)}) copy-start(f32[32,2048]{1,0:T(8,128)} %copy-done.7) | copy-start | bytes 786436
  108.0 6.8 %copy-start.2 = (bf16[512,32,2,64]{0,3,2,1:T(8,128)(2,1)S(1)}, bf16[512,32,2,64]{0,3,2,1:T(8,128)(2,1)}, u32[]{:S(2)}) copy-start(bf16[512,32,2,64]{0,3,2,1:T(8,128)(2,1)} %copy.27) | copy-start | bytes 12582916
  114.8 6.9 %copy-start.37 = (f32[3,3,1024]{2,1,0:T(4,128)S(1)}, f32[3,3,1024]{2,1,0:T(4,128)}, u32[]{:S(2)}) copy-start(f32[3,3,1024]{2,1,0:T(4,128)} %param.7) | copy-start | bytes 110596
  121.6 18.1 %collective-permute-start.2 = (bf16[3,512,256]{2,1,0:T(8,128)(2,1)S(1)}, bf16[3,512,256]{2,1,0:T(8,128)(2,1)}, u32[]{:S(2)}, u32[]{:S(2)}) collective-permute-start(bf16[3,512,256]{2,1,0:T(8,128)(2,1)S(1)} %constant_dynamic-slice_fusion), channel_id=1, source_target_pairs={{0,128},{128,0},{1,129},{129,1},{2,130},{130,2},{3,131},{131,3},{4... | collective-permute-start | bytes 2359304 | tf_op jit(solution)/shard_map/ppermute | solution.py:165
  141.7 9.2 %collective-permute-start.3 = (bf16[3,1024,2]{1,2,0:T(2,128)(2,1)S(1)}, bf16[3,1024,2]{1,2,0:T(2,128)(2,1)S(1)}, u32[]{:S(2)}, u32[]{:S(2)}) collective-permute-start(bf16[3,1024,2]{1,2,0:T(2,128)(2,1)S(1)} %copy.30), channel_id=1, source_target_pairs={{0,4},{4,8},{8,12},{12,16},{16,20},{20,24},{24,28},{28,32},{32,36}... | collective-permute-start | bytes 36872 | tf_op jit(solution)/shard_map/ppermute | solution.py:16
  161.7 27.5 %all-to-all-start.1 = ((bf16[64,16,256]{2,1,0:T(8,128)(2,1)}), bf16[64,16,256]{2,1,0:T(8,128)(2,1)}, u32[]{:S(2)}, u32[]{:S(2)}) async-start(bf16[64,16,256]{2,1,0:T(8,128)(2,1)} %bitcast.145), calls=%async_computation.1 | async-start | bytes 1048576 | tf_op jit(solution)/shard_map/all_to_all | solution.py:169
  193.4 4.3 %copy-start.9 = (f32[16,1024]{1,0:T(8,128)S(1)}, f32[16,1024]{1,0:T(8,128)}, u32[]{:S(2)}) copy-start(f32[16,1024]{1,0:T(8,128)} %get-tuple-element.21) | copy-start | bytes 196612
  193.4 4.3 %copy-start.10 = (f32[16,1024]{1,0:T(8,128)S(1)}, f32[16,1024]{1,0:T(8,128)}, u32[]{:S(2)}) copy-start(f32[16,1024]{1,0:T(8,128)} %get-tuple-element.22) | copy-start | bytes 196612
  193.4 4.3 %copy-start.11 = (f32[16,1024]{1,0:T(8,128)S(1)}, f32[16,1024]{1,0:T(8,128)}, u32[]{:S(2)}) copy-start(f32[16,1024]{1,0:T(8,128)} %get-tuple-element.23) | copy-start | bytes 196612
  193.4 4.3 %copy-start.12 = (f32[16,1024]{1,0:T(8,128)S(1)}, f32[16,1024]{1,0:T(8,128)}, u32[]{:S(2)}) copy-start(f32[16,1024]{1,0:T(8,128)} %get-tuple-element.24) | copy-start | bytes 196612
  193.4 4.3 %copy-start.13 = (f32[16,1024]{1,0:T(8,128)S(1)}, f32[16,1024]{1,0:T(8,128)}, u32[]{:S(2)}) copy-start(f32[16,1024]{1,0:T(8,128)} %get-tuple-element.25) | copy-start | bytes 196612
  193.5 4.3 %copy-start.14 = (f32[16,1024]{1,0:T(8,128)S(1)}, f32[16,1024]{1,0:T(8,128)}, u32[]{:S(2)}) copy-start(f32[16,1024]{1,0:T(8,128)} %get-tuple-element.26) | copy-start | bytes 196612
  193.5 4.3 %copy-start.15 = (f32[16,1024]{1,0:T(8,128)S(1)}, f32[16,1024]{1,0:T(8,128)}, u32[]{:S(2)}) copy-start(f32[16,1024]{1,0:T(8,128)} %get-tuple-element.27) | copy-start | bytes 196612
  193.5 4.3 %copy-start.16 = (f32[16,1024]{1,0:T(8,128)S(1)}, f32[16,1024]{1,0:T(8,128)}, u32[]{:S(2)}) copy-start(f32[16,1024]{1,0:T(8,128)} %get-tuple-element.28) | copy-start | bytes 196612
  193.5 4.3 %copy-start.17 = (f32[16,1024]{1,0:T(8,128)S(1)}, f32[16,1024]{1,0:T(8,128)}, u32[]{:S(2)}) copy-start(f32[16,1024]{1,0:T(8,128)} %get-tuple-element.29) | copy-start | bytes 196612
  193.5 4.3 %copy-start.18 = (f32[16,1024]{1,0:T(8,128)S(1)}, f32[16,1024]{1,0:T(8,128)}, u32[]{:S(2)}) copy-start(f32[16,1024]{1,0:T(8,128)} %get-tuple-element.30) | copy-start | bytes 196612
  193.5 4.3 %copy-start.19 = (f32[16,1024]{1,0:T(8,128)S(1)}, f32[16,1024]{1,0:T(8,128)}, u32[]{:S(2)}) copy-start(f32[16,1024]{1,0:T(8,128)} %get-tuple-element.31) | copy-start | bytes 196612
  193.5 4.3 %copy-start.20 = (f32[16,1024]{1,0:T(8,128)S(1)}, f32[16,1024]{1,0:T(8,128)}, u32[]{:S(2)}) copy-start(f32[16,1024]{1,0:T(8,128)} %get-tuple-element.32) | copy-start | bytes 196612
  193.5 4.3 %copy-start.21 = (f32[16,1024]{1,0:T(8,128)S(1)}, f32[16,1024]{1,0:T(8,128)}, u32[]{:S(2)}) copy-start(f32[16,1024]{1,0:T(8,128)} %get-tuple-element.33) | copy-start | bytes 196612
  193.5 4.3 %copy-start.22 = (f32[16,1024]{1,0:T(8,128)S(1)}, f32[16,1024]{1,0:T(8,128)}, u32[]{:S(2)}) copy-start(f32[16,1024]{1,0:T(8,128)} %get-tuple-element.34) | copy-start | bytes 196612
  193.5 4.3 %copy-start.23 = (f32[16,1024]{1,0:T(8,128)S(1)}, f32[16,1024]{1,0:T(8,128)}, u32[]{:S(2)}) copy-start(f32[16,1024]{1,0:T(8,128)} %get-tuple-element.35) | copy-start | bytes 196612
  193.6 4.3 %copy-start.24 = (f32[16,1024]{1,0:T(8,128)S(1)}, f32[16,1024]{1,0:T(8,128)}, u32[]{:S(2)}) copy-start(f32[16,1024]{1,0:T(8,128)} %get-tuple-element.36) | copy-start | bytes 196612
  193.6 4.3 %copy-start.25 = (f32[16,1024]{1,0:T(8,128)S(1)}, f32[16,1024]{1,0:T(8,128)}, u32[]{:S(2)}) copy-start(f32[16,1024]{1,0:T(8,128)} %get-tuple-element.37) | copy-start | bytes 196612
  193.6 4.3 %copy-start.26 = (f32[16,1024]{1,0:T(8,128)S(1)}, f32[16,1024]{1,0:T(8,128)}, u32[]{:S(2)}) copy-start(f32[16,1024]{1,0:T(8,128)} %get-tuple-element.38) | copy-start | bytes 196612
  193.6 4.3 %copy-start.27 = (f32[16,1024]{1,0:T(8,128)S(1)}, f32[16,1024]{1,0:T(8,128)}, u32[]{:S(2)}) copy-start(f32[16,1024]{1,0:T(8,128)} %get-tuple-element.39) | copy-start | bytes 196612
  193.6 4.3 %copy-start.28 = (f32[16,1024]{1,0:T(8,128)S(1)}, f32[16,1024]{1,0:T(8,128)}, u32[]{:S(2)}) copy-start(f32[16,1024]{1,0:T(8,128)} %get-tuple-element.40) | copy-start | bytes 196612
  193.6 4.3 %copy-start.29 = (f32[16,1024]{1,0:T(8,128)S(1)}, f32[16,1024]{1,0:T(8,128)}, u32[]{:S(2)}) copy-start(f32[16,1024]{1,0:T(8,128)} %get-tuple-element.41) | copy-start | bytes 196612
  193.6 4.3 %copy-start.30 = (f32[16,1024]{1,0:T(8,128)S(1)}, f32[16,1024]{1,0:T(8,128)}, u32[]{:S(2)}) copy-start(f32[16,1024]{1,0:T(8,128)} %get-tuple-element.42) | copy-start | bytes 196612
  193.6 4.3 %copy-start.31 = (f32[16,1024]{1,0:T(8,128)S(1)}, f32[16,1024]{1,0:T(8,128)}, u32[]{:S(2)}) copy-start(f32[16,1024]{1,0:T(8,128)} %get-tuple-element.43) | copy-start | bytes 196612
  193.6 4.3 %copy-start.32 = (f32[16,1024]{1,0:T(8,128)S(1)}, f32[16,1024]{1,0:T(8,128)}, u32[]{:S(2)}) copy-start(f32[16,1024]{1,0:T(8,128)} %get-tuple-element.44) | copy-start | bytes 196612
  193.6 4.3 %copy-start.33 = (f32[16,1024]{1,0:T(8,128)S(1)}, f32[16,1024]{1,0:T(8,128)}, u32[]{:S(2)}) copy-start(f32[16,1024]{1,0:T(8,128)} %get-tuple-element.45) | copy-start | bytes 196612
  193.7 4.3 %copy-start.34 = (f32[16,1024]{1,0:T(8,128)S(1)}, f32[16,1024]{1,0:T(8,128)}, u32[]{:S(2)}) copy-start(f32[16,1024]{1,0:T(8,128)} %get-tuple-element.46) | copy-start | bytes 196612
  193.7 14.1 %slice-start = ((s8[8388608]{0:T(1024)(128)(4,1)}), s8[4194304]{0:T(1024)(128)(4,1)S(1)}, s32[]{:S(2)}) async-start(s8[8388608]{0:T(1024)(128)(4,1)} %bitcast.140), calls=%async_computation.4 | async-start | bytes 8388608
  197.5 10.3 %slice-start.1 = ((s8[8388608]{0:T(1024)(128)(4,1)}), s8[4194304]{0:T(1024)(128)(4,1)S(1)}, s32[]{:S(2)}) async-start(s8[8388608]{0:T(1024)(128)(4,1)} %bitcast.140), calls=%async_computation.5 | async-start | bytes 8388608
  210.2 3.8 %copy-start.38 = (f32[1,16]{1,0:T(1,128)S(1)}, f32[1,16]{1,0:T(1,128)}, u32[]{:S(2)}) copy-start(f32[1,16]{1,0:T(1,128)} %param.9) | copy-start | bytes 196
Sparse Core Ops, SparseCore 0:
  16.8 84.7 all-gather.2

commit v3 on v2

--- a/solution.py
+++ b/solution.py
@@ -138,20 +138,14 @@
         own_cols = lax.dynamic_slice_in_dim(in_weight, half * width, width, axis=2)
         other_cols = lax.dynamic_slice_in_dim(in_weight, (1 - half) * width, width, axis=2)
         partner_rows = lax.ppermute(other_cols, "yh", swap)
-        rows_pair = by_half(half, own_cols, partner_rows)
-        gathered = lax.all_gather(rows_pair, "cq", axis=0, tiled=False)
-        whole_weight = gathered.transpose(2, 0, 1, 3, 4).reshape(branches, -1, width)
+        rows_pair = jnp.stack(list(by_half(half, own_cols, partner_rows)), axis=1)
+        gathered = lax.all_gather(rows_pair, "cq", axis=2, tiled=False)
+        whole_weight = gathered.reshape(branches, -1, width)
         partner_tokens = lax.ppermute(tokens, "yh", swap)
         token_pair = by_half(half, tokens, partner_tokens)
         copies = jnp.broadcast_to(token_pair[None], (n_ch,) + token_pair.shape)
-        pieces = lax.all_to_all(copies, "ch", split_axis=0, concat_axis=0, tiled=True)
-        n_q = n_ctx // 2
-        whole_tokens = (
-            pieces.transpose(1, 2, 0, 3)
-            .reshape(2 * local_tokens, 2, n_q, local_rows)
-            .transpose(0, 2, 1, 3)
-            .reshape(2 * local_tokens, -1)
-        )
+        pieces = lax.all_to_all(copies, "ch", split_axis=0, concat_axis=3, tiled=True)
+        whole_tokens = pieces.reshape(2 * local_tokens, n_ch * local_features)
         forward, inverse = spectral_tables(tile_extent)
         spec_k = filter_spectra(long_filter[0], forward, tile_extent)
         whole_weight, forward, inverse, spec_k = lax.optimization_barrier(

time: 248 us -> 243 us (0.980)
  local copies, waits for them, and re-layouts: 41.5 us -> 33.4 us
  matrix products: 17.3 us -> 21.7 us
    all_to_all x0 -> x1, local copies, waits for them, and re-layouts: none -> 7.44 us  [shards(): lax.all_to_all(copies, 'ch', split_axis=0, concat_axis=3, tiled=True)]
    all_gather x1 -> x0, local copies, waits for them, and re-layouts: 6.79 us -> none  [shards(): gathered = lax.all_gather(rows_pair, 'cq', axis=0, tiled=False)]
    transpose x1 -> x0, local copies, waits for them, and re-layouts: 4.75 us -> none  [shards(): whole_tokens = pieces.transpose(1, 2, 0, 3).reshape(2 * local_tokens, 2,...]
    dot_general x1, matrix products: 6.74 us -> 11 us  [shards(): jnp.einsum('pdc,ld->pcl', whole_weight, whole_tokens, preferred_element_t...]
    another operation x4 -> x2, other arithmetic: 3.99 us -> 1.22 us  [by_half(): return jnp.stack([first, second])]
    another operation x1 -> x0, local copies, waits for them, and re-layouts: 2.51 us -> none  [by_half(): return jnp.stack([first, second])]
  transfers between devices with their start and end apart: 7 -> 7, of which waited for: 4 -> 4; matrix products, arithmetic and copies ran while one was open for 25% -> 24% of each run, Pallas kernels for 0% -> 0%
where the time goes in v3:
time: 243 us; the launch traced here: 242 us
  waiting for transfers between devices  61.7 us (25%)
  other arithmetic  57.3 us (24%)
  local copies, waits for them, and re-layouts  33.4 us (14%)
  starting transfers between devices  30.6 us (13%)
  blocking collectives  23.4 us (10%)
  matrix products  21.7 us (9%)
  between operations  14.1 us (6%)
    all_to_all x1, waiting for transfers between devices, shards(): lax.all_to_all(copies, 'ch', split_axis=0, concat_axis=3, tiled=True)  27.2 us
    all_to_all x1, blocking collectives, shards(): lax.all_to_all(outgoing, ctx, split_axis=0, concat_axis=0, tiled=True)  23.4 us
    ppermute x1, waiting for transfers between devices, shards(): received = lax.ppermute(other_part, 'yh', swap)  17.9 us
    another operation x6, other arithmetic, run(): return lax.with_sharding_constraint(mapped(*args), out_sharding)  16.3 us
    all_to_all x1, waiting for transfers between devices, shards(): lax.all_to_all(gate_wave, ctx, split_axis=0, concat_axis=1, tiled=True)  12.9 us
    dot_general x1, matrix products, shards(): jnp.einsum('pdc,ld->pcl', whole_weight, whole_tokens, preferred_element_t...  11 us
    all_to_all x1, starting transfers between devices, shards(): lax.all_to_all(gate_wave, ctx, split_axis=0, concat_axis=1, tiled=True)  10.7 us
    concatenate x1, other arithmetic, spectral_tables(): jnp.concatenate([weights * cos_b, jnp.where(first_row, alt_t / period, -(...  8.51 us
  transfers between devices with their start and end apart: 7, of which 4 were waited for; matrix products, arithmetic and copies ran while one was open for 24% of the time, Pallas kernels for 0%

profile of v3, /device:TPU:1, one launch (start us, length us, event | category | flops | bytes accessed | tf_op | source)
XLA Modules:
  0.0 242.2 jit_solution(16253634610348974272)
XLA Ops:
  6.5 0.9 constant_dynamic-slice_fusion.1
  7.5 3.8 %collective-permute-start = (bf16[3,64,512]{2,1,0:T(8,128)(2,1)S(1)}, bf16[3,64,512]{2,1,0:T(8,128)(2,1)S(1)}, u32[]{:S(2)}, u32[]{:S(2)}) collective-permute-start(bf16[3,64,512]{2,1,0:T(8,128)(2,1)S(1)} %constant_dynamic-slice_fusion.1), channel_id=1, source_target_pairs={{0,128},{128,0},{1,129},{129,1},{2,130},{130,2},{3,131},{131,3},{4... | collective-permute-start | bytes 589832 | tf_op jit(solution)/shard_map/ppermute | solution.py:140
  11.3 3.6 %collective-permute-done = bf16[3,64,512]{2,1,0:T(8,128)(2,1)S(1)} collective-permute-done((bf16[3,64,512]{2,1,0:T(8,128)(2,1)S(1)}, bf16[3,64,512]{2,1,0:T(8,128)(2,1)S(1)}, u32[]{:S(2)}, u32[]{:S(2)}) %collective-permute-start) | collective-permute-done | bytes 196640 | tf_op jit(solution)/shard_map/ppermute | solution.py:140
  14.9 1.0 select_bitcast_fusion.3
  15.9 0.8 pad_maximum_fusion.5
  16.7 0.0 all-gather.3.cloned.1.call-update
  16.7 3.8 %collective-permute-start.1 = (bf16[256,1024]{1,0:T(8,128)(2,1)}, bf16[256,1024]{1,0:T(8,128)(2,1)}, u32[]{:S(2)}, u32[]{:S(2)}) collective-permute-start(bf16[256,1024]{1,0:T(8,128)(2,1)} %param.5), channel_id=1, source_target_pairs={{0,128},{128,0},{1,129},{129,1},{2,130},{130,2},{3,131},{131,3},{4... | collective-permute-start | bytes 1572872 | tf_op jit(solution)/shard_map/ppermute | solution.py:144
  20.5 1.3 convert_element_type.97
  21.8 0.3 copy.29
  22.1 1.1 copy.18
  23.2 0.5 fusion.50
  23.7 0.6 fusion.53
  24.3 1.0 fusion.40
  25.4 0.8 add_negate_fusion
  26.1 0.8 subtract_convert_fusion
  26.9 0.3 fusion.6
  27.3 2.6 %pad_maximum_fusion.1 = bf16[1024,2048]{1,0:T(8,128)(2,1)} fusion(bf16[1024,1024]{1,0:T(8,128)(2,1)S(1)} %fusion.6, bf16[1024,1024]{1,0:T(8,128)(2,1)S(1)} %bitcast.134), kind=kLoop, calls=%fused_computation.41 | loop fusion | flops 8388608 | bytes 8388608 | tf_op jit(solution)/shard_map/concatenate | solution.py:39
  29.9 1.1 fusion.43
  31.0 3.5 %add_multiply_fusion = bf16[32,32,2048]{2,1,0:T(8,128)(2,1)} fusion(f32[32,2048]{1,0:T(8,128)S(1)} %get-tuple-element.62, f32[32,2048]{1,0:T(8,128)S(1)} %get-tuple-element.57, f32[32,2048]{1,0:T(8,128)S(1)} %get-tuple-element.63, f32[32,2048]{1,0:T(8,128)S(1)} %get-tuple-element.56), kind=kLoop, calls=%fused_computation.7 | loop fusion | flops 10485760 | bytes 5242880 | tf_op jit(solution)/shard_map/mul | solution.py:47
  34.6 0.0 collective-permute-done.1
  34.6 1.1 select_bitcast_fusion.1
  35.7 0.1 pad_maximum_fusion.4
  35.8 2.5 %broadcast_in_dim.110 = bf16[4,2,256,1024]{3,2,1,0:T(8,128)(2,1)} broadcast(bf16[2,256,1024]{2,1,0:T(8,128)(2,1)S(1)} %pad_maximum_fusion.4), dimensions={1,2,3} | broadcast | bytes 5242880 | tf_op jit(solution)/shard_map/broadcast_in_dim | solution.py:146
  38.3 5.0 %all-to-all-start = ((bf16[4,2,256,1024]{3,2,1,0:T(8,128)(2,1)}), bf16[4,2,256,1024]{3,2,1,0:T(8,128)(2,1)}, u32[]{:S(2)}, u32[]{:S(2)}) async-start(bf16[4,2,256,1024]{3,2,1,0:T(8,128)(2,1)} %broadcast_in_dim.110), calls=%async_computation | async-start | bytes 8388608 | tf_op jit(solution)/shard_map/all_to_all | solution.py:147
  43.3 4.6 %fusion.64 = f32[2048,256]{0,1:T(8,128)} fusion(bf16[256,1024]{1,0:T(8,128)(2,1)} %bitcast.141, bf16[1024,1024]{1,0:T(8,128)(2,1)} %copy-done.1, bf16[1024,1024]{1,0:T(8,128)(2,1)S(1)} %bitcast.135), kind=kOutput, calls=%fused_computation.182 | convolution fusion | flops 1082130432 | bytes 6815744 | tf_op jit(solution)/shard_map/dot_general | solution.py:61
  47.9 2.9 %fusion.2 = bf16[1024,2048]{1,0:T(8,128)(2,1)} fusion(bf16[32,32,2048]{2,1,0:T(8,128)(2,1)S(1)} %copy-done, bf16[2048]{0:T(1024)(128)(2,1)S(1)} %select_multiply_fusion, pred[1024]{0:T(1024)(128)(4,1)S(1)} %iota_compare_fusion), kind=kLoop, calls=%fused_computation.4 | loop fusion | flops 2097152 | bytes 8393728 | tf_op jit(solution)/shard_map/convert.4 | solution.py:199
  50.8 1.2 multiply_subtract_fusion
  52.0 2.5 %fusion.3 = bf16[1024,2048]{1,0:T(8,128)(2,1)} fusion(f32[32,32,2048]{2,1,0:T(8,128)S(1)} %multiply_subtract_fusion, f32[1024]{0:T(1024)S(1)} %select_multiply_fusion.1), kind=kLoop, calls=%fused_computation.6 | loop fusion | flops 4194304 | bytes 12587008 | tf_op jit(solution)/shard_map/convert.3 | solution.py:199
  54.5 8.5 %pad_maximum_fusion = bf16[2048,2048]{1,0:T(8,128)(2,1)} fusion(bf16[1024,2048]{1,0:T(8,128)(2,1)} %fusion.2, bf16[1024,2048]{1,0:T(8,128)(2,1)} %fusion.3), kind=kLoop, calls=%fused_computation | loop fusion | flops 16777216 | bytes 16777216 | tf_op jit(solution)/shard_map/concatenate | solution.py:46
  63.0 27.2 %all-to-all-done = bf16[4,2,256,1024]{3,2,1,0:T(8,128)(2,1)} async-done(((bf16[4,2,256,1024]{3,2,1,0:T(8,128)(2,1)}), bf16[4,2,256,1024]{3,2,1,0:T(8,128)(2,1)}, u32[]{:S(2)}, u32[]{:S(2)}) %all-to-all-start) | async-done | bytes 4194336 | tf_op jit(solution)/shard_map/all_to_all | solution.py:147
  90.3 7.4 %copy.19 = bf16[1,2,256,4,1024]{4,3,2,1,0:T(4,128)(2,1)} copy(bf16[1,2,256,4,1024]{4,2,1,3,0:T(8,128)(2,1)} %bitcast.15) | data formatting | bytes 8388608 | tf_op jit(solution)/shard_map/all_to_all | solution.py:147
  97.7 7.8 %reshape.344 = bf16[512,4096,1]{1,0,2:T(8,128)(2,1)} reshape(bf16[1,2,256,4,1024]{4,3,2,1,0:T(4,128)(2,1)} %copy.19) | data formatting | bytes 8388608 | tf_op jit(solution)/shard_map/reshape | solution.py:148
  105.5 11.0 %convolution_convert_fusion = bf16[3,512,512]{2,1,0:T(8,128)(2,1)S(1)} fusion(bf16[3,4096,512]{2,1,0:T(8,128)(2,1)} %bitcast.144, bf16[512,4096,1]{1,0,2:T(8,128)(2,1)} %reshape.344), kind=kOutput, calls=%fused_computation.57 | convolution fusion | flops 6443237376 | bytes 18350080 | tf_op jit(solution)/shard_map/pdc,ld->pcl/dot_general | solution.py:154
  116.5 0.1 constant_dynamic-slice_fusion
  116.6 0.3 collective-permute-start.2
  117.0 17.9 %collective-permute-done.2 = bf16[3,512,256]{2,1,0:T(8,128)(2,1)} collective-permute-done((bf16[3,512,256]{2,1,0:T(8,128)(2,1)S(1)}, bf16[3,512,256]{2,1,0:T(8,128)(2,1)}, u32[]{:S(2)}, u32[]{:S(2)}) %collective-permute-start.2) | collective-permute-done | bytes 786464 | tf_op jit(solution)/shard_map/ppermute | solution.py:159
  134.9 1.4 broadcast_select_fusion
  136.3 0.3 fusion.20
  136.6 0.3 copy.21
  136.9 7.0 %collective-permute-start.3 = (bf16[3,1024,2]{1,2,0:T(2,128)(2,1)S(1)}, bf16[3,1024,2]{1,2,0:T(2,128)(2,1)S(1)}, u32[]{:S(2)}, u32[]{:S(2)}) collective-permute-start(bf16[3,1024,2]{1,2,0:T(2,128)(2,1)S(1)} %copy.21), channel_id=1, source_target_pairs={{0,4},{4,8},{8,12},{12,16},{16,20},{20,24},{24,28},{28,32},{32,36}... | collective-permute-start | bytes 36872 | tf_op jit(solution)/shard_map/ppermute | solution.py:16
  143.9 1.9 fusion.12
  145.8 0.0 collective-permute-done.3
  145.8 1.5 copy.22
  147.3 8.3 %fusion.10 = f32[3,1024,256]{2,1,0:T(8,128)S(1)} fusion(f32[3,1024,2]{2,1,0:T(8,128)} %copy.22, f32[3,1024,256]{2,1,0:T(8,128)} %fusion.12, f32[3,1024]{1,0:T(4,128)S(1)} %get-tuple-element.64, f32[3,1024]{1,0:T(4,128)S(1)} %get-tuple-element.65, f32[3,1024]{1,0:T(4,128)S(1)} %bitcast.142), kind=kLoop, calls=%fused_computation.51 | loop fusion | flops 5505024 | bytes 6352896 | tf_op jit(solution)/shard_map/add | solution.py:112
  155.6 0.9 fusion.13
  156.5 10.7 %all-to-all-start.1 = ((bf16[64,16,256]{2,1,0:T(8,128)(2,1)}), bf16[64,16,256]{2,1,0:T(8,128)(2,1)}, u32[]{:S(2)}, u32[]{:S(2)}) async-start(bf16[64,16,256]{2,1,0:T(8,128)(2,1)} %bitcast.136), calls=%async_computation.1 | async-start | bytes 1048576 | tf_op jit(solution)/shard_map/all_to_all | solution.py:163
  167.2 2.1 slice_bitcast_fusion.31
  169.3 2.2 slice_bitcast_fusion.32
  171.5 12.9 %all-to-all-done.1 = bf16[64,16,256]{2,1,0:T(8,128)(2,1)} async-done(((bf16[64,16,256]{2,1,0:T(8,128)(2,1)}), bf16[64,16,256]{2,1,0:T(8,128)(2,1)}, u32[]{:S(2)}, u32[]{:S(2)}) %all-to-all-start.1) | async-done | bytes 524320 | tf_op jit(solution)/shard_map/all_to_all | solution.py:163
  184.4 2.0 copy.23
  186.4 2.2 dot_general.19
  188.8 0.0 slice-start
  188.8 3.8 %fusion.4 = f32[16,16,2048]{2,1,0:T(8,128)S(1)} fusion(bf16[16,16,1024]{2,1,0:T(8,128)(2,1)} %dot_general.19, bf16[1024,2048]{1,0:T(8,128)(2,1)} %pad_maximum_fusion.1), kind=kOutput, calls=%fused_computation.42 | convolution fusion | flops 1073741824 | bytes 6815744 | tf_op jit(solution)/shard_map/dot_general | solution.py:70
  192.6 0.2 fusion.65
  193.1 4.5 %subtract_convert_fusion.1 = bf16[16,16,1024]{2,1,0:T(8,128)(2,1)S(1)} fusion(f32[16,16,1024]{2,1,0:T(8,128)S(1)} %get-tuple-element.48, f32[16,1024]{1,0:T(8,128)S(1)} %copy-done.13, f32[16,1024]{1,0:T(8,128)S(1)} %copy-done.14, f32[16,1024]{1,0:T(8,128)S(1)} %copy-done.16, f32[16,1024]{1,0:T(8,128)S(1)} %copy-done.17, f32[16,1024]{1,0:T(8,128)S(1)} %copy-done.18, ...), kind=kLoop, calls=%fused_computation.72 | loop fusion | flops 17039360 | bytes 4719616 | tf_op jit(solution)/shard_map/convert.1 | solution.py:199
  197.6 5.2 %select_convert_fusion = bf16[16,16,1024]{2,1,0:T(8,128)(2,1)S(1)} fusion(f32[16,16,1024]{2,1,0:T(8,128)S(1)} %get-tuple-element.48, f32[16,16,1024]{2,1,0:T(8,128)S(1)} %get-tuple-element.47, f32[16,1024]{1,0:T(8,128)S(1)} %get-tuple-element.16, f32[16,1024]{1,0:T(8,128)S(1)} %get-tuple-element.17, f32[16,1024]{1,0:T(8,128)S(1)} %get-tuple-element.18, ...), kind=kLoop, calls=%fused_computation.71 | loop fusion | flops 25165824 | bytes 4719616 | tf_op jit(solution)/shard_map/convert.2 | solution.py:199
  202.9 2.4 fusion
  205.3 0.0 copy-start.30
  205.3 0.1 slice.346
  205.4 1.2 slice_add_fusion
  206.5 2.5 %reshape.340 = f32[16,64,256]{2,1,0:T(8,128)} reshape(f32[16,16,1024]{2,1,0:T(8,128)} %slice_add_fusion) | data formatting | bytes 2097152 | tf_op jit(solution)/shard_map/reshape | solution.py:101
  209.1 2.0 fusion.21
  211.0 23.4 %all_to_all.33 = bf16[64,16,256]{2,1,0:T(8,128)(2,1)S(1)} all-to-all(bf16[64,16,256]{2,1,0:T(8,128)(2,1)S(1)} %fusion.21), channel_id=1, replica_groups=mesh['yh'=2,'cq'=32,'ch'=4] {'yh','cq'}, dimensions={0} | all-to-all | bytes 1048576 | tf_op jit(solution)/shard_map/all_to_all | solution.py:169
  234.4 0.9 fusion.15
  (75 shorter events, 0.2 us)
Async XLA Ops:
  6.5 99.0 %all-gather.3.cloned.1.call-start = ((), (), s32[]{:S(2)}) async-start(), calls=%async_computation.3 | async-start | bytes 12976128 | tf_op jit(solution)/shard_map/all_gather | solution.py:142
  7.5 7.4 %collective-permute-start = (bf16[3,64,512]{2,1,0:T(8,128)(2,1)S(1)}, bf16[3,64,512]{2,1,0:T(8,128)(2,1)S(1)}, u32[]{:S(2)}, u32[]{:S(2)}) collective-permute-start(bf16[3,64,512]{2,1,0:T(8,128)(2,1)S(1)} %constant_dynamic-slice_fusion.1), channel_id=1, source_target_pairs={{0,128},{128,0},{1,129},{129,1},{2,130},{130,2},{3,131},{131,3},{4... | collective-permute-start | bytes 589832 | tf_op jit(solution)/shard_map/ppermute | solution.py:140
  16.7 17.9 %collective-permute-start.1 = (bf16[256,1024]{1,0:T(8,128)(2,1)}, bf16[256,1024]{1,0:T(8,128)(2,1)}, u32[]{:S(2)}, u32[]{:S(2)}) collective-permute-start(bf16[256,1024]{1,0:T(8,128)(2,1)} %param.5), channel_id=1, source_target_pairs={{0,128},{128,0},{1,129},{129,1},{2,130},{130,2},{3,131},{131,3},{4... | collective-permute-start | bytes 1572872 | tf_op jit(solution)/shard_map/ppermute | solution.py:144
  27.3 2.6 %copy-start.1 = (bf16[1024,1024]{1,0:T(8,128)(2,1)}, bf16[1024,1024]{1,0:T(8,128)(2,1)S(1)}, u32[]{:S(2)}) copy-start(bf16[1024,1024]{1,0:T(8,128)(2,1)S(1)} %fusion.6) | copy-start | bytes 6291460
  29.9 4.7 %copy-start.28 = (bf16[256,1024]{1,0:T(8,128)(2,1)S(1)}, bf16[256,1024]{1,0:T(8,128)(2,1)}, u32[]{:S(2)}) copy-start(bf16[256,1024]{1,0:T(8,128)(2,1)} %param.5) | copy-start | bytes 1572868
  38.3 52.0 %all-to-all-start = ((bf16[4,2,256,1024]{3,2,1,0:T(8,128)(2,1)}), bf16[4,2,256,1024]{3,2,1,0:T(8,128)(2,1)}, u32[]{:S(2)}, u32[]{:S(2)}) async-start(bf16[4,2,256,1024]{3,2,1,0:T(8,128)(2,1)} %broadcast_in_dim.110), calls=%async_computation | async-start | bytes 8388608 | tf_op jit(solution)/shard_map/all_to_all | solution.py:147
  43.3 4.6 %copy-start = (bf16[32,32,2048]{2,1,0:T(8,128)(2,1)S(1)}, bf16[32,32,2048]{2,1,0:T(8,128)(2,1)}, u32[]{:S(2)}) copy-start(bf16[32,32,2048]{2,1,0:T(8,128)(2,1)} %add_multiply_fusion) | copy-start | bytes 12582916
  105.5 11.4 %copy-start.29 = (f32[3,3,1024]{2,1,0:T(4,128)S(1)}, f32[3,3,1024]{2,1,0:T(4,128)}, u32[]{:S(2)}) copy-start(f32[3,3,1024]{2,1,0:T(4,128)} %param.7) | copy-start | bytes 110596
  116.6 18.3 %collective-permute-start.2 = (bf16[3,512,256]{2,1,0:T(8,128)(2,1)S(1)}, bf16[3,512,256]{2,1,0:T(8,128)(2,1)}, u32[]{:S(2)}, u32[]{:S(2)}) collective-permute-start(bf16[3,512,256]{2,1,0:T(8,128)(2,1)S(1)} %constant_dynamic-slice_fusion), channel_id=1, source_target_pairs={{0,128},{128,0},{1,129},{129,1},{2,130},{130,2},{3,131},{131,3},{4... | collective-permute-start | bytes 2359304 | tf_op jit(solution)/shard_map/ppermute | solution.py:159
  136.9 8.9 %collective-permute-start.3 = (bf16[3,1024,2]{1,2,0:T(2,128)(2,1)S(1)}, bf16[3,1024,2]{1,2,0:T(2,128)(2,1)S(1)}, u32[]{:S(2)}, u32[]{:S(2)}) collective-permute-start(bf16[3,1024,2]{1,2,0:T(2,128)(2,1)S(1)} %copy.21), channel_id=1, source_target_pairs={{0,4},{4,8},{8,12},{12,16},{16,20},{20,24},{24,28},{28,32},{32,36}... | collective-permute-start | bytes 36872 | tf_op jit(solution)/shard_map/ppermute | solution.py:16
  156.5 27.9 %all-to-all-start.1 = ((bf16[64,16,256]{2,1,0:T(8,128)(2,1)}), bf16[64,16,256]{2,1,0:T(8,128)(2,1)}, u32[]{:S(2)}, u32[]{:S(2)}) async-start(bf16[64,16,256]{2,1,0:T(8,128)(2,1)} %bitcast.136), calls=%async_computation.1 | async-start | bytes 1048576 | tf_op jit(solution)/shard_map/all_to_all | solution.py:163
  188.5 4.3 %copy-start.2 = (f32[16,1024]{1,0:T(8,128)S(1)}, f32[16,1024]{1,0:T(8,128)}, u32[]{:S(2)}) copy-start(f32[16,1024]{1,0:T(8,128)} %get-tuple-element.21) | copy-start | bytes 196612
  188.5 4.3 %copy-start.3 = (f32[16,1024]{1,0:T(8,128)S(1)}, f32[16,1024]{1,0:T(8,128)}, u32[]{:S(2)}) copy-start(f32[16,1024]{1,0:T(8,128)} %get-tuple-element.22) | copy-start | bytes 196612
  188.5 4.3 %copy-start.4 = (f32[16,1024]{1,0:T(8,128)S(1)}, f32[16,1024]{1,0:T(8,128)}, u32[]{:S(2)}) copy-start(f32[16,1024]{1,0:T(8,128)} %get-tuple-element.23) | copy-start | bytes 196612
  188.5 4.3 %copy-start.5 = (f32[16,1024]{1,0:T(8,128)S(1)}, f32[16,1024]{1,0:T(8,128)}, u32[]{:S(2)}) copy-start(f32[16,1024]{1,0:T(8,128)} %get-tuple-element.24) | copy-start | bytes 196612
  188.5 4.3 %copy-start.6 = (f32[16,1024]{1,0:T(8,128)S(1)}, f32[16,1024]{1,0:T(8,128)}, u32[]{:S(2)}) copy-start(f32[16,1024]{1,0:T(8,128)} %get-tuple-element.25) | copy-start | bytes 196612
  188.5 4.3 %copy-start.7 = (f32[16,1024]{1,0:T(8,128)S(1)}, f32[16,1024]{1,0:T(8,128)}, u32[]{:S(2)}) copy-start(f32[16,1024]{1,0:T(8,128)} %get-tuple-element.26) | copy-start | bytes 196612
  188.6 4.3 %copy-start.8 = (f32[16,1024]{1,0:T(8,128)S(1)}, f32[16,1024]{1,0:T(8,128)}, u32[]{:S(2)}) copy-start(f32[16,1024]{1,0:T(8,128)} %get-tuple-element.27) | copy-start | bytes 196612
  188.6 4.3 %copy-start.9 = (f32[16,1024]{1,0:T(8,128)S(1)}, f32[16,1024]{1,0:T(8,128)}, u32[]{:S(2)}) copy-start(f32[16,1024]{1,0:T(8,128)} %get-tuple-element.28) | copy-start | bytes 196612
  188.6 4.3 %copy-start.10 = (f32[16,1024]{1,0:T(8,128)S(1)}, f32[16,1024]{1,0:T(8,128)}, u32[]{:S(2)}) copy-start(f32[16,1024]{1,0:T(8,128)} %get-tuple-element.29) | copy-start | bytes 196612
  188.6 4.3 %copy-start.11 = (f32[16,1024]{1,0:T(8,128)S(1)}, f32[16,1024]{1,0:T(8,128)}, u32[]{:S(2)}) copy-start(f32[16,1024]{1,0:T(8,128)} %get-tuple-element.30) | copy-start | bytes 196612
  188.6 4.3 %copy-start.12 = (f32[16,1024]{1,0:T(8,128)S(1)}, f32[16,1024]{1,0:T(8,128)}, u32[]{:S(2)}) copy-start(f32[16,1024]{1,0:T(8,128)} %get-tuple-element.31) | copy-start | bytes 196612
  188.6 4.3 %copy-start.13 = (f32[16,1024]{1,0:T(8,128)S(1)}, f32[16,1024]{1,0:T(8,128)}, u32[]{:S(2)}) copy-start(f32[16,1024]{1,0:T(8,128)} %get-tuple-element.32) | copy-start | bytes 196612
  188.6 4.3 %copy-start.14 = (f32[16,1024]{1,0:T(8,128)S(1)}, f32[16,1024]{1,0:T(8,128)}, u32[]{:S(2)}) copy-start(f32[16,1024]{1,0:T(8,128)} %get-tuple-element.33) | copy-start | bytes 196612
  188.6 4.3 %copy-start.15 = (f32[16,1024]{1,0:T(8,128)S(1)}, f32[16,1024]{1,0:T(8,128)}, u32[]{:S(2)}) copy-start(f32[16,1024]{1,0:T(8,128)} %get-tuple-element.34) | copy-start | bytes 196612
  188.6 4.3 %copy-start.16 = (f32[16,1024]{1,0:T(8,128)S(1)}, f32[16,1024]{1,0:T(8,128)}, u32[]{:S(2)}) copy-start(f32[16,1024]{1,0:T(8,128)} %get-tuple-element.35) | copy-start | bytes 196612
  188.6 4.3 %copy-start.17 = (f32[16,1024]{1,0:T(8,128)S(1)}, f32[16,1024]{1,0:T(8,128)}, u32[]{:S(2)}) copy-start(f32[16,1024]{1,0:T(8,128)} %get-tuple-element.36) | copy-start | bytes 196612
  188.7 4.3 %copy-start.18 = (f32[16,1024]{1,0:T(8,128)S(1)}, f32[16,1024]{1,0:T(8,128)}, u32[]{:S(2)}) copy-start(f32[16,1024]{1,0:T(8,128)} %get-tuple-element.37) | copy-start | bytes 196612
  188.7 4.3 %copy-start.19 = (f32[16,1024]{1,0:T(8,128)S(1)}, f32[16,1024]{1,0:T(8,128)}, u32[]{:S(2)}) copy-start(f32[16,1024]{1,0:T(8,128)} %get-tuple-element.38) | copy-start | bytes 196612
  188.7 4.3 %copy-start.20 = (f32[16,1024]{1,0:T(8,128)S(1)}, f32[16,1024]{1,0:T(8,128)}, u32[]{:S(2)}) copy-start(f32[16,1024]{1,0:T(8,128)} %get-tuple-element.39) | copy-start | bytes 196612
  188.7 4.3 %copy-start.21 = (f32[16,1024]{1,0:T(8,128)S(1)}, f32[16,1024]{1,0:T(8,128)}, u32[]{:S(2)}) copy-start(f32[16,1024]{1,0:T(8,128)} %get-tuple-element.40) | copy-start | bytes 196612
  188.7 4.3 %copy-start.22 = (f32[16,1024]{1,0:T(8,128)S(1)}, f32[16,1024]{1,0:T(8,128)}, u32[]{:S(2)}) copy-start(f32[16,1024]{1,0:T(8,128)} %get-tuple-element.41) | copy-start | bytes 196612
  188.7 4.3 %copy-start.23 = (f32[16,1024]{1,0:T(8,128)S(1)}, f32[16,1024]{1,0:T(8,128)}, u32[]{:S(2)}) copy-start(f32[16,1024]{1,0:T(8,128)} %get-tuple-element.42) | copy-start | bytes 196612
  188.7 4.3 %copy-start.24 = (f32[16,1024]{1,0:T(8,128)S(1)}, f32[16,1024]{1,0:T(8,128)}, u32[]{:S(2)}) copy-start(f32[16,1024]{1,0:T(8,128)} %get-tuple-element.43) | copy-start | bytes 196612
  188.7 4.3 %copy-start.25 = (f32[16,1024]{1,0:T(8,128)S(1)}, f32[16,1024]{1,0:T(8,128)}, u32[]{:S(2)}) copy-start(f32[16,1024]{1,0:T(8,128)} %get-tuple-element.44) | copy-start | bytes 196612
  188.7 4.3 %copy-start.26 = (f32[16,1024]{1,0:T(8,128)S(1)}, f32[16,1024]{1,0:T(8,128)}, u32[]{:S(2)}) copy-start(f32[16,1024]{1,0:T(8,128)} %get-tuple-element.45) | copy-start | bytes 196612
  188.7 4.3 %copy-start.27 = (f32[16,1024]{1,0:T(8,128)S(1)}, f32[16,1024]{1,0:T(8,128)}, u32[]{:S(2)}) copy-start(f32[16,1024]{1,0:T(8,128)} %get-tuple-element.46) | copy-start | bytes 196612
  188.8 14.1 %slice-start = ((s8[8388608]{0:T(1024)(128)(4,1)}), s8[4194304]{0:T(1024)(128)(4,1)S(1)}, s32[]{:S(2)}) async-start(s8[8388608]{0:T(1024)(128)(4,1)} %bitcast.132), calls=%async_computation.4 | async-start | bytes 8388608
  192.6 10.3 %slice-start.1 = ((s8[8388608]{0:T(1024)(128)(4,1)}), s8[4194304]{0:T(1024)(128)(4,1)S(1)}, s32[]{:S(2)}) async-start(s8[8388608]{0:T(1024)(128)(4,1)} %bitcast.132), calls=%async_computation.5 | async-start | bytes 8388608
  205.3 3.8 %copy-start.30 = (f32[1,16]{1,0:T(1,128)S(1)}, f32[1,16]{1,0:T(1,128)}, u32[]{:S(2)}) copy-start(f32[1,16]{1,0:T(1,128)} %param.9) | copy-start | bytes 196
Sparse Core Ops, SparseCore 0:
  16.8 84.7 all-gather.2

commit v4 on v3

--- a/solution.py
+++ b/solution.py
@@ -135,6 +135,7 @@
         local_tokens, local_features = tokens.shape
         branches, local_rows, lanes = in_weight.shape
         width = lanes // 2
+        n_q = n_ctx // 2
         own_cols = lax.dynamic_slice_in_dim(in_weight, half * width, width, axis=2)
         other_cols = lax.dynamic_slice_in_dim(in_weight, (1 - half) * width, width, axis=2)
         partner_rows = lax.ppermute(other_cols, "yh", swap)
@@ -154,13 +155,33 @@
         summed = jnp.einsum(
             "pdc,ld->pcl", whole_weight, whole_tokens, preferred_element_type=jnp.float32
         ).astype(jnp.bfloat16)
-        own_part = lax.dynamic_slice_in_dim(summed, half * local_tokens, local_tokens, axis=2)
-        other_part = lax.dynamic_slice_in_dim(summed, (1 - half) * local_tokens, local_tokens, axis=2)
+        own_part = lax.dynamic_slice_in_dim(summed[0:1], half * local_tokens, local_tokens, axis=2)
+        other_part = lax.dynamic_slice_in_dim(
+            summed[0:1], (1 - half) * local_tokens, local_tokens, axis=2
+        )
         received = lax.ppermute(other_part, "yh", swap)
-        projected = jnp.concatenate(list(by_half(half, own_part, received)), axis=1)
-        embedding_result = featured(projected, short_taps)
-        gate_wave = (embedding_result[1] * embedding_result[2]).astype(jnp.bfloat16)
-        per_channel_view = lax.all_to_all(gate_wave, ctx, split_axis=0, concat_axis=1, tiled=True)
+        projected0 = jnp.concatenate(list(by_half(half, own_part, received)), axis=1)
+        embed0 = featured(projected0, short_taps[0:1])
+        q = lax.axis_index("cq")
+        blocks = summed[1:3].reshape(2, width, 2, local_tokens)
+        tails = blocks[:, :, :, local_tokens - 2 :]
+        ring = [(i, (i + 1) % n_q) for i in range(n_q)]
+        arrived = lax.ppermute(tails, "cq", ring)
+        first = jnp.concatenate([jnp.zeros_like(arrived[:, :, :1]), arrived[:, :, :1]], axis=2)
+        halo = jnp.where(q == 0, first, arrived)
+        taps12 = lax.dynamic_slice_in_dim(short_taps[1:3], half * width, width, axis=2)
+        extended = jnp.concatenate([halo, blocks], axis=3).astype(jnp.float32)
+        embed12 = None
+        for offset in range(3):
+            term = taps12[:, offset, :][:, :, None, None] * extended[
+                :, :, :, 2 - offset : 2 - offset + local_tokens
+            ]
+            embed12 = term if embed12 is None else embed12 + term
+        gate_wave = (embed12[0] * embed12[1]).astype(jnp.bfloat16)
+        lanes_each = width // n_q
+        outgoing12 = gate_wave.reshape(n_q, lanes_each, 2, local_tokens)
+        got = lax.all_to_all(outgoing12, "cq", split_axis=0, concat_axis=0, tiled=True)
+        per_channel_view = got.transpose(1, 2, 0, 3).reshape(lanes_each, -1)
         blended_lines = global_causal_smear(
             per_channel_view, spec_k, skip_gain[0], forward, inverse, tile_extent
         )
@@ -168,7 +189,7 @@
         outgoing = blended_lines.reshape(lines, n_ctx, span // n_ctx).transpose(1, 0, 2)
         returned = lax.all_to_all(outgoing, ctx, split_axis=0, concat_axis=0, tiled=True)
         by_token = returned.reshape(n_ctx * lines, span // n_ctx)
-        gated_output = (embedding_result[0] * by_token.astype(jnp.float32)).astype(jnp.bfloat16)
+        gated_output = (embed0[0] * by_token.astype(jnp.float32)).astype(jnp.bfloat16)
         return gated_output
 
     return shards

time: 243 us -> 217 us (0.89)
  blocking collectives: 23.4 us -> 0 us
  other arithmetic: 57.3 us -> 45.5 us
  starting transfers between devices: 30.6 us -> 42.2 us
  local copies, waits for them, and re-layouts: 33.4 us -> 28.5 us
    all_to_all x1 -> x0, blocking collectives: 23.4 us -> none  [shards(): lax.all_to_all(outgoing, ctx, split_axis=0, concat_axis=0, tiled=True)]
    ppermute x1, waiting for transfers between devices: 17.9 us -> 10 us  [shards(): received = lax.ppermute(other_part, 'yh', swap)]
    add x1, other arithmetic: 8.32 us -> 1.67 us  [shards(): embed12 = term if embed12 is None else embed12 + term]
    all_to_all x1 -> x2, starting transfers between devices: 10.7 us -> 17.2 us  [the longest x1 10.9 us: shards(): lax.all_to_all(outgoing12, 'cq', split_axis=0, concat_axis=0, tiled=True)]
    ppermute x0 -> x1, waiting for transfers between devices: none -> 6.11 us  [shards(): arrived = lax.ppermute(tails, 'cq', ring)]
    ppermute x0 -> x1, starting transfers between devices: none -> 4.5 us  [shards(): arrived = lax.ppermute(tails, 'cq', ring)]
    ppermute x1, starting transfers between devices: 0.31 us -> 3.06 us  [shards(): received = lax.ppermute(other_part, 'yh', swap)]
    mul x2, local copies, waits for them, and re-layouts: 4.32 us -> 1.7 us  [global_causal_smear(): terms = (f_re * s_re, f_im * s_im, f_re * s_im, f_im * s_re)]
  transfers between devices with their start and end apart: 7 -> 9, of which waited for: 4 -> 6; matrix products, arithmetic and copies ran while one was open for 24% -> 26% of each run, Pallas kernels for 0% -> 0%
where the time goes in v4:
time: 217 us; the launch traced here: 214 us
  waiting for transfers between devices  62.5 us (29%)
  other arithmetic  45.5 us (21%)
  starting transfers between devices  42.2 us (19%)
  local copies, waits for them, and re-layouts  28.5 us (13%)
  matrix products  21.4 us (10%)
  between operations  14.1 us (6%)
    all_to_all x1, waiting for transfers between devices, shards(): lax.all_to_all(copies, 'ch', split_axis=0, concat_axis=3, tiled=True)  27.3 us
    another operation x6, other arithmetic, run(): return lax.with_sharding_constraint(mapped(*args), out_sharding)  16.3 us
    all_to_all x1, waiting for transfers between devices, shards(): lax.all_to_all(outgoing12, 'cq', split_axis=0, concat_axis=0, tiled=True)  14.9 us
    all_to_all x1, starting transfers between devices, shards(): lax.all_to_all(outgoing12, 'cq', split_axis=0, concat_axis=0, tiled=True)  10.9 us
    dot_general x1, matrix products, shards(): jnp.einsum('pdc,ld->pcl', whole_weight, whole_tokens, preferred_element_t...  10.9 us
    ppermute x1, waiting for transfers between devices, shards(): received = lax.ppermute(other_part, 'yh', swap)  10 us
    concatenate x1, other arithmetic, spectral_tables(): jnp.concatenate([weights * cos_b, jnp.where(first_row, alt_t / period, -(...  8.51 us
    reshape x1, local copies, waits for them, and re-layouts, shards(): whole_tokens = pieces.reshape(2 * local_tokens, n_ch * local_features)  7.82 us
  transfers between devices with their start and end apart: 9, of which 6 were waited for; matrix products, arithmetic and copies ran while one was open for 26% of the time, Pallas kernels for 0%

profile of v4, /device:TPU:1, one launch (start us, length us, event | category | flops | bytes accessed | tf_op | source)
XLA Modules:
  0.0 214.3 jit_solution(1651660094598049867)
XLA Ops:
  6.5 1.0 constant_dynamic-slice_fusion.4
  7.5 3.8 %collective-permute-start = (bf16[3,64,512]{2,1,0:T(8,128)(2,1)S(1)}, bf16[3,64,512]{2,1,0:T(8,128)(2,1)S(1)}, u32[]{:S(2)}, u32[]{:S(2)}) collective-permute-start(bf16[3,64,512]{2,1,0:T(8,128)(2,1)S(1)} %constant_dynamic-slice_fusion.4), channel_id=1, source_target_pairs={{0,128},{128,0},{1,129},{129,1},{2,130},{130,2},{3,131},{131,3},{4... | collective-permute-start | bytes 589832 | tf_op jit(solution)/shard_map/ppermute | solution.py:141
  11.3 3.6 %collective-permute-done = bf16[3,64,512]{2,1,0:T(8,128)(2,1)S(1)} collective-permute-done((bf16[3,64,512]{2,1,0:T(8,128)(2,1)S(1)}, bf16[3,64,512]{2,1,0:T(8,128)(2,1)S(1)}, u32[]{:S(2)}, u32[]{:S(2)}) %collective-permute-start) | collective-permute-done | bytes 196640 | tf_op jit(solution)/shard_map/ppermute | solution.py:141
  14.9 1.0 select_bitcast_fusion.3
  15.9 0.8 pad_maximum_fusion.5
  16.7 3.8 %collective-permute-start.1 = (bf16[256,1024]{1,0:T(8,128)(2,1)}, bf16[256,1024]{1,0:T(8,128)(2,1)}, u32[]{:S(2)}, u32[]{:S(2)}) collective-permute-start(bf16[256,1024]{1,0:T(8,128)(2,1)} %param.5), channel_id=1, source_target_pairs={{0,128},{128,0},{1,129},{129,1},{2,130},{130,2},{3,131},{131,3},{4... | collective-permute-start | bytes 1572872 | tf_op jit(solution)/shard_map/ppermute | solution.py:145
  20.5 1.3 convert_element_type.115
  21.8 0.3 copy.39
  22.1 1.1 copy.26
  23.3 0.5 fusion.52
  23.8 0.6 fusion.55
  24.4 1.0 fusion.42
  25.5 0.8 add_negate_fusion
  26.3 0.8 subtract_convert_fusion
  27.1 0.3 fusion.6
  27.4 2.6 %pad_maximum_fusion.1 = bf16[1024,2048]{1,0:T(8,128)(2,1)} fusion(bf16[1024,1024]{1,0:T(8,128)(2,1)S(1)} %fusion.6, bf16[1024,1024]{1,0:T(8,128)(2,1)S(1)} %bitcast.145), kind=kLoop, calls=%fused_computation.39 | loop fusion | flops 8388608 | bytes 8388608 | tf_op jit(solution)/shard_map/concatenate | solution.py:39
  30.0 1.1 fusion.45
  31.1 3.5 %add_multiply_fusion = bf16[32,32,2048]{2,1,0:T(8,128)(2,1)} fusion(f32[32,2048]{1,0:T(8,128)S(1)} %get-tuple-element.65, f32[32,2048]{1,0:T(8,128)S(1)} %get-tuple-element.60, f32[32,2048]{1,0:T(8,128)S(1)} %get-tuple-element.66, f32[32,2048]{1,0:T(8,128)S(1)} %get-tuple-element.59), kind=kLoop, calls=%fused_computation.7 | loop fusion | flops 10485760 | bytes 5242880 | tf_op jit(solution)/shard_map/mul | solution.py:47
  34.7 1.1 select_bitcast_fusion.1
  35.9 2.5 %broadcast_in_dim.111 = bf16[4,2,256,1024]{3,2,1,0:T(8,128)(2,1)} broadcast(bf16[2,256,1024]{2,1,0:T(8,128)(2,1)S(1)} %pad_maximum_fusion.3), dimensions={1,2,3} | broadcast | bytes 5242880 | tf_op jit(solution)/shard_map/broadcast_in_dim | solution.py:147
  38.4 5.1 %all-to-all-start = ((bf16[4,2,256,1024]{3,2,1,0:T(8,128)(2,1)}), bf16[4,2,256,1024]{3,2,1,0:T(8,128)(2,1)}, u32[]{:S(2)}, u32[]{:S(2)}) async-start(bf16[4,2,256,1024]{3,2,1,0:T(8,128)(2,1)} %broadcast_in_dim.111), calls=%async_computation | async-start | bytes 8388608 | tf_op jit(solution)/shard_map/all_to_all | solution.py:148
  43.5 4.5 %fusion.67 = f32[2048,256]{0,1:T(8,128)} fusion(bf16[256,1024]{1,0:T(8,128)(2,1)} %bitcast.154, bf16[1024,1024]{1,0:T(8,128)(2,1)} %copy-done.1, bf16[1024,1024]{1,0:T(8,128)(2,1)S(1)} %bitcast.146), kind=kOutput, calls=%fused_computation.194 | convolution fusion | flops 1082130432 | bytes 6815744 | tf_op jit(solution)/shard_map/dot_general | solution.py:61
  48.0 2.9 %fusion.2 = bf16[1024,2048]{1,0:T(8,128)(2,1)} fusion(bf16[32,32,2048]{2,1,0:T(8,128)(2,1)S(1)} %copy-done, bf16[2048]{0:T(1024)(128)(2,1)S(1)} %select_multiply_fusion, pred[1024]{0:T(1024)(128)(4,1)S(1)} %iota_compare_fusion), kind=kLoop, calls=%fused_computation.4 | loop fusion | flops 2097152 | bytes 8393728 | tf_op jit(solution)/shard_map/convert.5 | solution.py:220
  50.9 1.2 multiply_subtract_fusion
  52.1 2.5 %fusion.3 = bf16[1024,2048]{1,0:T(8,128)(2,1)} fusion(f32[32,32,2048]{2,1,0:T(8,128)S(1)} %multiply_subtract_fusion, f32[1024]{0:T(1024)S(1)} %select_multiply_fusion.1), kind=kLoop, calls=%fused_computation.6 | loop fusion | flops 4194304 | bytes 12587008 | tf_op jit(solution)/shard_map/convert.4 | solution.py:220
  54.6 8.5 %pad_maximum_fusion = bf16[2048,2048]{1,0:T(8,128)(2,1)} fusion(bf16[1024,2048]{1,0:T(8,128)(2,1)} %fusion.2, bf16[1024,2048]{1,0:T(8,128)(2,1)} %fusion.3), kind=kLoop, calls=%fused_computation | loop fusion | flops 16777216 | bytes 16777216 | tf_op jit(solution)/shard_map/concatenate | solution.py:46
  63.1 27.3 %all-to-all-done = bf16[4,2,256,1024]{3,2,1,0:T(8,128)(2,1)} async-done(((bf16[4,2,256,1024]{3,2,1,0:T(8,128)(2,1)}), bf16[4,2,256,1024]{3,2,1,0:T(8,128)(2,1)}, u32[]{:S(2)}, u32[]{:S(2)}) %all-to-all-start) | async-done | bytes 4194336 | tf_op jit(solution)/shard_map/all_to_all | solution.py:148
  90.4 7.4 %copy.27 = bf16[1,2,256,4,1024]{4,3,2,1,0:T(4,128)(2,1)} copy(bf16[1,2,256,4,1024]{4,2,1,3,0:T(8,128)(2,1)} %bitcast.16) | data formatting | bytes 8388608 | tf_op jit(solution)/shard_map/all_to_all | solution.py:148
  97.9 7.8 %reshape.434 = bf16[512,4096,1]{1,0,2:T(8,128)(2,1)} reshape(bf16[1,2,256,4,1024]{4,3,2,1,0:T(4,128)(2,1)} %copy.27) | data formatting | bytes 8388608 | tf_op jit(solution)/shard_map/reshape | solution.py:149
  105.7 10.9 %convolution_convert_fusion = bf16[3,512,512]{1,2,0:T(8,128)(2,1)S(1)} fusion(bf16[512,4096,1]{1,0,2:T(8,128)(2,1)} %reshape.434, bf16[3,4096,512]{2,1,0:T(8,128)(2,1)} %bitcast.160), kind=kOutput, calls=%fused_computation.51 | convolution fusion | flops 6443237376 | bytes 18350080 | tf_op jit(solution)/shard_map/pdc,ld->pcl/dot_general | solution.py:155
  116.7 1.1 copy-done.3
  117.7 0.5 copy.28
  118.3 0.2 slice.387
  118.5 4.5 %collective-permute-start.4 = (bf16[2,512,2,2]{3,1,2,0:T(8,128)(2,1)S(1)}, bf16[2,512,2,2]{3,1,2,0:T(8,128)(2,1)S(1)}, u32[]{:S(2)}, u32[]{:S(2)}) collective-permute-start(bf16[2,512,2,2]{3,1,2,0:T(8,128)(2,1)S(1)} %slice.387), channel_id=1, source_target_pairs={{0,4},{4,8},{8,12},{12,16},{16,20},{20,24},{24,28},{28,32},{32,36}... | collective-permute-start | bytes 24584 | tf_op jit(solution)/shard_map/ppermute | solution.py:169
  123.0 6.1 %collective-permute-done.4 = bf16[2,512,2,2]{3,1,2,0:T(8,128)(2,1)S(1)} collective-permute-done((bf16[2,512,2,2]{3,1,2,0:T(8,128)(2,1)S(1)}, bf16[2,512,2,2]{3,1,2,0:T(8,128)(2,1)S(1)}, u32[]{:S(2)}, u32[]{:S(2)}) %collective-permute-start.4) | collective-permute-done | bytes 8224 | tf_op jit(solution)/shard_map/ppermute | solution.py:169
  129.2 0.7 maximum_convert_fusion
  129.9 1.7 fusion.7
  131.7 0.9 copy.30
  132.5 10.9 %all-to-all-start.1 = ((bf16[32,16,2,256]{3,1,2,0:T(8,128)(2,1)}), bf16[32,16,2,256]{3,1,2,0:T(8,128)(2,1)S(1)}, u32[]{:S(2)}, u32[]{:S(2)}) async-start(bf16[32,16,2,256]{3,1,2,0:T(8,128)(2,1)} %copy.30), calls=%async_computation.1 | async-start | bytes 1048576 | tf_op jit(solution)/shard_map/all_to_all | solution.py:183
  143.5 0.9 slice_bitcast_fusion.30
  144.4 0.8 slice_bitcast_fusion.31
  145.2 14.9 %all-to-all-done.1 = bf16[32,16,2,256]{3,1,2,0:T(8,128)(2,1)S(1)} async-done(((bf16[32,16,2,256]{3,1,2,0:T(8,128)(2,1)}), bf16[32,16,2,256]{3,1,2,0:T(8,128)(2,1)S(1)}, u32[]{:S(2)}, u32[]{:S(2)}) %all-to-all-start.1) | async-done | bytes 524320 | tf_op jit(solution)/shard_map/all_to_all | solution.py:183
  160.1 0.3 copy.31
  160.3 0.3 dot_general.19
  160.9 3.6 %fusion.4 = f32[16,16,2048]{2,1,0:T(8,128)S(1)} fusion(bf16[16,16,1024]{2,1,0:T(8,128)(2,1)S(1)} %dot_general.19, bf16[1024,2048]{1,0:T(8,128)(2,1)} %pad_maximum_fusion.1), kind=kOutput, calls=%fused_computation.40 | convolution fusion | flops 1073741824 | bytes 6815744 | tf_op jit(solution)/shard_map/dot_general | solution.py:70
  164.5 0.2 fusion.68
  164.9 4.5 %subtract_convert_fusion.1 = bf16[16,16,1024]{2,1,0:T(8,128)(2,1)S(1)} fusion(f32[16,16,1024]{2,1,0:T(8,128)S(1)} %get-tuple-element.46, f32[16,1024]{1,0:T(8,128)S(1)} %copy-done.7, f32[16,1024]{1,0:T(8,128)S(1)} %copy-done.8, f32[16,1024]{1,0:T(8,128)S(1)} %copy-done.10, f32[16,1024]{1,0:T(8,128)S(1)} %copy-done.11, f32[16,1024]{1,0:T(8,128)S(1)} %copy-done.12, ...), kind=kLoop, calls=%fused_computation.75 | loop fusion | flops 17039360 | bytes 4719616 | tf_op jit(solution)/shard_map/convert.2 | solution.py:220
  169.5 5.2 %select_convert_fusion = bf16[16,16,1024]{2,1,0:T(8,128)(2,1)S(1)} fusion(f32[16,16,1024]{2,1,0:T(8,128)S(1)} %get-tuple-element.46, f32[16,16,1024]{2,1,0:T(8,128)S(1)} %get-tuple-element.45, f32[16,1024]{1,0:T(8,128)S(1)} %get-tuple-element.14, f32[16,1024]{1,0:T(8,128)S(1)} %get-tuple-element.15, f32[16,1024]{1,0:T(8,128)S(1)} %get-tuple-element.16, ...), kind=kLoop, calls=%fused_computation.74 | loop fusion | flops 25165824 | bytes 4719616 | tf_op jit(solution)/shard_map/convert.3 | solution.py:220
  174.7 2.4 %fusion = f32[16,16,2048]{2,1,0:T(8,128)S(1)} fusion(bf16[2048,2048]{1,0:T(8,128)(2,1)S(1)} %bitcast.144, bf16[16,16,1024]{2,1,0:T(8,128)(2,1)S(1)} %select_convert_fusion, bf16[16,16,1024]{2,1,0:T(8,128)(2,1)S(1)} %subtract_convert_fusion.1), kind=kOutput, calls=%fused_computation.1 | convolution fusion | flops 2149580800 | bytes 11534336 | tf_op jit(solution)/shard_map/dot_general | solution.py:91
  177.2 0.2 slice_add_fusion
  177.4 0.3 reshape.429
  177.7 0.1 bitcast_convert_fusion.1
  178.0 1.4 fusion.22
  179.4 6.2 %all-to-all-start.2 = ((bf16[64,16,256]{2,1,0:T(8,128)(2,1)}), bf16[64,16,256]{2,1,0:T(8,128)(2,1)S(1)}, u32[]{:S(2)}, u32[]{:S(2)}) async-start(bf16[64,16,256]{2,1,0:T(8,128)(2,1)} %bitcast.59), calls=%async_computation.2 | async-start | bytes 1048576 | tf_op jit(solution)/shard_map/all_to_all | solution.py:190
  185.7 1.1 slice.381
  186.8 3.1 %collective-permute-start.2 = (bf16[1,512,256]{1,2,0:T(8,128)(2,1)S(1)}, bf16[1,512,256]{1,2,0:T(8,128)(2,1)S(1)}, u32[]{:S(2)}, u32[]{:S(2)}) collective-permute-start(bf16[1,512,256]{1,2,0:T(8,128)(2,1)S(1)} %constant_dynamic-slice_fusion.3), channel_id=1, source_target_pairs={{0,128},{128,0},{1,129},{129,1},{2,130},{130,2},{3,131},{131,3},{4... | collective-permute-start | bytes 786440 | tf_op jit(solution)/shard_map/ppermute | solution.py:162
  189.9 10.0 %collective-permute-done.2 = bf16[1,512,256]{1,2,0:T(8,128)(2,1)S(1)} collective-permute-done((bf16[1,512,256]{1,2,0:T(8,128)(2,1)S(1)}, bf16[1,512,256]{1,2,0:T(8,128)(2,1)S(1)}, u32[]{:S(2)}, u32[]{:S(2)}) %collective-permute-start.2) | collective-permute-done | bytes 262176 | tf_op jit(solution)/shard_map/ppermute | solution.py:162
  199.9 0.1 broadcast_select_fusion
  200.0 4.8 %collective-permute-start.3 = (bf16[1,1024,2]{1,2,0:T(2,128)(2,1)S(1)}, bf16[1,1024,2]{1,2,0:T(2,128)(2,1)S(1)}, u32[]{:S(2)}, u32[]{:S(2)}) collective-permute-start(bf16[1,1024,2]{1,2,0:T(2,128)(2,1)S(1)} %fusion.60), channel_id=1, source_target_pairs={{0,4},{4,8},{8,12},{12,16},{16,20},{20,24},{24,28},{28,32},{32,36}... | collective-permute-start | bytes 12296 | tf_op jit(solution)/shard_map/ppermute | solution.py:16
  204.9 0.1 fusion.23
  205.0 0.6 collective-permute-done.3
  205.7 0.3 copy.34
  206.1 0.4 fusion.15
  206.4 1.0 copy.35
  (81 shorter events, 0.9 us)
Async XLA Ops:
  6.5 16.7 %slice-start.2 = ((f32[3,3,1024]{2,1,0:T(4,128)}), f32[2,3,1024]{2,1,0:T(4,128)S(1)}, s32[]{:S(2)}) async-start(f32[3,3,1024]{2,1,0:T(4,128)} %param.7), calls=%async_computation.6 | async-start | bytes 65536 | tf_op jit(solution)/shard_map/slice | solution.py:172
  6.5 99.1 %all-gather.3.cloned.1.call-start = ((), (), s32[]{:S(2)}) async-start(), calls=%async_computation.3 | async-start | bytes 12976128 | tf_op jit(solution)/shard_map/all_gather | solution.py:143
  7.5 7.4 %collective-permute-start = (bf16[3,64,512]{2,1,0:T(8,128)(2,1)S(1)}, bf16[3,64,512]{2,1,0:T(8,128)(2,1)S(1)}, u32[]{:S(2)}, u32[]{:S(2)}) collective-permute-start(bf16[3,64,512]{2,1,0:T(8,128)(2,1)S(1)} %constant_dynamic-slice_fusion.4), channel_id=1, source_target_pairs={{0,128},{128,0},{1,129},{129,1},{2,130},{130,2},{3,131},{131,3},{4... | collective-permute-start | bytes 589832 | tf_op jit(solution)/shard_map/ppermute | solution.py:141
  16.7 18.0 %collective-permute-start.1 = (bf16[256,1024]{1,0:T(8,128)(2,1)}, bf16[256,1024]{1,0:T(8,128)(2,1)}, u32[]{:S(2)}, u32[]{:S(2)}) collective-permute-start(bf16[256,1024]{1,0:T(8,128)(2,1)} %param.5), channel_id=1, source_target_pairs={{0,128},{128,0},{1,129},{129,1},{2,130},{130,2},{3,131},{131,3},{4... | collective-permute-start | bytes 1572872 | tf_op jit(solution)/shard_map/ppermute | solution.py:145
  27.4 2.6 %copy-start.1 = (bf16[1024,1024]{1,0:T(8,128)(2,1)}, bf16[1024,1024]{1,0:T(8,128)(2,1)S(1)}, u32[]{:S(2)}) copy-start(bf16[1024,1024]{1,0:T(8,128)(2,1)S(1)} %fusion.6) | copy-start | bytes 6291460
  30.0 4.7 %copy-start.22 = (bf16[256,1024]{1,0:T(8,128)(2,1)S(1)}, bf16[256,1024]{1,0:T(8,128)(2,1)}, u32[]{:S(2)}) copy-start(bf16[256,1024]{1,0:T(8,128)(2,1)} %param.5) | copy-start | bytes 1572868
  38.4 52.0 %all-to-all-start = ((bf16[4,2,256,1024]{3,2,1,0:T(8,128)(2,1)}), bf16[4,2,256,1024]{3,2,1,0:T(8,128)(2,1)}, u32[]{:S(2)}, u32[]{:S(2)}) async-start(bf16[4,2,256,1024]{3,2,1,0:T(8,128)(2,1)} %broadcast_in_dim.111), calls=%async_computation | async-start | bytes 8388608 | tf_op jit(solution)/shard_map/all_to_all | solution.py:148
  43.5 4.5 %copy-start = (bf16[32,32,2048]{2,1,0:T(8,128)(2,1)S(1)}, bf16[32,32,2048]{2,1,0:T(8,128)(2,1)}, u32[]{:S(2)}) copy-start(bf16[32,32,2048]{2,1,0:T(8,128)(2,1)} %add_multiply_fusion) | copy-start | bytes 12582916
  116.6 1.2 copy-start.3
  118.5 10.6 %collective-permute-start.4 = (bf16[2,512,2,2]{3,1,2,0:T(8,128)(2,1)S(1)}, bf16[2,512,2,2]{3,1,2,0:T(8,128)(2,1)S(1)}, u32[]{:S(2)}, u32[]{:S(2)}) collective-permute-start(bf16[2,512,2,2]{3,1,2,0:T(8,128)(2,1)S(1)} %slice.387), channel_id=1, source_target_pairs={{0,4},{4,8},{8,12},{12,16},{16,20},{20,24},{24,28},{28,32},{32,36}... | collective-permute-start | bytes 24584 | tf_op jit(solution)/shard_map/ppermute | solution.py:169
  131.6 11.9 %copy-start.2 = (f32[2048,256]{0,1:T(8,128)S(1)}, f32[2048,256]{0,1:T(8,128)}, u32[]{:S(2)}) copy-start(f32[2048,256]{0,1:T(8,128)} %fusion.67) | copy-start | bytes 6291460
  132.5 27.5 %all-to-all-start.1 = ((bf16[32,16,2,256]{3,1,2,0:T(8,128)(2,1)}), bf16[32,16,2,256]{3,1,2,0:T(8,128)(2,1)S(1)}, u32[]{:S(2)}, u32[]{:S(2)}) async-start(bf16[32,16,2,256]{3,1,2,0:T(8,128)(2,1)} %copy.30), calls=%async_computation.1 | async-start | bytes 1048576 | tf_op jit(solution)/shard_map/all_to_all | solution.py:183
  160.7 4.1 %copy-start.4 = (f32[16,1024]{1,0:T(8,128)S(1)}, f32[16,1024]{1,0:T(8,128)}, u32[]{:S(2)}) copy-start(f32[16,1024]{1,0:T(8,128)} %get-tuple-element.27) | copy-start | bytes 196612
  160.7 4.1 %copy-start.5 = (f32[16,1024]{1,0:T(8,128)S(1)}, f32[16,1024]{1,0:T(8,128)}, u32[]{:S(2)}) copy-start(f32[16,1024]{1,0:T(8,128)} %get-tuple-element.28) | copy-start | bytes 196612
  160.7 4.1 %copy-start.6 = (f32[16,1024]{1,0:T(8,128)S(1)}, f32[16,1024]{1,0:T(8,128)}, u32[]{:S(2)}) copy-start(f32[16,1024]{1,0:T(8,128)} %get-tuple-element.29) | copy-start | bytes 196612
  160.7 4.1 %copy-start.7 = (f32[16,1024]{1,0:T(8,128)S(1)}, f32[16,1024]{1,0:T(8,128)}, u32[]{:S(2)}) copy-start(f32[16,1024]{1,0:T(8,128)} %get-tuple-element.30) | copy-start | bytes 196612
  160.7 4.1 %copy-start.8 = (f32[16,1024]{1,0:T(8,128)S(1)}, f32[16,1024]{1,0:T(8,128)}, u32[]{:S(2)}) copy-start(f32[16,1024]{1,0:T(8,128)} %get-tuple-element.31) | copy-start | bytes 196612
  160.7 4.1 %copy-start.9 = (f32[16,1024]{1,0:T(8,128)S(1)}, f32[16,1024]{1,0:T(8,128)}, u32[]{:S(2)}) copy-start(f32[16,1024]{1,0:T(8,128)} %get-tuple-element.32) | copy-start | bytes 196612
  160.7 4.1 %copy-start.10 = (f32[16,1024]{1,0:T(8,128)S(1)}, f32[16,1024]{1,0:T(8,128)}, u32[]{:S(2)}) copy-start(f32[16,1024]{1,0:T(8,128)} %get-tuple-element.33) | copy-start | bytes 196612
  160.7 4.1 %copy-start.11 = (f32[16,1024]{1,0:T(8,128)S(1)}, f32[16,1024]{1,0:T(8,128)}, u32[]{:S(2)}) copy-start(f32[16,1024]{1,0:T(8,128)} %get-tuple-element.34) | copy-start | bytes 196612
  160.7 4.1 %copy-start.12 = (f32[16,1024]{1,0:T(8,128)S(1)}, f32[16,1024]{1,0:T(8,128)}, u32[]{:S(2)}) copy-start(f32[16,1024]{1,0:T(8,128)} %get-tuple-element.35) | copy-start | bytes 196612
  160.8 4.1 %copy-start.13 = (f32[16,1024]{1,0:T(8,128)S(1)}, f32[16,1024]{1,0:T(8,128)}, u32[]{:S(2)}) copy-start(f32[16,1024]{1,0:T(8,128)} %get-tuple-element.36) | copy-start | bytes 196612
  160.8 4.1 %copy-start.14 = (f32[16,1024]{1,0:T(8,128)S(1)}, f32[16,1024]{1,0:T(8,128)}, u32[]{:S(2)}) copy-start(f32[16,1024]{1,0:T(8,128)} %get-tuple-element.37) | copy-start | bytes 196612
  160.8 4.1 %copy-start.15 = (f32[16,1024]{1,0:T(8,128)S(1)}, f32[16,1024]{1,0:T(8,128)}, u32[]{:S(2)}) copy-start(f32[16,1024]{1,0:T(8,128)} %get-tuple-element.38) | copy-start | bytes 196612
  160.8 4.1 %copy-start.16 = (f32[16,1024]{1,0:T(8,128)S(1)}, f32[16,1024]{1,0:T(8,128)}, u32[]{:S(2)}) copy-start(f32[16,1024]{1,0:T(8,128)} %get-tuple-element.39) | copy-start | bytes 196612
  160.8 4.1 %copy-start.17 = (f32[16,1024]{1,0:T(8,128)S(1)}, f32[16,1024]{1,0:T(8,128)}, u32[]{:S(2)}) copy-start(f32[16,1024]{1,0:T(8,128)} %get-tuple-element.40) | copy-start | bytes 196612
  160.8 4.1 %copy-start.18 = (f32[16,1024]{1,0:T(8,128)S(1)}, f32[16,1024]{1,0:T(8,128)}, u32[]{:S(2)}) copy-start(f32[16,1024]{1,0:T(8,128)} %get-tuple-element.41) | copy-start | bytes 196612
  160.8 4.1 %copy-start.19 = (f32[16,1024]{1,0:T(8,128)S(1)}, f32[16,1024]{1,0:T(8,128)}, u32[]{:S(2)}) copy-start(f32[16,1024]{1,0:T(8,128)} %get-tuple-element.42) | copy-start | bytes 196612
  160.8 4.1 %copy-start.20 = (f32[16,1024]{1,0:T(8,128)S(1)}, f32[16,1024]{1,0:T(8,128)}, u32[]{:S(2)}) copy-start(f32[16,1024]{1,0:T(8,128)} %get-tuple-element.43) | copy-start | bytes 196612
  160.8 4.1 %copy-start.21 = (f32[16,1024]{1,0:T(8,128)S(1)}, f32[16,1024]{1,0:T(8,128)}, u32[]{:S(2)}) copy-start(f32[16,1024]{1,0:T(8,128)} %get-tuple-element.44) | copy-start | bytes 196612
  160.8 13.8 %slice-start = ((s8[8388608]{0:T(1024)(128)(4,1)}), s8[4194304]{0:T(1024)(128)(4,1)S(1)}, s32[]{:S(2)}) async-start(s8[8388608]{0:T(1024)(128)(4,1)} %bitcast.143), calls=%async_computation.4 | async-start | bytes 8388608
  164.5 10.2 %slice-start.1 = ((s8[8388608]{0:T(1024)(128)(4,1)}), s8[4194304]{0:T(1024)(128)(4,1)S(1)}, s32[]{:S(2)}) async-start(s8[8388608]{0:T(1024)(128)(4,1)} %bitcast.143), calls=%async_computation.5 | async-start | bytes 8388608
  177.2 0.8 copy-start.24
  177.7 12.1 %copy-start.23 = (f32[3,3,1024]{2,1,0:T(4,128)S(1)}, f32[3,3,1024]{2,1,0:T(4,128)}, u32[]{:S(2)}) copy-start(f32[3,3,1024]{2,1,0:T(4,128)} %param.7) | copy-start | bytes 110596
  179.4 26.2 %all-to-all-start.2 = ((bf16[64,16,256]{2,1,0:T(8,128)(2,1)}), bf16[64,16,256]{2,1,0:T(8,128)(2,1)S(1)}, u32[]{:S(2)}, u32[]{:S(2)}) async-start(bf16[64,16,256]{2,1,0:T(8,128)(2,1)} %bitcast.59), calls=%async_computation.2 | async-start | bytes 1048576 | tf_op jit(solution)/shard_map/all_to_all | solution.py:190
  186.8 13.1 %collective-permute-start.2 = (bf16[1,512,256]{1,2,0:T(8,128)(2,1)S(1)}, bf16[1,512,256]{1,2,0:T(8,128)(2,1)S(1)}, u32[]{:S(2)}, u32[]{:S(2)}) collective-permute-start(bf16[1,512,256]{1,2,0:T(8,128)(2,1)S(1)} %constant_dynamic-slice_fusion.3), channel_id=1, source_target_pairs={{0,128},{128,0},{1,129},{129,1},{2,130},{130,2},{3,131},{131,3},{4... | collective-permute-start | bytes 786440 | tf_op jit(solution)/shard_map/ppermute | solution.py:162
  200.0 5.6 %collective-permute-start.3 = (bf16[1,1024,2]{1,2,0:T(2,128)(2,1)S(1)}, bf16[1,1024,2]{1,2,0:T(2,128)(2,1)S(1)}, u32[]{:S(2)}, u32[]{:S(2)}) collective-permute-start(bf16[1,1024,2]{1,2,0:T(2,128)(2,1)S(1)} %fusion.60), channel_id=1, source_target_pairs={{0,4},{4,8},{8,12},{12,16},{16,20},{20,24},{24,28},{28,32},{32,36}... | collective-permute-start | bytes 12296 | tf_op jit(solution)/shard_map/ppermute | solution.py:16
Sparse Core Ops, SparseCore 0:
  16.8 84.8 all-gather.2

commit v5 on v4

--- a/solution.py
+++ b/solution.py
@@ -160,13 +160,11 @@
             summed[0:1], (1 - half) * local_tokens, local_tokens, axis=2
         )
         received = lax.ppermute(other_part, "yh", swap)
-        projected0 = jnp.concatenate(list(by_half(half, own_part, received)), axis=1)
-        embed0 = featured(projected0, short_taps[0:1])
         q = lax.axis_index("cq")
         blocks = summed[1:3].reshape(2, width, 2, local_tokens)
-        tails = blocks[:, :, :, local_tokens - 2 :]
+        tails = blocks[:, :, :, local_tokens - 2 :].transpose(0, 2, 3, 1).reshape(-1, width)
         ring = [(i, (i + 1) % n_q) for i in range(n_q)]
-        arrived = lax.ppermute(tails, "cq", ring)
+        arrived = lax.ppermute(tails, "cq", ring).reshape(2, 2, 2, width).transpose(0, 3, 1, 2)
         first = jnp.concatenate([jnp.zeros_like(arrived[:, :, :1]), arrived[:, :, :1]], axis=2)
         halo = jnp.where(q == 0, first, arrived)
         taps12 = lax.dynamic_slice_in_dim(short_taps[1:3], half * width, width, axis=2)
@@ -181,7 +179,10 @@
         lanes_each = width // n_q
         outgoing12 = gate_wave.reshape(n_q, lanes_each, 2, local_tokens)
         got = lax.all_to_all(outgoing12, "cq", split_axis=0, concat_axis=0, tiled=True)
+        received, got = lax.optimization_barrier((received, got))
         per_channel_view = got.transpose(1, 2, 0, 3).reshape(lanes_each, -1)
+        projected0 = jnp.concatenate(list(by_half(half, own_part, received)), axis=1)
+        embed0 = featured(projected0, short_taps[0:1])
         blended_lines = global_causal_smear(
             per_channel_view, spec_k, skip_gain[0], forward, inverse, tile_extent
         )

time: 217 us -> 209 us (0.963)
  waiting for transfers between devices: 62.5 us -> 55.2 us
    all_to_all x1, waiting for transfers between devices: 14.9 us -> 1.53 us  [shards(): lax.all_to_all(outgoing12, 'cq', split_axis=0, concat_axis=0, tiled=True)]
    all_to_all x1, waiting for transfers between devices: 0.01 us -> 9.01 us  [shards(): lax.all_to_all(outgoing, ctx, split_axis=0, concat_axis=0, tiled=True)]
    ppermute x1, waiting for transfers between devices: 6.11 us -> 0.25 us  [shards(): lax.ppermute(tails, 'cq', ring).reshape(2, 2, 2, width)]
    ppermute x1, waiting for transfers between devices: 0.61 us -> 3.71 us  [shifted(): return lax.ppermute(block, axis, route)]
  transfers between devices with their start and end apart: 9 -> 9, of which waited for: 6 -> 7; matrix products, arithmetic and copies ran while one was open for 26% -> 28% of each run, Pallas kernels for 0% -> 0%
where the time goes in v5:
time: 209 us; the launch traced here: 208 us
  waiting for transfers between devices  55.2 us (26%)
  other arithmetic  46.3 us (22%)
  starting transfers between devices  41.1 us (20%)
  local copies, waits for them, and re-layouts  29.5 us (14%)
  matrix products  21.4 us (10%)
  between operations  14.2 us (7%)
    all_to_all x1, waiting for transfers between devices, shards(): lax.all_to_all(copies, 'ch', split_axis=0, concat_axis=3, tiled=True)  27.3 us
    another operation x6, other arithmetic, run(): return lax.with_sharding_constraint(mapped(*args), out_sharding)  16.2 us
    dot_general x1, matrix products, shards(): jnp.einsum('pdc,ld->pcl', whole_weight, whole_tokens, preferred_element_t...  10.9 us
    all_to_all x1, starting transfers between devices, shards(): lax.all_to_all(outgoing12, 'cq', split_axis=0, concat_axis=0, tiled=True)  10.7 us
    ppermute x1, waiting for transfers between devices, shards(): received = lax.ppermute(other_part, 'yh', swap)  9.8 us
    all_to_all x1, waiting for transfers between devices, shards(): lax.all_to_all(outgoing, ctx, split_axis=0, concat_axis=0, tiled=True)  9.01 us
    concatenate x1, other arithmetic, spectral_tables(): jnp.concatenate([weights * cos_b, jnp.where(first_row, alt_t / period, -(...  8.5 us
    all_to_all x1, starting transfers between devices, shards(): lax.all_to_all(outgoing, ctx, split_axis=0, concat_axis=0, tiled=True)  8.09 us
  transfers between devices with their start and end apart: 9, of which 7 were waited for; matrix products, arithmetic and copies ran while one was open for 28% of the time, Pallas kernels for 0%

profile of v5, /device:TPU:1, one launch (start us, length us, event | category | flops | bytes accessed | tf_op | source)
XLA Modules:
  0.0 207.8 jit_solution(14225138241267218314)
XLA Ops:
  6.5 1.0 constant_dynamic-slice_fusion.4
  7.5 3.8 %collective-permute-start = (bf16[3,64,512]{2,1,0:T(8,128)(2,1)S(1)}, bf16[3,64,512]{2,1,0:T(8,128)(2,1)S(1)}, u32[]{:S(2)}, u32[]{:S(2)}) collective-permute-start(bf16[3,64,512]{2,1,0:T(8,128)(2,1)S(1)} %constant_dynamic-slice_fusion.4), channel_id=1, source_target_pairs={{0,128},{128,0},{1,129},{129,1},{2,130},{130,2},{3,131},{131,3},{4... | collective-permute-start | bytes 589832 | tf_op jit(solution)/shard_map/ppermute | solution.py:141
  11.3 3.6 %collective-permute-done = bf16[3,64,512]{2,1,0:T(8,128)(2,1)S(1)} collective-permute-done((bf16[3,64,512]{2,1,0:T(8,128)(2,1)S(1)}, bf16[3,64,512]{2,1,0:T(8,128)(2,1)S(1)}, u32[]{:S(2)}, u32[]{:S(2)}) %collective-permute-start) | collective-permute-done | bytes 196640 | tf_op jit(solution)/shard_map/ppermute | solution.py:141
  14.9 1.0 select_bitcast_fusion.3
  15.9 0.8 pad_maximum_fusion.5
  16.7 3.8 %collective-permute-start.1 = (bf16[256,1024]{1,0:T(8,128)(2,1)}, bf16[256,1024]{1,0:T(8,128)(2,1)}, u32[]{:S(2)}, u32[]{:S(2)}) collective-permute-start(bf16[256,1024]{1,0:T(8,128)(2,1)} %param.5), channel_id=1, source_target_pairs={{0,128},{128,0},{1,129},{129,1},{2,130},{130,2},{3,131},{131,3},{4... | collective-permute-start | bytes 1572872 | tf_op jit(solution)/shard_map/ppermute | solution.py:145
  20.5 1.3 convert_element_type.115
  21.8 0.3 copy.37
  22.1 1.1 copy.24
  23.3 0.5 fusion.52
  23.9 0.6 fusion.55
  24.4 1.0 fusion.42
  25.5 0.8 add_negate_fusion
  26.3 0.8 subtract_convert_fusion
  27.1 0.3 fusion.6
  27.4 2.6 %pad_maximum_fusion.1 = bf16[1024,2048]{1,0:T(8,128)(2,1)} fusion(bf16[1024,1024]{1,0:T(8,128)(2,1)S(1)} %fusion.6, bf16[1024,1024]{1,0:T(8,128)(2,1)S(1)} %bitcast.149), kind=kLoop, calls=%fused_computation.39 | loop fusion | flops 8388608 | bytes 8388608 | tf_op jit(solution)/shard_map/concatenate | solution.py:39
  30.0 1.1 fusion.45
  31.1 3.5 %add_multiply_fusion = bf16[32,32,2048]{2,1,0:T(8,128)(2,1)} fusion(f32[32,2048]{1,0:T(8,128)S(1)} %get-tuple-element.69, f32[32,2048]{1,0:T(8,128)S(1)} %get-tuple-element.64, f32[32,2048]{1,0:T(8,128)S(1)} %get-tuple-element.70, f32[32,2048]{1,0:T(8,128)S(1)} %get-tuple-element.63), kind=kLoop, calls=%fused_computation.7 | loop fusion | flops 10485760 | bytes 5242880 | tf_op jit(solution)/shard_map/mul | solution.py:47
  34.7 1.1 select_bitcast_fusion.1
  35.9 2.5 %broadcast_in_dim.111 = bf16[4,2,256,1024]{3,2,1,0:T(8,128)(2,1)} broadcast(bf16[2,256,1024]{2,1,0:T(8,128)(2,1)S(1)} %pad_maximum_fusion.3), dimensions={1,2,3} | broadcast | bytes 5242880 | tf_op jit(solution)/shard_map/broadcast_in_dim | solution.py:147
  38.4 5.1 %all-to-all-start = ((bf16[4,2,256,1024]{3,2,1,0:T(8,128)(2,1)}), bf16[4,2,256,1024]{3,2,1,0:T(8,128)(2,1)}, u32[]{:S(2)}, u32[]{:S(2)}) async-start(bf16[4,2,256,1024]{3,2,1,0:T(8,128)(2,1)} %broadcast_in_dim.111), calls=%async_computation | async-start | bytes 8388608 | tf_op jit(solution)/shard_map/all_to_all | solution.py:148
  43.5 4.5 %fusion.67 = f32[2048,256]{0,1:T(8,128)} fusion(bf16[256,1024]{1,0:T(8,128)(2,1)} %bitcast.159, bf16[1024,1024]{1,0:T(8,128)(2,1)} %copy-done.1, bf16[1024,1024]{1,0:T(8,128)(2,1)S(1)} %bitcast.150), kind=kOutput, calls=%fused_computation.195 | convolution fusion | flops 1082130432 | bytes 6815744 | tf_op jit(solution)/shard_map/dot_general | solution.py:61
  48.0 2.9 %fusion.2 = bf16[1024,2048]{1,0:T(8,128)(2,1)} fusion(bf16[32,32,2048]{2,1,0:T(8,128)(2,1)S(1)} %copy-done, bf16[2048]{0:T(1024)(128)(2,1)S(1)} %select_multiply_fusion, pred[1024]{0:T(1024)(128)(4,1)S(1)} %iota_compare_fusion), kind=kLoop, calls=%fused_computation.4 | loop fusion | flops 2097152 | bytes 8393728 | tf_op jit(solution)/shard_map/convert.5 | solution.py:221
  50.9 1.2 multiply_subtract_fusion
  52.1 2.5 %fusion.3 = bf16[1024,2048]{1,0:T(8,128)(2,1)} fusion(f32[32,32,2048]{2,1,0:T(8,128)S(1)} %multiply_subtract_fusion, f32[1024]{0:T(1024)S(1)} %select_multiply_fusion.1), kind=kLoop, calls=%fused_computation.6 | loop fusion | flops 4194304 | bytes 12587008 | tf_op jit(solution)/shard_map/convert.4 | solution.py:221
  54.6 8.5 %pad_maximum_fusion = bf16[2048,2048]{1,0:T(8,128)(2,1)} fusion(bf16[1024,2048]{1,0:T(8,128)(2,1)} %fusion.2, bf16[1024,2048]{1,0:T(8,128)(2,1)} %fusion.3), kind=kLoop, calls=%fused_computation | loop fusion | flops 16777216 | bytes 16777216 | tf_op jit(solution)/shard_map/concatenate | solution.py:46
  63.1 27.3 %all-to-all-done = bf16[4,2,256,1024]{3,2,1,0:T(8,128)(2,1)} async-done(((bf16[4,2,256,1024]{3,2,1,0:T(8,128)(2,1)}), bf16[4,2,256,1024]{3,2,1,0:T(8,128)(2,1)}, u32[]{:S(2)}, u32[]{:S(2)}) %all-to-all-start) | async-done | bytes 4194336 | tf_op jit(solution)/shard_map/all_to_all | solution.py:148
  90.4 7.4 %copy.25 = bf16[1,2,256,4,1024]{4,3,2,1,0:T(4,128)(2,1)} copy(bf16[1,2,256,4,1024]{4,2,1,3,0:T(8,128)(2,1)} %bitcast.16) | data formatting | bytes 8388608 | tf_op jit(solution)/shard_map/all_to_all | solution.py:148
  97.8 7.8 %reshape.442 = bf16[512,4096,1]{1,0,2:T(8,128)(2,1)} reshape(bf16[1,2,256,4,1024]{4,3,2,1,0:T(4,128)(2,1)} %copy.25) | data formatting | bytes 8388608 | tf_op jit(solution)/shard_map/reshape | solution.py:149
  105.7 10.9 %convolution_convert_fusion = bf16[3,512,512]{1,2,0:T(8,128)(2,1)S(1)} fusion(bf16[512,4096,1]{1,0,2:T(8,128)(2,1)} %reshape.442, bf16[3,4096,512]{2,1,0:T(8,128)(2,1)} %bitcast.166), kind=kOutput, calls=%fused_computation.51 | convolution fusion | flops 6443237376 | bytes 18350080 | tf_op jit(solution)/shard_map/pdc,ld->pcl/dot_general | solution.py:155
  116.6 1.2 copy-done.5
  117.8 4.5 %collective-permute-start.3 = (bf16[8,512]{1,0:T(8,128)(2,1)S(1)}, bf16[8,512]{1,0:T(8,128)(2,1)S(1)}, u32[]{:S(2)}, u32[]{:S(2)}) collective-permute-start(bf16[8,512]{1,0:T(8,128)(2,1)S(1)} %reshape.435), channel_id=1, source_target_pairs={{0,4},{4,8},{8,12},{12,16},{16,20},{20,24},{24,28},{28,32},{32,36}... | collective-permute-start | bytes 24584 | tf_op jit(solution)/shard_map/ppermute | solution.py:167
  122.4 0.5 copy.27
  122.9 0.2 collective-permute-done.3
  123.2 0.3 copy.26
  123.5 0.7 maximum_convert_fusion
  124.2 1.7 fusion.7
  126.0 0.9 copy.28
  126.8 10.7 %all-to-all-start.1 = ((bf16[32,16,2,256]{3,1,2,0:T(8,128)(2,1)}), bf16[32,16,2,256]{3,1,2,0:T(8,128)(2,1)S(1)}, u32[]{:S(2)}, u32[]{:S(2)}) async-start(bf16[32,16,2,256]{3,1,2,0:T(8,128)(2,1)} %copy.28), calls=%async_computation.1 | async-start | bytes 1048576 | tf_op jit(solution)/shard_map/all_to_all | solution.py:181
  137.6 1.1 slice.381
  138.6 0.8 copy-done.2
  139.5 1.6 collective-permute-start.2
  141.1 0.9 slice_bitcast_fusion.30
  142.0 0.8 slice_bitcast_fusion.31
  142.8 9.8 %collective-permute-done.2 = bf16[1,512,256]{1,2,0:T(8,128)(2,1)} collective-permute-done((bf16[1,512,256]{1,2,0:T(8,128)(2,1)S(1)}, bf16[1,512,256]{1,2,0:T(8,128)(2,1)}, u32[]{:S(2)}, u32[]{:S(2)}) %collective-permute-start.2) | collective-permute-done | bytes 262176 | tf_op jit(solution)/shard_map/ppermute | solution.py:162
  152.6 1.5 all-to-all-done.1
  154.1 0.3 copy.29
  154.4 0.3 dot_general.19
  154.9 3.6 %fusion.4 = f32[16,16,2048]{2,1,0:T(8,128)S(1)} fusion(bf16[16,16,1024]{2,1,0:T(8,128)(2,1)S(1)} %dot_general.19, bf16[1024,2048]{1,0:T(8,128)(2,1)} %pad_maximum_fusion.1), kind=kOutput, calls=%fused_computation.40 | convolution fusion | flops 1073741824 | bytes 6815744 | tf_op jit(solution)/shard_map/dot_general | solution.py:70
  158.6 0.2 fusion.68
  159.0 4.5 %subtract_convert_fusion.1 = bf16[16,16,1024]{2,1,0:T(8,128)(2,1)S(1)} fusion(f32[16,16,1024]{2,1,0:T(8,128)S(1)} %get-tuple-element.50, f32[16,1024]{1,0:T(8,128)S(1)} %copy-done.9, f32[16,1024]{1,0:T(8,128)S(1)} %copy-done.10, f32[16,1024]{1,0:T(8,128)S(1)} %copy-done.12, f32[16,1024]{1,0:T(8,128)S(1)} %copy-done.13, f32[16,1024]{1,0:T(8,128)S(1)} %copy-done.14, ...), kind=kLoop, calls=%fused_computation.75 | loop fusion | flops 17039360 | bytes 4719616 | tf_op jit(solution)/shard_map/convert.2 | solution.py:221
  163.6 5.2 %select_convert_fusion = bf16[16,16,1024]{2,1,0:T(8,128)(2,1)S(1)} fusion(f32[16,16,1024]{2,1,0:T(8,128)S(1)} %get-tuple-element.50, f32[16,16,1024]{2,1,0:T(8,128)S(1)} %get-tuple-element.49, f32[16,1024]{1,0:T(8,128)S(1)} %get-tuple-element.18, f32[16,1024]{1,0:T(8,128)S(1)} %get-tuple-element.19, f32[16,1024]{1,0:T(8,128)S(1)} %get-tuple-element.20, ...), kind=kLoop, calls=%fused_computation.74 | loop fusion | flops 25165824 | bytes 4719616 | tf_op jit(solution)/shard_map/convert.3 | solution.py:221
  168.9 2.4 %fusion = f32[16,16,2048]{2,1,0:T(8,128)S(1)} fusion(bf16[2048,2048]{1,0:T(8,128)(2,1)S(1)} %bitcast.148, bf16[16,16,1024]{2,1,0:T(8,128)(2,1)S(1)} %select_convert_fusion, bf16[16,16,1024]{2,1,0:T(8,128)(2,1)S(1)} %subtract_convert_fusion.1), kind=kOutput, calls=%fused_computation.1 | convolution fusion | flops 2149580800 | bytes 11534336 | tf_op jit(solution)/shard_map/dot_general | solution.py:91
  171.4 0.2 slice_add_fusion
  171.6 0.3 reshape.437
  172.1 1.4 fusion.22
  173.5 8.1 %all-to-all-start.2 = ((bf16[64,16,256]{2,1,0:T(8,128)(2,1)}), bf16[64,16,256]{2,1,0:T(8,128)(2,1)S(1)}, u32[]{:S(2)}, u32[]{:S(2)}) async-start(bf16[64,16,256]{2,1,0:T(8,128)(2,1)} %bitcast.61), calls=%async_computation.2 | async-start | bytes 1048576 | tf_op jit(solution)/shard_map/all_to_all | solution.py:191
  181.6 1.0 broadcast_select_fusion
  182.7 3.5 %collective-permute-start.4 = (bf16[1,1024,2]{1,2,0:T(2,128)(2,1)S(1)}, bf16[1,1024,2]{1,2,0:T(2,128)(2,1)S(1)}, u32[]{:S(2)}, u32[]{:S(2)}) collective-permute-start(bf16[1,1024,2]{1,2,0:T(2,128)(2,1)S(1)} %fusion.60), channel_id=1, source_target_pairs={{0,4},{4,8},{8,12},{12,16},{16,20},{20,24},{24,28},{28,32},{32,36}... | collective-permute-start | bytes 12296 | tf_op jit(solution)/shard_map/ppermute | solution.py:16
  186.4 3.7 %collective-permute-done.4 = bf16[1,1024,2]{1,2,0:T(2,128)(2,1)S(1)} collective-permute-done((bf16[1,1024,2]{1,2,0:T(2,128)(2,1)S(1)}, bf16[1,1024,2]{1,2,0:T(2,128)(2,1)S(1)}, u32[]{:S(2)}, u32[]{:S(2)}) %collective-permute-start.4) | collective-permute-done | bytes 4128 | tf_op jit(solution)/shard_map/ppermute | solution.py:16
  190.1 9.0 %all-to-all-done.2 = bf16[64,16,256]{2,1,0:T(8,128)(2,1)S(1)} async-done(((bf16[64,16,256]{2,1,0:T(8,128)(2,1)}), bf16[64,16,256]{2,1,0:T(8,128)(2,1)S(1)}, u32[]{:S(2)}, u32[]{:S(2)}) %all-to-all-start.2) | async-done | bytes 524320 | tf_op jit(solution)/shard_map/all_to_all | solution.py:191
  199.2 0.3 copy.32
  199.6 0.4 fusion.15
  199.9 1.0 copy.33
  (88 shorter events, 1.2 us)
Async XLA Ops:
  6.5 16.7 %slice-start.2 = ((f32[3,3,1024]{2,1,0:T(4,128)}), f32[2,3,1024]{2,1,0:T(4,128)S(1)}, s32[]{:S(2)}) async-start(f32[3,3,1024]{2,1,0:T(4,128)} %param.7), calls=%async_computation.6 | async-start | bytes 65536 | tf_op jit(solution)/shard_map/slice | solution.py:170
  6.5 99.1 %all-gather.3.cloned.1.call-start = ((), (), s32[]{:S(2)}) async-start(), calls=%async_computation.3 | async-start | bytes 12976128 | tf_op jit(solution)/shard_map/all_gather | solution.py:143
  7.5 7.4 %collective-permute-start = (bf16[3,64,512]{2,1,0:T(8,128)(2,1)S(1)}, bf16[3,64,512]{2,1,0:T(8,128)(2,1)S(1)}, u32[]{:S(2)}, u32[]{:S(2)}) collective-permute-start(bf16[3,64,512]{2,1,0:T(8,128)(2,1)S(1)} %constant_dynamic-slice_fusion.4), channel_id=1, source_target_pairs={{0,128},{128,0},{1,129},{129,1},{2,130},{130,2},{3,131},{131,3},{4... | collective-permute-start | bytes 589832 | tf_op jit(solution)/shard_map/ppermute | solution.py:141
  16.7 18.0 %collective-permute-start.1 = (bf16[256,1024]{1,0:T(8,128)(2,1)}, bf16[256,1024]{1,0:T(8,128)(2,1)}, u32[]{:S(2)}, u32[]{:S(2)}) collective-permute-start(bf16[256,1024]{1,0:T(8,128)(2,1)} %param.5), channel_id=1, source_target_pairs={{0,128},{128,0},{1,129},{129,1},{2,130},{130,2},{3,131},{131,3},{4... | collective-permute-start | bytes 1572872 | tf_op jit(solution)/shard_map/ppermute | solution.py:145
  27.4 2.6 %copy-start.1 = (bf16[1024,1024]{1,0:T(8,128)(2,1)}, bf16[1024,1024]{1,0:T(8,128)(2,1)S(1)}, u32[]{:S(2)}) copy-start(bf16[1024,1024]{1,0:T(8,128)(2,1)S(1)} %fusion.6) | copy-start | bytes 6291460
  30.0 4.6 %copy-start.24 = (bf16[256,1024]{1,0:T(8,128)(2,1)S(1)}, bf16[256,1024]{1,0:T(8,128)(2,1)}, u32[]{:S(2)}) copy-start(bf16[256,1024]{1,0:T(8,128)(2,1)} %param.5) | copy-start | bytes 1572868
  38.4 52.0 %all-to-all-start = ((bf16[4,2,256,1024]{3,2,1,0:T(8,128)(2,1)}), bf16[4,2,256,1024]{3,2,1,0:T(8,128)(2,1)}, u32[]{:S(2)}, u32[]{:S(2)}) async-start(bf16[4,2,256,1024]{3,2,1,0:T(8,128)(2,1)} %broadcast_in_dim.111), calls=%async_computation | async-start | bytes 8388608 | tf_op jit(solution)/shard_map/all_to_all | solution.py:148
  43.5 4.5 %copy-start = (bf16[32,32,2048]{2,1,0:T(8,128)(2,1)S(1)}, bf16[32,32,2048]{2,1,0:T(8,128)(2,1)}, u32[]{:S(2)}) copy-start(bf16[32,32,2048]{2,1,0:T(8,128)(2,1)} %add_multiply_fusion) | copy-start | bytes 12582916
  116.6 1.2 copy-start.5
  117.8 5.3 %collective-permute-start.3 = (bf16[8,512]{1,0:T(8,128)(2,1)S(1)}, bf16[8,512]{1,0:T(8,128)(2,1)S(1)}, u32[]{:S(2)}, u32[]{:S(2)}) collective-permute-start(bf16[8,512]{1,0:T(8,128)(2,1)S(1)} %reshape.435), channel_id=1, source_target_pairs={{0,4},{4,8},{8,12},{12,16},{16,20},{20,24},{24,28},{28,32},{32,36}... | collective-permute-start | bytes 24584 | tf_op jit(solution)/shard_map/ppermute | solution.py:167
  125.8 15.2 %copy-start.4 = (f32[2048,256]{0,1:T(8,128)S(1)}, f32[2048,256]{0,1:T(8,128)}, u32[]{:S(2)}) copy-start(f32[2048,256]{0,1:T(8,128)} %fusion.67) | copy-start | bytes 6291460
  126.8 27.3 %all-to-all-start.1 = ((bf16[32,16,2,256]{3,1,2,0:T(8,128)(2,1)}), bf16[32,16,2,256]{3,1,2,0:T(8,128)(2,1)S(1)}, u32[]{:S(2)}, u32[]{:S(2)}) async-start(bf16[32,16,2,256]{3,1,2,0:T(8,128)(2,1)} %copy.28), calls=%async_computation.1 | async-start | bytes 1048576 | tf_op jit(solution)/shard_map/all_to_all | solution.py:181
  138.6 0.8 copy-start.2
  139.5 13.1 %collective-permute-start.2 = (bf16[1,512,256]{1,2,0:T(8,128)(2,1)S(1)}, bf16[1,512,256]{1,2,0:T(8,128)(2,1)}, u32[]{:S(2)}, u32[]{:S(2)}) collective-permute-start(bf16[1,512,256]{1,2,0:T(8,128)(2,1)S(1)} %constant_dynamic-slice_fusion.3), channel_id=1, source_target_pairs={{0,128},{128,0},{1,129},{129,1},{2,130},{130,2},{3,131},{131,3},{4... | collective-permute-start | bytes 786440 | tf_op jit(solution)/shard_map/ppermute | solution.py:162
  154.8 4.1 %copy-start.6 = (f32[16,1024]{1,0:T(8,128)S(1)}, f32[16,1024]{1,0:T(8,128)}, u32[]{:S(2)}) copy-start(f32[16,1024]{1,0:T(8,128)} %get-tuple-element.31) | copy-start | bytes 196612
  154.8 4.1 %copy-start.7 = (f32[16,1024]{1,0:T(8,128)S(1)}, f32[16,1024]{1,0:T(8,128)}, u32[]{:S(2)}) copy-start(f32[16,1024]{1,0:T(8,128)} %get-tuple-element.32) | copy-start | bytes 196612
  154.8 4.1 %copy-start.8 = (f32[16,1024]{1,0:T(8,128)S(1)}, f32[16,1024]{1,0:T(8,128)}, u32[]{:S(2)}) copy-start(f32[16,1024]{1,0:T(8,128)} %get-tuple-element.33) | copy-start | bytes 196612
  154.8 4.1 %copy-start.9 = (f32[16,1024]{1,0:T(8,128)S(1)}, f32[16,1024]{1,0:T(8,128)}, u32[]{:S(2)}) copy-start(f32[16,1024]{1,0:T(8,128)} %get-tuple-element.34) | copy-start | bytes 196612
  154.8 4.1 %copy-start.10 = (f32[16,1024]{1,0:T(8,128)S(1)}, f32[16,1024]{1,0:T(8,128)}, u32[]{:S(2)}) copy-start(f32[16,1024]{1,0:T(8,128)} %get-tuple-element.35) | copy-start | bytes 196612
  154.8 4.1 %copy-start.11 = (f32[16,1024]{1,0:T(8,128)S(1)}, f32[16,1024]{1,0:T(8,128)}, u32[]{:S(2)}) copy-start(f32[16,1024]{1,0:T(8,128)} %get-tuple-element.36) | copy-start | bytes 196612
  154.8 4.1 %copy-start.12 = (f32[16,1024]{1,0:T(8,128)S(1)}, f32[16,1024]{1,0:T(8,128)}, u32[]{:S(2)}) copy-start(f32[16,1024]{1,0:T(8,128)} %get-tuple-element.37) | copy-start | bytes 196612
  154.8 4.1 %copy-start.13 = (f32[16,1024]{1,0:T(8,128)S(1)}, f32[16,1024]{1,0:T(8,128)}, u32[]{:S(2)}) copy-start(f32[16,1024]{1,0:T(8,128)} %get-tuple-element.38) | copy-start | bytes 196612
  154.8 4.1 %copy-start.14 = (f32[16,1024]{1,0:T(8,128)S(1)}, f32[16,1024]{1,0:T(8,128)}, u32[]{:S(2)}) copy-start(f32[16,1024]{1,0:T(8,128)} %get-tuple-element.39) | copy-start | bytes 196612
  154.8 4.1 %copy-start.15 = (f32[16,1024]{1,0:T(8,128)S(1)}, f32[16,1024]{1,0:T(8,128)}, u32[]{:S(2)}) copy-start(f32[16,1024]{1,0:T(8,128)} %get-tuple-element.40) | copy-start | bytes 196612
  154.9 4.1 %copy-start.16 = (f32[16,1024]{1,0:T(8,128)S(1)}, f32[16,1024]{1,0:T(8,128)}, u32[]{:S(2)}) copy-start(f32[16,1024]{1,0:T(8,128)} %get-tuple-element.41) | copy-start | bytes 196612
  154.9 4.1 %copy-start.17 = (f32[16,1024]{1,0:T(8,128)S(1)}, f32[16,1024]{1,0:T(8,128)}, u32[]{:S(2)}) copy-start(f32[16,1024]{1,0:T(8,128)} %get-tuple-element.42) | copy-start | bytes 196612
  154.9 4.1 %copy-start.18 = (f32[16,1024]{1,0:T(8,128)S(1)}, f32[16,1024]{1,0:T(8,128)}, u32[]{:S(2)}) copy-start(f32[16,1024]{1,0:T(8,128)} %get-tuple-element.43) | copy-start | bytes 196612
  154.9 4.1 %copy-start.19 = (f32[16,1024]{1,0:T(8,128)S(1)}, f32[16,1024]{1,0:T(8,128)}, u32[]{:S(2)}) copy-start(f32[16,1024]{1,0:T(8,128)} %get-tuple-element.44) | copy-start | bytes 196612
  154.9 4.1 %copy-start.20 = (f32[16,1024]{1,0:T(8,128)S(1)}, f32[16,1024]{1,0:T(8,128)}, u32[]{:S(2)}) copy-start(f32[16,1024]{1,0:T(8,128)} %get-tuple-element.45) | copy-start | bytes 196612
  154.9 4.1 %copy-start.21 = (f32[16,1024]{1,0:T(8,128)S(1)}, f32[16,1024]{1,0:T(8,128)}, u32[]{:S(2)}) copy-start(f32[16,1024]{1,0:T(8,128)} %get-tuple-element.46) | copy-start | bytes 196612
  154.9 4.1 %copy-start.22 = (f32[16,1024]{1,0:T(8,128)S(1)}, f32[16,1024]{1,0:T(8,128)}, u32[]{:S(2)}) copy-start(f32[16,1024]{1,0:T(8,128)} %get-tuple-element.47) | copy-start | bytes 196612
  154.9 4.1 %copy-start.23 = (f32[16,1024]{1,0:T(8,128)S(1)}, f32[16,1024]{1,0:T(8,128)}, u32[]{:S(2)}) copy-start(f32[16,1024]{1,0:T(8,128)} %get-tuple-element.48) | copy-start | bytes 196612
  158.6 10.4 %slice-start = ((s8[8388608]{0:T(1024)(128)(4,1)}), s8[4194304]{0:T(1024)(128)(4,1)S(1)}, s32[]{:S(2)}) async-start(s8[8388608]{0:T(1024)(128)(4,1)} %bitcast.147), calls=%async_computation.4 | async-start | bytes 8388608
  159.0 9.9 %slice-start.1 = ((s8[8388608]{0:T(1024)(128)(4,1)}), s8[4194304]{0:T(1024)(128)(4,1)S(1)}, s32[]{:S(2)}) async-start(s8[8388608]{0:T(1024)(128)(4,1)} %bitcast.147), calls=%async_computation.5 | async-start | bytes 8388608
  171.4 0.7 copy-start.26
  171.6 10.0 %copy-start.25 = (f32[3,3,1024]{2,1,0:T(4,128)S(1)}, f32[3,3,1024]{2,1,0:T(4,128)}, u32[]{:S(2)}) copy-start(f32[3,3,1024]{2,1,0:T(4,128)} %param.7) | copy-start | bytes 110596
  171.9 9.7 %copy-start.3 = (bf16[1,512,512]{1,2,0:T(8,128)(2,1)S(1)}, bf16[1,512,512]{1,2,0:T(8,128)(2,1)}, u32[]{:S(2)}) copy-start(bf16[1,512,512]{1,2,0:T(8,128)(2,1)} %copy-done.2) | copy-start | bytes 1572868
  173.5 25.6 %all-to-all-start.2 = ((bf16[64,16,256]{2,1,0:T(8,128)(2,1)}), bf16[64,16,256]{2,1,0:T(8,128)(2,1)S(1)}, u32[]{:S(2)}, u32[]{:S(2)}) async-start(bf16[64,16,256]{2,1,0:T(8,128)(2,1)} %bitcast.61), calls=%async_computation.2 | async-start | bytes 1048576 | tf_op jit(solution)/shard_map/all_to_all | solution.py:191
  182.7 7.4 %collective-permute-start.4 = (bf16[1,1024,2]{1,2,0:T(2,128)(2,1)S(1)}, bf16[1,1024,2]{1,2,0:T(2,128)(2,1)S(1)}, u32[]{:S(2)}, u32[]{:S(2)}) collective-permute-start(bf16[1,1024,2]{1,2,0:T(2,128)(2,1)S(1)} %fusion.60), channel_id=1, source_target_pairs={{0,4},{4,8},{8,12},{12,16},{16,20},{20,24},{24,28},{28,32},{32,36}... | collective-permute-start | bytes 12296 | tf_op jit(solution)/shard_map/ppermute | solution.py:16
Sparse Core Ops, SparseCore 0:
  16.8 84.7 all-gather.2
